TPU v7x, 32 devices: a whole 2x2x4 slice. The times are simulated.
32 devices in a mesh: groups: 2 (over y), seq: 16 (over z, x, core).
Axes of the slice: x: 2, y: 2, z: 4, core: 2. Of those that a mesh axis runs over, the one named last changes fastest.
Arguments:
- queries: bfloat16 [8192, 2048], P(('groups', 'seq')), parts along dimension 0, may hold values from -6 to 6
- keys: bfloat16 [8192, 2048], P(('groups', 'seq')), parts along dimension 0, may hold values from -6 to 6
- values: bfloat16 [8192, 2048], P(('groups', 'seq')), parts along dimension 0, may hold values from -6 to 6
Outputs:
- attended: bfloat16 [8192, 2048], P(('groups', 'seq')), parts along dimension 0
There are 2 independent parts, one for each index of `groups`. A program takes and returns all parts, laid end to end along the dimension named above; each array names one. Nothing has to cross between parts.
All inputs are finite; a program needn't handle non-finite values.
Results may differ from a plain program's by a relative error of at most 0.0049.
Values may be sent and summed in bfloat16 or wider, within the bound.
No kernel may reach another device: no remote copies, remote signals or barrier semaphores. Data moves between devices by JAX's collectives and lax.ppermute only.
A program may use at most 256 MiB of HBM per device.

v0:
```python
import jax
import jax.numpy as jnp
from jax import lax
from jax.sharding import PartitionSpec as P

HEADS = 16
DK = 128


def on_device(queries, keys, values):
    tok = queries.shape[0]
    q_blk = queries.reshape(tok, HEADS, DK)
    k_blk = keys.reshape(tok, HEADS, DK)
    v_blk = values.reshape(tok, HEADS, DK)
    local_state = jnp.einsum("thd,the->hde", k_blk, v_blk, preferred_element_type=jnp.float32)
    flat = local_state.reshape(1, HEADS * DK, DK)
    received = lax.all_to_all(flat, "seq", split_axis=1, concat_axis=0, tiled=True)
    sources = received.shape[0]
    row_index = lax.broadcasted_iota(jnp.int32, (sources, sources), 0)
    col_index = lax.broadcasted_iota(jnp.int32, (sources, sources), 1)
    lower = (col_index < row_index).astype(jnp.float32)
    earlier = jnp.einsum(
        "cb,brd->crd",
        lower,
        received,
        precision=lax.Precision.HIGHEST,
        preferred_element_type=jnp.float32,
    )
    summed = lax.all_to_all(
        earlier.astype(jnp.bfloat16), "seq", split_axis=0, concat_axis=1, tiled=True
    )
    carried = summed.reshape(HEADS, DK, DK)
    rows = lax.broadcasted_iota(jnp.int32, (tok, tok), 0)
    cols = lax.broadcasted_iota(jnp.int32, (tok, tok), 1)
    causal = cols <= rows
    scores = jnp.einsum("thd,shd->hts", q_blk, k_blk, preferred_element_type=jnp.float32)
    scores = jnp.where(causal[None], scores, jnp.float32(0.0)).astype(jnp.bfloat16)
    intra = jnp.einsum("hts,she->the", scores, v_blk, preferred_element_type=jnp.float32)
    inter = jnp.einsum("thd,hde->the", q_blk, carried, preferred_element_type=jnp.float32)
    scale = 1.0 / jnp.sqrt(jnp.float32(DK * tok * lax.axis_size("seq")))
    attended = ((intra + inter) * scale).astype(jnp.bfloat16)
    return attended.reshape(tok, HEADS * DK)


def solution(mesh):
    placed = (P(("groups", "seq"), None), P(("groups", "seq"), None), P(("groups", "seq"), None))
    return jax.shard_map(
        on_device, mesh=mesh, in_specs=placed, out_specs=P(("groups", "seq"), None), check_vma=False
    )
```

profile of v0, /device:TPU:1, one launch (start us, length us, event | category | flops | bytes accessed | tf_op | source)
XLA Modules:
  0.0 59.0 jit_solution(12003108728023571996)
XLA Ops:
  0.0 0.0 copy-start
  0.0 0.0 copy-start.1
  0.0 1.6 %copy.17 = bf16[256,2048]{0,1:T(8,128)(2,1)S(1)} copy(bf16[256,2048]{1,0:T(8,128)(2,1)} %param.4) | data formatting | bytes 2097152 | tf_op jit(solution)/shard_map/reshape | solution.py:13
  1.6 0.0 copy-done.1
  1.6 0.4 fusion.4
  2.1 32.3 %all_to_all.21 = f32[1,2048,128]{2,0,1:T(1,128)S(1)} all-to-all(f32[1,2048,128]{2,0,1:T(1,128)S(1)} %bitcast.48), channel_id=1, replica_groups=mesh['groups'=2,'seq'=16] {'seq'}, dimensions={1} | all-to-all | bytes 2097152 | tf_op jit(solution)/shard_map/all_to_all | solution.py:17
  34.4 1.2 %fusion.9 = bf16[16,128,128]{2,0,1:T(8,128)(2,1)S(1)} fusion(f32[16,128,128]{2,1,0:T(8,128)S(1)} %bitcast.49), kind=kOutput, calls=%fused_computation.10 | convolution fusion | flops 50331904 | bytes 1572864 | tf_op jit(solution)/shard_map/cb,brd->crd/dot_general | solution.py:22
  35.6 1.2 %copy.16 = bf16[16,128,128]{1,2,0:T(8,128)(2,1)} copy(bf16[16,128,128]{2,0,1:T(8,128)(2,1)S(1)} %fusion.9) | data formatting | bytes 1048576 | tf_op jit(solution)/shard_map/cb,brd->crd/dot_general | solution.py:22
  36.8 4.6 %all-to-all-start.1 = ((bf16[16,128,128]{1,2,0:T(8,128)(2,1)}), bf16[16,128,128]{1,2,0:T(8,128)(2,1)S(1)}, u32[]{:S(2)}, u32[]{:S(2)}) async-start(bf16[16,128,128]{1,2,0:T(8,128)(2,1)} %copy.16), calls=%async_computation.1 | async-start | bytes 1048576 | tf_op jit(solution)/shard_map/all_to_all | solution.py:29
  41.5 0.0 copy-done
  41.5 3.9 %fusion.2 = f32[16,256,128]{1,2,0:T(8,128)} fusion(bf16[256,16,128]{0,2,1:T(8,128)(2,1)S(1)} %bitcast.47, pred[256,256]{1,0:T(8,128)(4,1)S(1)} %iota_compare_fusion, bf16[256,2048]{1,0:T(8,128)(2,1)} %param.5, bf16[256,2048]{1,0:T(8,128)(2,1)S(1)} %copy-done), kind=kOutput, calls=%fused_computation.4 | convolution fusion | flops 538968064 | bytes 5308416 | tf_op jit(solution)/shard_map/hts,she->the/dot_general | solution.py:38
  45.4 10.2 %all-to-all-done.1 = bf16[16,128,128]{1,2,0:T(8,128)(2,1)S(1)} async-done(((bf16[16,128,128]{1,2,0:T(8,128)(2,1)}), bf16[16,128,128]{1,2,0:T(8,128)(2,1)S(1)}, u32[]{:S(2)}, u32[]{:S(2)}) %all-to-all-start.1) | async-done | bytes 524320 | tf_op jit(solution)/shard_map/all_to_all | solution.py:29
  55.6 2.0 %fusion.1 = bf16[256,16,128]{0,2,1:T(8,128)(2,1)S(1)} fusion(f32[16,256,128]{1,2,0:T(8,128)} %fusion.2, bf16[16,128,128]{1,2,0:T(8,128)(2,1)S(1)} %all-to-all-done.1, bf16[256,2048]{1,0:T(8,128)(2,1)S(1)} %copy-done), kind=kOutput, calls=%fused_computation.3 | convolution fusion | flops 135790592 | bytes 4718592 | tf_op jit(solution)/shard_map/thd,hde->the/dot_general | solution.py:39
  57.6 1.4 %copy.14 = bf16[256,2048]{1,0:T(8,128)(2,1)} copy(bf16[256,2048]{0,1:T(8,128)(2,1)S(1)} %bitcast.50) | data formatting | bytes 2097152 | tf_op jit(solution)/shard_map/reshape | solution.py:42
  (1 shorter events, 0.0 us)
Async XLA Ops:
  0.0 41.5 %copy-start = (bf16[256,2048]{1,0:T(8,128)(2,1)S(1)}, bf16[256,2048]{1,0:T(8,128)(2,1)}, u32[]{:S(2)}) copy-start(bf16[256,2048]{1,0:T(8,128)(2,1)} %param.3) | copy-start | bytes 3145732
  0.0 1.6 %copy-start.1 = (bf16[256,2048]{1,0:T(8,128)(2,1)S(1)}, bf16[256,2048]{1,0:T(8,128)(2,1)}, u32[]{:S(2)}) copy-start(bf16[256,2048]{1,0:T(8,128)(2,1)} %param.5) | copy-start | bytes 3145732
  36.8 18.7 %all-to-all-start.1 = ((bf16[16,128,128]{1,2,0:T(8,128)(2,1)}), bf16[16,128,128]{1,2,0:T(8,128)(2,1)S(1)}, u32[]{:S(2)}, u32[]{:S(2)}) async-start(bf16[16,128,128]{1,2,0:T(8,128)(2,1)} %copy.16), calls=%async_computation.1 | async-start | bytes 1048576 | tf_op jit(solution)/shard_map/all_to_all | solution.py:29
where the time goes:
time: 59.8 us; the launch traced here: 59 us
  blocking collectives  32.3 us (54%)
  waiting for transfers between devices  10.2 us (17%)
  matrix products  7.54 us (13%)
  starting transfers between devices  4.64 us (8%)
  local copies, waits for them, and re-layouts  4.29 us (7%)
    all_to_all x1, blocking collectives, on_device(): lax.all_to_all(flat, 'seq', split_axis=1, concat_axis=0, tiled=True)  32.3 us
    all_to_all x1, waiting for transfers between devices, on_device(): lax.all_to_all(earlier.astype(jnp.bfloat16), 'seq', split_axis=0, concat_...  10.2 us
    all_to_all x1, starting transfers between devices, on_device(): lax.all_to_all(earlier.astype(jnp.bfloat16), 'seq', split_axis=0, concat_...  4.64 us
    dot_general x1, matrix products, on_device(): jnp.einsum('hts,she->the', scores, v_blk, preferred_element_type=jnp.floa...  3.88 us
    dot_general x1, matrix products, on_device(): jnp.einsum('thd,hde->the', q_blk, carried, preferred_element_type=jnp.flo...  2.03 us
    reshape x1, local copies, waits for them, and re-layouts, on_device(): k_blk = keys.reshape(tok, HEADS, DK)  1.62 us
    reshape x1, local copies, waits for them, and re-layouts, on_device(): return attended.reshape(tok, HEADS * DK)  1.42 us
    dot_general x1, local copies, waits for them, and re-layouts, on_device(): jnp.einsum('cb,brd->crd', lower, received, precision=lax.Precision.HIGHES...  1.23 us
  transfers between devices with their start and end apart: 1, of which 1 were waited for; matrix products, arithmetic and copies ran while one was open for 7% of the time, Pallas kernels for 0%

commit v1 on v0

v1 whole, which is shorter than its diff:
```python
import jax
import jax.numpy as jnp
from jax import lax
from jax.sharding import PartitionSpec as P

HEADS = 16
DK = 128


def on_device(queries, keys, values):
    tok = queries.shape[0]
    sources = lax.axis_size("seq")
    q_blk = queries.reshape(tok, HEADS, DK)
    k_blk = keys.reshape(tok, HEADS, DK)
    v_blk = values.reshape(tok, HEADS, DK)
    local_state = jnp.einsum("thd,the->hde", k_blk, v_blk, preferred_element_type=jnp.float32)
    flat = local_state.reshape(HEADS * DK, DK).astype(jnp.bfloat16)
    received = lax.all_to_all(flat, "seq", split_axis=0, concat_axis=0, tiled=True)
    received = received.reshape(sources, HEADS * DK // sources, DK)
    row_index = lax.broadcasted_iota(jnp.int32, (sources, sources), 0)
    col_index = lax.broadcasted_iota(jnp.int32, (sources, sources), 1)
    lower = (col_index < row_index).astype(jnp.bfloat16)
    earlier = jnp.einsum("cb,brd->crd", lower, received, preferred_element_type=jnp.float32)
    summed = lax.all_to_all(
        earlier.astype(jnp.bfloat16), "seq", split_axis=0, concat_axis=0, tiled=True
    )
    carried = summed.reshape(HEADS, DK, DK)
    rows = lax.broadcasted_iota(jnp.int32, (tok, tok), 0)
    cols = lax.broadcasted_iota(jnp.int32, (tok, tok), 1)
    causal = cols <= rows
    scores = jnp.einsum("thd,shd->hts", q_blk, k_blk, preferred_element_type=jnp.float32)
    scores = jnp.where(causal[None], scores, jnp.float32(0.0)).astype(jnp.bfloat16)
    intra = jnp.einsum("hts,she->the", scores, v_blk, preferred_element_type=jnp.float32)
    inter = jnp.einsum("thd,hde->the", q_blk, carried, preferred_element_type=jnp.float32)
    scale = 1.0 / jnp.sqrt(jnp.float32(DK * tok * sources))
    attended = ((intra + inter) * scale).astype(jnp.bfloat16)
    return attended.reshape(tok, HEADS * DK)


def solution(mesh):
    placed = (P(("groups", "seq"), None), P(("groups", "seq"), None), P(("groups", "seq"), None))
    return jax.shard_map(
        on_device, mesh=mesh, in_specs=placed, out_specs=P(("groups", "seq"), None), check_vma=False
    )
```

time: 59.8 us -> 47.7 us (0.80)
  blocking collectives: 32.3 us -> 21.2 us
  matrix products: 7.54 us -> 6.74 us
    all_to_all x1, blocking collectives: 32.3 us -> 21.2 us  [on_device(): lax.all_to_all(flat, 'seq', split_axis=0, concat_axis=0, tiled=True)]
    dot_general x1, matrix products: 1.21 us -> 0.41 us  [on_device(): jnp.einsum('cb,brd->crd', lower, received, preferred_element_type=jnp.flo...]
  transfers between devices with their start and end apart: 1 -> 1, of which waited for: 1 -> 1; matrix products, arithmetic and copies ran while one was open for 7% -> 8% of each run, Pallas kernels for 0% -> 0%
where the time goes in v1:
time: 47.7 us; the launch traced here: 46.9 us
  blocking collectives  21.2 us (44%)
  waiting for transfers between devices  10.2 us (21%)
  matrix products  6.74 us (14%)
  starting transfers between devices  4.5 us (9%)
  local copies, waits for them, and re-layouts  4.29 us (9%)
    all_to_all x1, blocking collectives, on_device(): lax.all_to_all(flat, 'seq', split_axis=0, concat_axis=0, tiled=True)  21.2 us
    all_to_all x1, waiting for transfers between devices, on_device(): lax.all_to_all(earlier.astype(jnp.bfloat16), 'seq', split_axis=0, concat_...  10.2 us
    all_to_all x1, starting transfers between devices, on_device(): lax.all_to_all(earlier.astype(jnp.bfloat16), 'seq', split_axis=0, concat_...  4.5 us
    dot_general x1, matrix products, on_device(): jnp.einsum('hts,she->the', scores, v_blk, preferred_element_type=jnp.floa...  3.88 us
    dot_general x1, matrix products, on_device(): jnp.einsum('thd,hde->the', q_blk, carried, preferred_element_type=jnp.flo...  2.03 us
    reshape x1, local copies, waits for them, and re-layouts, on_device(): k_blk = keys.reshape(tok, HEADS, DK)  1.62 us
    reshape x1, local copies, waits for them, and re-layouts, on_device(): return attended.reshape(tok, HEADS * DK)  1.42 us
    dot_general x1, local copies, waits for them, and re-layouts, on_device(): jnp.einsum('cb,brd->crd', lower, received, preferred_element_type=jnp.flo...  1.23 us
  transfers between devices with their start and end apart: 1, of which 1 were waited for; matrix products, arithmetic and copies ran while one was open for 8% of the time, Pallas kernels for 0%

profile of v1, /device:TPU:1, one launch (start us, length us, event | category | flops | bytes accessed | tf_op | source)
XLA Modules:
  0.0 46.9 jit_solution(6540692937816569142)
XLA Ops:
  0.0 0.0 copy-start
  0.0 0.0 copy-start.1
  0.0 1.6 %copy.11 = bf16[256,2048]{0,1:T(8,128)(2,1)S(1)} copy(bf16[256,2048]{1,0:T(8,128)(2,1)} %param.4) | data formatting | bytes 2097152 | tf_op jit(solution)/shard_map/reshape | solution.py:14
  1.6 0.0 copy-done.1
  1.6 0.4 convolution_convert_fusion
  2.1 21.2 %all_to_all.11 = bf16[16,128,128]{2,1,0:T(8,128)(2,1)S(1)} all-to-all(bf16[16,128,128]{2,1,0:T(8,128)(2,1)S(1)} %convolution_convert_fusion), channel_id=1, replica_groups=mesh['groups'=2,'seq'=16] {'seq'}, dimensions={0} | all-to-all | bytes 1048576 | tf_op jit(solution)/shard_map/all_to_all | solution.py:18
  23.3 0.4 fusion.13
  23.7 1.2 %copy.10 = bf16[16,128,128]{1,2,0:T(8,128)(2,1)} copy(bf16[16,128,128]{2,0,1:T(8,128)(2,1)S(1)} %fusion.13) | data formatting | bytes 1048576 | tf_op jit(solution)/shard_map/cb,brd->crd/dot_general | solution.py:23
  24.9 4.5 %all-to-all-start.1 = ((bf16[16,128,128]{1,2,0:T(8,128)(2,1)}), bf16[16,128,128]{1,2,0:T(8,128)(2,1)S(1)}, u32[]{:S(2)}, u32[]{:S(2)}) async-start(bf16[16,128,128]{1,2,0:T(8,128)(2,1)} %copy.10), calls=%async_computation.1 | async-start | bytes 1048576 | tf_op jit(solution)/shard_map/all_to_all | solution.py:24
  29.4 0.0 copy-done
  29.4 3.9 %fusion.2 = f32[16,256,128]{1,2,0:T(8,128)} fusion(bf16[256,16,128]{0,2,1:T(8,128)(2,1)S(1)} %bitcast.43, pred[256,256]{1,0:T(8,128)(4,1)S(1)} %iota_compare_fusion, bf16[256,2048]{1,0:T(8,128)(2,1)} %param.5, bf16[256,2048]{1,0:T(8,128)(2,1)S(1)} %copy-done), kind=kOutput, calls=%fused_computation.4 | convolution fusion | flops 538968064 | bytes 5308416 | tf_op jit(solution)/shard_map/hts,she->the/dot_general | solution.py:33
  33.3 10.2 %all-to-all-done.1 = bf16[16,128,128]{1,2,0:T(8,128)(2,1)S(1)} async-done(((bf16[16,128,128]{1,2,0:T(8,128)(2,1)}), bf16[16,128,128]{1,2,0:T(8,128)(2,1)S(1)}, u32[]{:S(2)}, u32[]{:S(2)}) %all-to-all-start.1) | async-done | bytes 524320 | tf_op jit(solution)/shard_map/all_to_all | solution.py:24
  43.5 2.0 %fusion.1 = bf16[256,16,128]{0,2,1:T(8,128)(2,1)S(1)} fusion(f32[16,256,128]{1,2,0:T(8,128)} %fusion.2, bf16[16,128,128]{1,2,0:T(8,128)(2,1)S(1)} %all-to-all-done.1, bf16[256,2048]{1,0:T(8,128)(2,1)S(1)} %copy-done), kind=kOutput, calls=%fused_computation.3 | convolution fusion | flops 135790592 | bytes 4718592 | tf_op jit(solution)/shard_map/thd,hde->the/dot_general | solution.py:34
  45.5 1.4 %copy.6 = bf16[256,2048]{1,0:T(8,128)(2,1)} copy(bf16[256,2048]{0,1:T(8,128)(2,1)S(1)} %bitcast.44) | data formatting | bytes 2097152 | tf_op jit(solution)/shard_map/reshape | solution.py:37
  (1 shorter events, 0.0 us)
Async XLA Ops:
  0.0 29.4 %copy-start = (bf16[256,2048]{1,0:T(8,128)(2,1)S(1)}, bf16[256,2048]{1,0:T(8,128)(2,1)}, u32[]{:S(2)}) copy-start(bf16[256,2048]{1,0:T(8,128)(2,1)} %param.3) | copy-start | bytes 3145732
  0.0 1.6 %copy-start.1 = (bf16[256,2048]{1,0:T(8,128)(2,1)S(1)}, bf16[256,2048]{1,0:T(8,128)(2,1)}, u32[]{:S(2)}) copy-start(bf16[256,2048]{1,0:T(8,128)(2,1)} %param.5) | copy-start | bytes 3145732
  24.9 18.6 %all-to-all-start.1 = ((bf16[16,128,128]{1,2,0:T(8,128)(2,1)}), bf16[16,128,128]{1,2,0:T(8,128)(2,1)S(1)}, u32[]{:S(2)}, u32[]{:S(2)}) async-start(bf16[16,128,128]{1,2,0:T(8,128)(2,1)} %copy.10), calls=%async_computation.1 | async-start | bytes 1048576 | tf_op jit(solution)/shard_map/all_to_all | solution.py:24

commit v2 on v1

--- a/solution.py
+++ b/solution.py
@@ -14,13 +14,19 @@
     k_blk = keys.reshape(tok, HEADS, DK)
     v_blk = values.reshape(tok, HEADS, DK)
     local_state = jnp.einsum("thd,the->hde", k_blk, v_blk, preferred_element_type=jnp.float32)
-    flat = local_state.reshape(HEADS * DK, DK).astype(jnp.bfloat16)
+    flat = local_state.reshape(HEADS * DK, DK).astype(jnp.float16)
     received = lax.all_to_all(flat, "seq", split_axis=0, concat_axis=0, tiled=True)
     received = received.reshape(sources, HEADS * DK // sources, DK)
     row_index = lax.broadcasted_iota(jnp.int32, (sources, sources), 0)
     col_index = lax.broadcasted_iota(jnp.int32, (sources, sources), 1)
-    lower = (col_index < row_index).astype(jnp.bfloat16)
-    earlier = jnp.einsum("cb,brd->crd", lower, received, preferred_element_type=jnp.float32)
+    lower = (col_index < row_index).astype(jnp.float32)
+    earlier = jnp.einsum(
+        "cb,brd->crd",
+        lower,
+        received.astype(jnp.float32),
+        precision=lax.Precision.HIGHEST,
+        preferred_element_type=jnp.float32,
+    )
     summed = lax.all_to_all(
         earlier.astype(jnp.bfloat16), "seq", split_axis=0, concat_axis=0, tiled=True
     )

time: 47.7 us -> 48 us (level)
  no operation moved by 1% of the time
where the time goes in v2:
time: 48 us; the launch traced here: 47.2 us
  blocking collectives  21.2 us (44%)
  waiting for transfers between devices  10.2 us (21%)
  matrix products  6.99 us (15%)
  starting transfers between devices  4.5 us (9%)
  local copies, waits for them, and re-layouts  4.29 us (9%)
    all_to_all x1, blocking collectives, on_device(): lax.all_to_all(flat, 'seq', split_axis=0, concat_axis=0, tiled=True)  21.2 us
    all_to_all x1, waiting for transfers between devices, on_device(): lax.all_to_all(earlier.astype(jnp.bfloat16), 'seq', split_axis=0, concat_...  10.2 us
    all_to_all x1, starting transfers between devices, on_device(): lax.all_to_all(earlier.astype(jnp.bfloat16), 'seq', split_axis=0, concat_...  4.5 us
    dot_general x1, matrix products, on_device(): jnp.einsum('hts,she->the', scores, v_blk, preferred_element_type=jnp.floa...  3.88 us
    dot_general x1, matrix products, on_device(): jnp.einsum('thd,hde->the', q_blk, carried, preferred_element_type=jnp.flo...  2.03 us
    reshape x1, local copies, waits for them, and re-layouts, on_device(): k_blk = keys.reshape(tok, HEADS, DK)  1.62 us
    reshape x1, local copies, waits for them, and re-layouts, on_device(): return attended.reshape(tok, HEADS * DK)  1.42 us
    dot_general x1, local copies, waits for them, and re-layouts, on_device(): jnp.einsum('cb,brd->crd', lower, received.astype(jnp.float32), precision=...  1.23 us
  transfers between devices with their start and end apart: 1, of which 1 were waited for; matrix products, arithmetic and copies ran while one was open for 8% of the time, Pallas kernels for 0%

profile of v2, /device:TPU:1, one launch (start us, length us, event | category | flops | bytes accessed | tf_op | source)
XLA Modules:
  0.0 47.2 jit_solution(15077650827598808452)
XLA Ops:
  0.0 0.0 copy-start
  0.0 0.0 copy-start.1
  0.0 1.6 %copy.11 = bf16[256,2048]{0,1:T(8,128)(2,1)S(1)} copy(bf16[256,2048]{1,0:T(8,128)(2,1)} %param.4) | data formatting | bytes 2097152 | tf_op jit(solution)/shard_map/reshape | solution.py:14
  1.6 0.0 copy-done.1
  1.6 0.4 convolution_convert_fusion
  2.1 21.2 %all_to_all.11 = f16[16,128,128]{2,1,0:T(8,128)(2,1)S(1)} all-to-all(f16[16,128,128]{2,1,0:T(8,128)(2,1)S(1)} %convolution_convert_fusion), channel_id=1, replica_groups=mesh['groups'=2,'seq'=16] {'seq'}, dimensions={0} | all-to-all | bytes 1048576 | tf_op jit(solution)/shard_map/all_to_all | solution.py:18
  23.3 0.6 %fusion.13 = bf16[16,128,128]{2,0,1:T(8,128)(2,1)S(1)} fusion(f16[16,128,128]{2,1,0:T(8,128)(2,1)S(1)} %all_to_all.11), kind=kOutput, calls=%fused_computation.14 | convolution fusion | flops 8388864 | bytes 1048576 | tf_op jit(solution)/shard_map/cb,brd->crd/dot_general | solution.py:23
  23.9 1.2 %copy.10 = bf16[16,128,128]{1,2,0:T(8,128)(2,1)} copy(bf16[16,128,128]{2,0,1:T(8,128)(2,1)S(1)} %fusion.13) | data formatting | bytes 1048576 | tf_op jit(solution)/shard_map/cb,brd->crd/dot_general | solution.py:23
  25.2 4.5 %all-to-all-start.1 = ((bf16[16,128,128]{1,2,0:T(8,128)(2,1)}), bf16[16,128,128]{1,2,0:T(8,128)(2,1)S(1)}, u32[]{:S(2)}, u32[]{:S(2)}) async-start(bf16[16,128,128]{1,2,0:T(8,128)(2,1)} %copy.10), calls=%async_computation.1 | async-start | bytes 1048576 | tf_op jit(solution)/shard_map/all_to_all | solution.py:30
  29.7 0.0 copy-done
  29.7 3.9 %fusion.2 = f32[16,256,128]{1,2,0:T(8,128)} fusion(bf16[256,16,128]{0,2,1:T(8,128)(2,1)S(1)} %bitcast.43, pred[256,256]{1,0:T(8,128)(4,1)S(1)} %iota_compare_fusion, bf16[256,2048]{1,0:T(8,128)(2,1)} %param.5, bf16[256,2048]{1,0:T(8,128)(2,1)S(1)} %copy-done), kind=kOutput, calls=%fused_computation.4 | convolution fusion | flops 538968064 | bytes 5308416 | tf_op jit(solution)/shard_map/hts,she->the/dot_general | solution.py:39
  33.6 10.2 %all-to-all-done.1 = bf16[16,128,128]{1,2,0:T(8,128)(2,1)S(1)} async-done(((bf16[16,128,128]{1,2,0:T(8,128)(2,1)}), bf16[16,128,128]{1,2,0:T(8,128)(2,1)S(1)}, u32[]{:S(2)}, u32[]{:S(2)}) %all-to-all-start.1) | async-done | bytes 524320 | tf_op jit(solution)/shard_map/all_to_all | solution.py:30
  43.7 2.0 %fusion.1 = bf16[256,16,128]{0,2,1:T(8,128)(2,1)S(1)} fusion(f32[16,256,128]{1,2,0:T(8,128)} %fusion.2, bf16[16,128,128]{1,2,0:T(8,128)(2,1)S(1)} %all-to-all-done.1, bf16[256,2048]{1,0:T(8,128)(2,1)S(1)} %copy-done), kind=kOutput, calls=%fused_computation.3 | convolution fusion | flops 135790592 | bytes 4718592 | tf_op jit(solution)/shard_map/thd,hde->the/dot_general | solution.py:40
  45.8 1.4 %copy.6 = bf16[256,2048]{1,0:T(8,128)(2,1)} copy(bf16[256,2048]{0,1:T(8,128)(2,1)S(1)} %bitcast.44) | data formatting | bytes 2097152 | tf_op jit(solution)/shard_map/reshape | solution.py:43
  (1 shorter events, 0.0 us)
Async XLA Ops:
  0.0 29.7 %copy-start = (bf16[256,2048]{1,0:T(8,128)(2,1)S(1)}, bf16[256,2048]{1,0:T(8,128)(2,1)}, u32[]{:S(2)}) copy-start(bf16[256,2048]{1,0:T(8,128)(2,1)} %param.3) | copy-start | bytes 3145732
  0.0 1.6 %copy-start.1 = (bf16[256,2048]{1,0:T(8,128)(2,1)S(1)}, bf16[256,2048]{1,0:T(8,128)(2,1)}, u32[]{:S(2)}) copy-start(bf16[256,2048]{1,0:T(8,128)(2,1)} %param.5) | copy-start | bytes 3145732
  25.2 18.6 %all-to-all-start.1 = ((bf16[16,128,128]{1,2,0:T(8,128)(2,1)}), bf16[16,128,128]{1,2,0:T(8,128)(2,1)S(1)}, u32[]{:S(2)}, u32[]{:S(2)}) async-start(bf16[16,128,128]{1,2,0:T(8,128)(2,1)} %copy.10), calls=%async_computation.1 | async-start | bytes 1048576 | tf_op jit(solution)/shard_map/all_to_all | solution.py:30

commit v3 on v2

v3 whole, which is shorter than its diff:
```python
import functools

import jax
import numpy as np
import jax.numpy as jnp
from jax import lax
from jax.experimental import pallas as pl
from jax.experimental.pallas import tpu as pltpu
from jax.sharding import PartitionSpec as P

HEADS = 16
DK = 128
GROUP = 4


def state_kernel(k_ref, v_ref, o_ref):
    for j in range(GROUP):
        cols = slice(j * DK, (j + 1) * DK)
        s = lax.dot_general(
            k_ref[:, cols], v_ref[:, cols], (((0,), (0,)), ((), ())),
            preferred_element_type=jnp.float32,
        )
        o_ref[j * DK:(j + 1) * DK, :] = s.astype(o_ref.dtype)


def intra_kernel(q_ref, k_ref, v_ref, o_ref):
    tok = q_ref.shape[0]
    rows = lax.broadcasted_iota(jnp.int32, (tok, tok), 0)
    cols_i = lax.broadcasted_iota(jnp.int32, (tok, tok), 1)
    causal = cols_i <= rows
    for j in range(GROUP):
        cols = slice(j * DK, (j + 1) * DK)
        s = lax.dot_general(
            q_ref[:, cols], k_ref[:, cols], (((1,), (1,)), ((), ())),
            preferred_element_type=jnp.float32,
        )
        s = jnp.where(causal, s, jnp.float32(0.0)).astype(jnp.bfloat16)
        o_ref[:, cols] = jnp.dot(s, v_ref[:, cols], preferred_element_type=jnp.float32)


def final_kernel(scale, q_ref, p_ref, intra_ref, o_ref):
    for j in range(GROUP):
        cols = slice(j * DK, (j + 1) * DK)
        inter = jnp.dot(q_ref[:, cols], p_ref[j * DK:(j + 1) * DK, :], preferred_element_type=jnp.float32)
        o_ref[:, cols] = ((intra_ref[:, cols] + inter) * scale).astype(o_ref.dtype)


def local_states(keys, values):
    tok = keys.shape[0]
    steps = HEADS // GROUP
    return pl.pallas_call(
        state_kernel,
        grid=(steps,),
        in_specs=[pl.BlockSpec((tok, GROUP * DK), lambda i: (0, i))] * 2,
        out_specs=pl.BlockSpec((GROUP * DK, DK), lambda i: (i, 0)),
        out_shape=jax.ShapeDtypeStruct((HEADS * DK, DK), jnp.float32),
        cost_estimate=pl.CostEstimate(
            flops=2 * tok * DK * DK * HEADS, transcendentals=0,
            bytes_accessed=2 * tok * HEADS * DK * 2 + HEADS * DK * DK * 4,
        ),
    )(keys, values)


def intra_block(queries, keys, values):
    tok = queries.shape[0]
    steps = HEADS // GROUP
    spec = pl.BlockSpec((tok, GROUP * DK), lambda i: (0, i))
    return pl.pallas_call(
        intra_kernel,
        grid=(steps,),
        in_specs=[spec] * 3,
        out_specs=spec,
        out_shape=jax.ShapeDtypeStruct((tok, HEADS * DK), jnp.float32),
        cost_estimate=pl.CostEstimate(
            flops=4 * tok * tok * DK * HEADS, transcendentals=0,
            bytes_accessed=3 * tok * HEADS * DK * 2 + tok * HEADS * DK * 4,
        ),
    )(queries, keys, values)


def combine(queries, carried, intra, scale):
    tok = queries.shape[0]
    steps = HEADS // GROUP
    spec = pl.BlockSpec((tok, GROUP * DK), lambda i: (0, i))
    return pl.pallas_call(
        functools.partial(final_kernel, scale),
        grid=(steps,),
        in_specs=[spec, pl.BlockSpec((GROUP * DK, DK), lambda i: (i, 0)), spec],
        out_specs=spec,
        out_shape=jax.ShapeDtypeStruct((tok, HEADS * DK), jnp.bfloat16),
        cost_estimate=pl.CostEstimate(
            flops=2 * tok * DK * DK * HEADS, transcendentals=0,
            bytes_accessed=2 * tok * HEADS * DK * 2 + tok * HEADS * DK * 4 + HEADS * DK * DK * 2,
        ),
    )(queries, carried, intra)


def on_device(queries, keys, values):
    tok = queries.shape[0]
    sources = lax.axis_size("seq")
    flat = local_states(keys, values).astype(jnp.float16)
    received = lax.all_to_all(flat, "seq", split_axis=0, concat_axis=0, tiled=True)
    received = received.reshape(sources, HEADS * DK // sources, DK)
    row_index = lax.broadcasted_iota(jnp.int32, (sources, sources), 0)
    col_index = lax.broadcasted_iota(jnp.int32, (sources, sources), 1)
    lower = (col_index < row_index).astype(jnp.float32)
    earlier = jnp.einsum(
        "cb,brd->crd",
        lower,
        received.astype(jnp.float32),
        precision=lax.Precision.HIGHEST,
        preferred_element_type=jnp.float32,
    )
    summed = lax.all_to_all(
        earlier.astype(jnp.bfloat16), "seq", split_axis=0, concat_axis=0, tiled=True
    )
    carried = summed.reshape(HEADS * DK, DK)
    intra = intra_block(queries, keys, values)
    scale = float(np.float32(1.0) / np.sqrt(np.float32(DK * tok * sources)))
    return combine(queries, carried, intra, scale)


def solution(mesh):
    placed = (P(("groups", "seq"), None), P(("groups", "seq"), None), P(("groups", "seq"), None))
    return jax.shard_map(
        on_device, mesh=mesh, in_specs=placed, out_specs=P(("groups", "seq"), None), check_vma=False
    )
```

time: 48 us -> 52.7 us (1.098)
  Pallas kernels: 0 us -> 13.6 us
  matrix products: 6.99 us -> 0.65 us
  local copies, waits for them, and re-layouts: 4.29 us -> 1.72 us
  waiting for transfers between devices: 10.2 us -> 8.75 us
  other arithmetic: 0.03 us -> 1.29 us
    pallas_call x0 -> x3, Pallas kernels: none -> 13.6 us  [the longest x1 5.32 us: intra_block(): pl.pallas_call(intra_kernel, grid=(steps,), in_specs=[spec] * 3, out_spec...]
    dot_general x3 -> x0, matrix products: 6.34 us -> none  [the longest x1 3.88 us: on_device(): jnp.einsum('hts,she->the', scores, v_blk, preferred_element_type=jnp.floa...]
    reshape x2 -> x0, local copies, waits for them, and re-layouts: 3.05 us -> none  [the longest x1 1.62 us: on_device(): k_blk = keys.reshape(tok, HEADS, DK)]
    all_to_all x1, waiting for transfers between devices: 10.2 us -> 8.75 us  [on_device(): lax.all_to_all(earlier.astype(jnp.bfloat16), 'seq', split_axis=0, concat_...]
    convert_element_type x0 -> x1, other arithmetic: none -> 1.29 us  [on_device(): flat = local_states(keys, values).astype(jnp.float16)]
    dot_general x1 -> x0, local copies, waits for them, and re-layouts: 1.23 us -> none  [on_device(): jnp.einsum('cb,brd->crd', lower, received.astype(jnp.float32), precision=...]
    convert_element_type x0 -> x1, local copies, waits for them, and re-layouts: none -> 0.93 us  [on_device(): earlier.astype(jnp.bfloat16)]
    unnamed x4 -> x2, local copies, waits for them, and re-layouts: 0.01 us -> 0.79 us
  transfers between devices with their start and end apart: 1 -> 1, of which waited for: 1 -> 1; matrix products, arithmetic and copies ran while one was open for 8% -> 0% of each run, Pallas kernels for 0% -> 10%
where the time goes in v3:
time: 52.7 us; the launch traced here: 51.7 us
  blocking collectives  21.2 us (40%)
  Pallas kernels  13.6 us (26%)
  waiting for transfers between devices  8.75 us (17%)
  starting transfers between devices  4.5 us (9%)
  local copies, waits for them, and re-layouts  1.72 us (3%)
  other arithmetic  1.29 us (2%)
  matrix products  0.65 us (1%)
    all_to_all x1, blocking collectives, on_device(): lax.all_to_all(flat, 'seq', split_axis=0, concat_axis=0, tiled=True)  21.2 us
    all_to_all x1, waiting for transfers between devices, on_device(): lax.all_to_all(earlier.astype(jnp.bfloat16), 'seq', split_axis=0, concat_...  8.75 us
    pallas_call x1, Pallas kernels, intra_block(): pl.pallas_call(intra_kernel, grid=(steps,), in_specs=[spec] * 3, out_spec...  5.32 us
    all_to_all x1, starting transfers between devices, on_device(): lax.all_to_all(earlier.astype(jnp.bfloat16), 'seq', split_axis=0, concat_...  4.5 us
    pallas_call x1, Pallas kernels, combine(): pl.pallas_call(functools.partial(final_kernel, scale), grid=(steps,), in_...  4.26 us
    pallas_call x1, Pallas kernels, local_states(): pl.pallas_call(state_kernel, grid=(steps,), in_specs=[pl.BlockSpec((tok,...  4.05 us
    convert_element_type x1, other arithmetic, on_device(): flat = local_states(keys, values).astype(jnp.float16)  1.29 us
  transfers between devices with their start and end apart: 1, of which 1 were waited for; matrix products, arithmetic and copies ran while one was open for 0% of the time, Pallas kernels for 10%

profile of v3, /device:TPU:1, one launch (start us, length us, event | category | flops | bytes accessed | tf_op | source)
XLA Modules:
  0.0 51.7 jit_solution(15389230651419638658)
XLA Ops:
  0.0 4.0 %shard_map.37 = f32[2048,128]{1,0:T(8,128)} custom-call(bf16[256,2048]{1,0:T(8,128)(2,1)} %k_ref.3, bf16[256,2048]{1,0:T(8,128)(2,1)} %v_ref.3), custom_call_target="tpu_custom_call" | custom-call | flops 134217728 | bytes 3145728 | tf_op jit(solution)/shard_map/pallas_call | solution.py:51
  4.0 1.3 %convert_element_type.8 = f16[2048,128]{1,0:T(8,128)(2,1)S(1)} convert(f32[2048,128]{1,0:T(8,128)} %shard_map.37) | non-fusion elementwise | flops 262144 | bytes 1572864 | tf_op jit(solution)/shard_map/convert_element_type | solution.py:101
  5.3 21.2 %all_to_all.14 = f16[16,128,128]{2,1,0:T(8,128)(2,1)S(1)} all-to-all(f16[16,128,128]{2,1,0:T(8,128)(2,1)S(1)} %bitcast.6), channel_id=1, replica_groups=mesh['groups'=2,'seq'=16] {'seq'}, dimensions={0} | all-to-all | bytes 1048576 | tf_op jit(solution)/shard_map/all_to_all | solution.py:102
  26.5 0.6 %convolution_convert_fusion = bf16[16,128,128]{2,0,1:T(8,128)(2,1)S(1)} fusion(f16[16,128,128]{2,1,0:T(8,128)(2,1)S(1)} %all_to_all.14), kind=kOutput, calls=%fused_computation | convolution fusion | flops 8651008 | bytes 1048576 | tf_op jit(solution)/shard_map/cb,brd->crd/dot_general | solution.py:107
  27.2 0.9 %copy.7 = bf16[16,128,128]{2,1,0:T(8,128)(2,1)} copy(bf16[16,128,128]{2,0,1:T(8,128)(2,1)S(1)} %convolution_convert_fusion) | data formatting | bytes 1048576 | tf_op jit(solution)/shard_map/convert_element_type | solution.py:115
  28.1 4.5 %all-to-all-start.1 = ((bf16[16,128,128]{2,1,0:T(8,128)(2,1)}), bf16[16,128,128]{2,1,0:T(8,128)(2,1)S(1)}, u32[]{:S(2)}, u32[]{:S(2)}) async-start(bf16[16,128,128]{2,1,0:T(8,128)(2,1)} %copy.7), calls=%async_computation.1 | async-start | bytes 1048576 | tf_op jit(solution)/shard_map/all_to_all | solution.py:114
  32.6 5.3 %shard_map.38.intra_ref = f32[256,2048]{1,0:T(8,128)} custom-call(bf16[256,2048]{1,0:T(8,128)(2,1)} %q_ref.3, bf16[256,2048]{1,0:T(8,128)(2,1)} %k_ref.3, bf16[256,2048]{1,0:T(8,128)(2,1)} %v_ref.3), custom_call_target="tpu_custom_call" | custom-call | flops 536870912 | bytes 5242880 | tf_op jit(solution)/shard_map/pallas_call | solution.py:68
  37.9 8.8 %all-to-all-done.1 = bf16[16,128,128]{2,1,0:T(8,128)(2,1)S(1)} async-done(((bf16[16,128,128]{2,1,0:T(8,128)(2,1)}), bf16[16,128,128]{2,1,0:T(8,128)(2,1)S(1)}, u32[]{:S(2)}, u32[]{:S(2)}) %all-to-all-start.1) | async-done | bytes 524320 | tf_op jit(solution)/shard_map/all_to_all | solution.py:114
  46.7 0.0 copy-start
  46.7 0.8 %copy-done = bf16[16,128,128]{2,1,0:T(8,128)(2,1)} copy-done((bf16[16,128,128]{2,1,0:T(8,128)(2,1)}, bf16[16,128,128]{2,1,0:T(8,128)(2,1)S(1)}, u32[]{:S(2)}) %copy-start) | copy-done | bytes 524312
  47.5 4.3 %shard_map.39 = bf16[256,2048]{1,0:T(8,128)(2,1)} custom-call(bf16[256,2048]{1,0:T(8,128)(2,1)} %q_ref.3, bf16[2048,128]{1,0:T(8,128)(2,1)} %bitcast.5, f32[256,2048]{1,0:T(8,128)} %shard_map.38.intra_ref), custom_call_target="tpu_custom_call" | custom-call | flops 134217728 | bytes 4718592 | tf_op jit(solution)/shard_map/pallas_call | solution.py:85
Async XLA Ops:
  28.1 18.6 %all-to-all-start.1 = ((bf16[16,128,128]{2,1,0:T(8,128)(2,1)}), bf16[16,128,128]{2,1,0:T(8,128)(2,1)S(1)}, u32[]{:S(2)}, u32[]{:S(2)}) async-start(bf16[16,128,128]{2,1,0:T(8,128)(2,1)} %copy.7), calls=%async_computation.1 | async-start | bytes 1048576 | tf_op jit(solution)/shard_map/all_to_all | solution.py:114
  46.7 0.8 %copy-start = (bf16[16,128,128]{2,1,0:T(8,128)(2,1)}, bf16[16,128,128]{2,1,0:T(8,128)(2,1)S(1)}, u32[]{:S(2)}) copy-start(bf16[16,128,128]{2,1,0:T(8,128)(2,1)S(1)} %all-to-all-done.1) | copy-start | bytes 1572868

commit v4 on v1

--- a/solution.py
+++ b/solution.py
@@ -14,13 +14,16 @@
     k_blk = keys.reshape(tok, HEADS, DK)
     v_blk = values.reshape(tok, HEADS, DK)
     local_state = jnp.einsum("thd,the->hde", k_blk, v_blk, preferred_element_type=jnp.float32)
-    flat = local_state.reshape(HEADS * DK, DK).astype(jnp.bfloat16)
+    flat = local_state.reshape(HEADS * DK, DK).astype(jnp.float16)
     received = lax.all_to_all(flat, "seq", split_axis=0, concat_axis=0, tiled=True)
     received = received.reshape(sources, HEADS * DK // sources, DK)
-    row_index = lax.broadcasted_iota(jnp.int32, (sources, sources), 0)
-    col_index = lax.broadcasted_iota(jnp.int32, (sources, sources), 1)
-    lower = (col_index < row_index).astype(jnp.bfloat16)
-    earlier = jnp.einsum("cb,brd->crd", lower, received, preferred_element_type=jnp.float32)
+    received = received.astype(jnp.float32)
+    running = jnp.zeros_like(received[0])
+    prefixes = []
+    for source in range(sources):
+        prefixes.append(running)
+        running = running + received[source]
+    earlier = jnp.stack(prefixes)
     summed = lax.all_to_all(
         earlier.astype(jnp.bfloat16), "seq", split_axis=0, concat_axis=0, tiled=True
     )

time: 47.7 us -> 56.7 us (1.19)
  blocking collectives: 21.2 us -> 0 us
  waiting for transfers between devices: 10.2 us -> 23.6 us
  other arithmetic: 0.03 us -> 8.86 us
  starting transfers between devices: 4.5 us -> 11.8 us
    all_to_all x1 -> x0, blocking collectives: 21.2 us -> none  [on_device(): lax.all_to_all(flat, 'seq', split_axis=0, concat_axis=0, tiled=True)]
    all_to_all x0 -> x1, waiting for transfers between devices: none -> 13.5 us  [on_device(): lax.all_to_all(flat, 'seq', split_axis=0, concat_axis=0, tiled=True)]
    unnamed x0 -> x13, other arithmetic: none -> 8.13 us
    all_to_all x0 -> x1, starting transfers between devices: none -> 7.32 us  [on_device(): lax.all_to_all(flat, 'seq', split_axis=0, concat_axis=0, tiled=True)]
    unnamed x4 -> x6, local copies, waits for them, and re-layouts: 0.01 us -> 1.25 us
    dot_general x1 -> x0, local copies, waits for them, and re-layouts: 1.23 us -> none  [on_device(): jnp.einsum('cb,brd->crd', lower, received, preferred_element_type=jnp.flo...]
    dot_general x1, matrix products: 0.42 us -> 1.22 us  [on_device(): jnp.einsum('thd,the->hde', k_blk, v_blk, preferred_element_type=jnp.float32)]
    another operation x0 -> x1, other arithmetic: none -> 0.63 us  [on_device(): earlier = jnp.stack(prefixes)]
  transfers between devices with their start and end apart: 1 -> 2, of which waited for: 1 -> 2; matrix products, arithmetic and copies ran while one was open for 8% -> 8% of each run, Pallas kernels for 0% -> 0%
where the time goes in v4:
time: 56.7 us; the launch traced here: 55.8 us
  waiting for transfers between devices  23.6 us (42%)
  starting transfers between devices  11.8 us (21%)
  other arithmetic  8.86 us (16%)
  matrix products  7.2 us (13%)
  local copies, waits for them, and re-layouts  4.3 us (8%)
    all_to_all x1, waiting for transfers between devices, on_device(): lax.all_to_all(flat, 'seq', split_axis=0, concat_axis=0, tiled=True)  13.5 us
    all_to_all x1, waiting for transfers between devices, on_device(): lax.all_to_all(earlier.astype(jnp.bfloat16), 'seq', split_axis=0, concat_...  10.2 us
    unnamed x13, other arithmetic  8.13 us
    all_to_all x1, starting transfers between devices, on_device(): lax.all_to_all(flat, 'seq', split_axis=0, concat_axis=0, tiled=True)  7.32 us
    all_to_all x1, starting transfers between devices, on_device(): lax.all_to_all(earlier.astype(jnp.bfloat16), 'seq', split_axis=0, concat_...  4.5 us
    dot_general x1, matrix products, on_device(): jnp.einsum('hts,she->the', scores, v_blk, preferred_element_type=jnp.floa...  3.88 us
    dot_general x1, matrix products, on_device(): jnp.einsum('thd,hde->the', q_blk, carried, preferred_element_type=jnp.flo...  2.09 us
    reshape x1, local copies, waits for them, and re-layouts, on_device(): k_blk = keys.reshape(tok, HEADS, DK)  1.62 us
  transfers between devices with their start and end apart: 2, of which 2 were waited for; matrix products, arithmetic and copies ran while one was open for 8% of the time, Pallas kernels for 0%

profile of v4, /device:TPU:1, one launch (start us, length us, event | category | flops | bytes accessed | tf_op | source)
XLA Modules:
  0.0 55.8 jit_solution(9288312183012298511)
XLA Ops:
  0.0 0.0 copy-start
  0.0 0.0 copy-start.1
  0.0 1.6 %copy.11 = bf16[256,2048]{0,1:T(8,128)(2,1)S(1)} copy(bf16[256,2048]{1,0:T(8,128)(2,1)} %param.4) | data formatting | bytes 2097152 | tf_op jit(solution)/shard_map/reshape | solution.py:14
  1.6 0.0 copy-done.1
  1.6 1.2 %convolution_convert_fusion = f16[16,128,128]{2,1,0:T(8,128)(2,1)} fusion(bf16[256,16,128]{0,2,1:T(8,128)(2,1)S(1)} %bitcast.39, bf16[256,2048]{1,0:T(8,128)(2,1)S(1)} %copy-done.1), kind=kOutput, calls=%fused_computation.5 | convolution fusion | flops 134479872 | bytes 2621440 | tf_op jit(solution)/shard_map/thd,the->hde/dot_general | solution.py:16
  2.9 7.3 %all-to-all-start = ((f16[16,128,128]{2,1,0:T(8,128)(2,1)}), f16[16,128,128]{2,1,0:T(8,128)(2,1)S(1)}, u32[]{:S(2)}, u32[]{:S(2)}) async-start(f16[16,128,128]{2,1,0:T(8,128)(2,1)} %convolution_convert_fusion), calls=%async_computation | async-start | bytes 1048576 | tf_op jit(solution)/shard_map/all_to_all | solution.py:18
  10.2 0.6 %constant_dynamic-update-slice_fusion.15 = bf16[16,128,128]{2,1,0:T(8,128)(2,1)} fusion(), kind=kLoop, calls=%fused_computation.46 | loop fusion | bytes 32768
  10.8 13.5 %all-to-all-done = f16[16,128,128]{2,1,0:T(8,128)(2,1)S(1)} async-done(((f16[16,128,128]{2,1,0:T(8,128)(2,1)}), f16[16,128,128]{2,1,0:T(8,128)(2,1)S(1)}, u32[]{:S(2)}, u32[]{:S(2)}) %all-to-all-start) | async-done | bytes 524320 | tf_op jit(solution)/shard_map/all_to_all | solution.py:18
  24.3 0.1 convert_element_type.16
  24.3 0.6 %constant_dynamic-update-slice_fusion.14 = bf16[16,128,128]{2,1,0:T(8,128)(2,1)} fusion(bf16[16,128,128]{2,1,0:T(8,128)(2,1)} %constant_dynamic-update-slice_fusion.15, f32[16,128,128]{2,1,0:T(8,128)S(1)} %convert_element_type.16), kind=kLoop, calls=%fused_computation.45 | loop fusion | bytes 65536
  25.0 0.6 %constant_dynamic-update-slice_fusion.13 = bf16[16,128,128]{2,1,0:T(8,128)(2,1)} fusion(bf16[16,128,128]{2,1,0:T(8,128)(2,1)} %constant_dynamic-update-slice_fusion.14, f32[16,128,128]{2,1,0:T(8,128)S(1)} %convert_element_type.16), kind=kLoop, calls=%fused_computation.44 | loop fusion | flops 32768 | bytes 163840
  25.6 0.6 %constant_dynamic-update-slice_fusion.12 = bf16[16,128,128]{2,1,0:T(8,128)(2,1)} fusion(bf16[16,128,128]{2,1,0:T(8,128)(2,1)} %constant_dynamic-update-slice_fusion.13, f32[16,128,128]{2,1,0:T(8,128)S(1)} %convert_element_type.16), kind=kLoop, calls=%fused_computation.43 | loop fusion | flops 49152 | bytes 229376
  26.2 0.6 %constant_dynamic-update-slice_fusion.11 = (bf16[16,128,128]{2,1,0:T(8,128)(2,1)}, f32[1,128,128]{2,1,0:T(8,128)S(1)}) fusion(bf16[16,128,128]{2,1,0:T(8,128)(2,1)} %constant_dynamic-update-slice_fusion.12, f32[16,128,128]{2,1,0:T(8,128)S(1)} %convert_element_type.16), kind=kLoop, calls=%fused_computation.42 | loop fusion | flops 65536 | bytes 360448
  26.9 0.6 %constant_dynamic-update-slice_fusion.10 = bf16[16,128,128]{2,1,0:T(8,128)(2,1)} fusion(bf16[16,128,128]{2,1,0:T(8,128)(2,1)} %get-tuple-element.13, f32[1,128,128]{2,1,0:T(8,128)S(1)} %get-tuple-element.14, f32[16,128,128]{2,1,0:T(8,128)S(1)} %convert_element_type.16), kind=kLoop, calls=%fused_computation.41 | loop fusion | flops 32768 | bytes 163840
  27.5 0.6 %constant_dynamic-update-slice_fusion.9 = (bf16[16,128,128]{2,1,0:T(8,128)(2,1)}, f32[1,128,128]{2,1,0:T(8,128)S(1)}) fusion(bf16[16,128,128]{2,1,0:T(8,128)(2,1)} %constant_dynamic-update-slice_fusion.10, f32[16,128,128]{2,1,0:T(8,128)S(1)} %convert_element_type.16, f32[1,128,128]{2,1,0:T(8,128)S(1)} %get-tuple-element.14), kind=kLoop, calls=%fused_computation.40 | loop fusion | flops 49152 | bytes 294912
  28.1 0.6 %constant_dynamic-update-slice_fusion.8 = bf16[16,128,128]{2,1,0:T(8,128)(2,1)} fusion(bf16[16,128,128]{2,1,0:T(8,128)(2,1)} %get-tuple-element.11, f32[1,128,128]{2,1,0:T(8,128)S(1)} %get-tuple-element.12, f32[16,128,128]{2,1,0:T(8,128)S(1)} %convert_element_type.16), kind=kLoop, calls=%fused_computation.39 | loop fusion | flops 32768 | bytes 163840
  28.7 0.6 %constant_dynamic-update-slice_fusion.7 = (bf16[16,128,128]{2,1,0:T(8,128)(2,1)}, f32[1,128,128]{2,1,0:T(8,128)S(1)}) fusion(bf16[16,128,128]{2,1,0:T(8,128)(2,1)} %constant_dynamic-update-slice_fusion.8, f32[16,128,128]{2,1,0:T(8,128)S(1)} %convert_element_type.16, f32[1,128,128]{2,1,0:T(8,128)S(1)} %get-tuple-element.12), kind=kLoop, calls=%fused_computation.38 | loop fusion | flops 49152 | bytes 294912
  29.4 0.6 %constant_dynamic-update-slice_fusion.6 = bf16[16,128,128]{2,1,0:T(8,128)(2,1)} fusion(bf16[16,128,128]{2,1,0:T(8,128)(2,1)} %get-tuple-element.9, f32[1,128,128]{2,1,0:T(8,128)S(1)} %get-tuple-element.10, f32[16,128,128]{2,1,0:T(8,128)S(1)} %convert_element_type.16), kind=kLoop, calls=%fused_computation.37 | loop fusion | flops 32768 | bytes 163840
  30.0 0.6 %constant_dynamic-update-slice_fusion.5 = (bf16[16,128,128]{2,1,0:T(8,128)(2,1)}, f32[1,128,128]{2,1,0:T(8,128)S(1)}) fusion(bf16[16,128,128]{2,1,0:T(8,128)(2,1)} %constant_dynamic-update-slice_fusion.6, f32[16,128,128]{2,1,0:T(8,128)S(1)} %convert_element_type.16, f32[1,128,128]{2,1,0:T(8,128)S(1)} %get-tuple-element.10), kind=kLoop, calls=%fused_computation.36 | loop fusion | flops 49152 | bytes 294912
  30.6 0.6 %constant_dynamic-update-slice_fusion.4 = bf16[16,128,128]{2,1,0:T(8,128)(2,1)} fusion(bf16[16,128,128]{2,1,0:T(8,128)(2,1)} %get-tuple-element.7, f32[1,128,128]{2,1,0:T(8,128)S(1)} %get-tuple-element.8, f32[16,128,128]{2,1,0:T(8,128)S(1)} %convert_element_type.16), kind=kLoop, calls=%fused_computation.35 | loop fusion | flops 32768 | bytes 163840
  31.2 0.6 %constant_dynamic-update-slice_fusion.3 = (bf16[16,128,128]{2,1,0:T(8,128)(2,1)}, f32[1,128,128]{2,1,0:T(8,128)S(1)}) fusion(bf16[16,128,128]{2,1,0:T(8,128)(2,1)} %constant_dynamic-update-slice_fusion.4, f32[16,128,128]{2,1,0:T(8,128)S(1)} %convert_element_type.16, f32[1,128,128]{2,1,0:T(8,128)S(1)} %get-tuple-element.8), kind=kLoop, calls=%fused_computation.34 | loop fusion | flops 49152 | bytes 294912
  31.9 0.6 %constant_dynamic-update-slice_fusion.2 = bf16[16,128,128]{2,1,0:T(8,128)(2,1)} fusion(bf16[16,128,128]{2,1,0:T(8,128)(2,1)} %get-tuple-element.5, f32[1,128,128]{2,1,0:T(8,128)S(1)} %get-tuple-element.6, f32[16,128,128]{2,1,0:T(8,128)S(1)} %convert_element_type.16), kind=kLoop, calls=%fused_computation.33 | loop fusion | flops 32768 | bytes 163840
  32.5 0.6 %constant_dynamic-update-slice_fusion.1 = bf16[16,128,128]{2,1,0:T(8,128)(2,1)} fusion(bf16[16,128,128]{2,1,0:T(8,128)(2,1)} %constant_dynamic-update-slice_fusion.2, f32[16,128,128]{2,1,0:T(8,128)S(1)} %convert_element_type.16, f32[1,128,128]{2,1,0:T(8,128)S(1)} %get-tuple-element.6), kind=kLoop, calls=%fused_computation.32 | loop fusion | flops 49152 | bytes 229376
  33.1 0.6 %constant_dynamic-update-slice_fusion = bf16[16,128,128]{2,1,0:T(8,128)(2,1)} fusion(bf16[16,128,128]{2,1,0:T(8,128)(2,1)} %constant_dynamic-update-slice_fusion.1, f32[16,128,128]{2,1,0:T(8,128)S(1)} %convert_element_type.16, f32[1,128,128]{2,1,0:T(8,128)S(1)} %get-tuple-element.6), kind=kLoop, calls=%fused_computation.31 | loop fusion | flops 65536 | bytes 294912 | tf_op jit(solution)/shard_map/stack | solution.py:26
  33.7 4.5 %all-to-all-start.1 = ((bf16[16,128,128]{2,1,0:T(8,128)(2,1)}), bf16[16,128,128]{2,1,0:T(8,128)(2,1)S(1)}, u32[]{:S(2)}, u32[]{:S(2)}) async-start(bf16[16,128,128]{2,1,0:T(8,128)(2,1)} %constant_dynamic-update-slice_fusion), calls=%async_computation.1 | async-start | bytes 1048576 | tf_op jit(solution)/shard_map/all_to_all | solution.py:27
  38.3 0.0 copy-done
  38.3 3.9 %fusion.2 = f32[16,256,128]{1,2,0:T(8,128)} fusion(bf16[256,16,128]{0,2,1:T(8,128)(2,1)S(1)} %bitcast.40, pred[256,256]{1,0:T(8,128)(4,1)S(1)} %iota_compare_fusion, bf16[256,2048]{1,0:T(8,128)(2,1)} %param.5, bf16[256,2048]{1,0:T(8,128)(2,1)S(1)} %copy-done), kind=kOutput, calls=%fused_computation.4 | convolution fusion | flops 538968064 | bytes 5308416 | tf_op jit(solution)/shard_map/hts,she->the/dot_general | solution.py:36
  42.2 10.2 %all-to-all-done.1 = bf16[16,128,128]{2,1,0:T(8,128)(2,1)S(1)} async-done(((bf16[16,128,128]{2,1,0:T(8,128)(2,1)}), bf16[16,128,128]{2,1,0:T(8,128)(2,1)S(1)}, u32[]{:S(2)}, u32[]{:S(2)}) %all-to-all-start.1) | async-done | bytes 524320 | tf_op jit(solution)/shard_map/all_to_all | solution.py:27
  52.3 2.1 %fusion.1 = bf16[256,16,128]{0,2,1:T(8,128)(2,1)S(1)} fusion(f32[16,256,128]{1,2,0:T(8,128)} %fusion.2, bf16[16,128,128]{2,1,0:T(8,128)(2,1)S(1)} %all-to-all-done.1, bf16[256,2048]{1,0:T(8,128)(2,1)S(1)} %copy-done), kind=kOutput, calls=%fused_computation.3 | convolution fusion | flops 135790592 | bytes 4718592 | tf_op jit(solution)/shard_map/thd,hde->the/dot_general | solution.py:37
  54.4 1.4 %copy.9 = bf16[256,2048]{1,0:T(8,128)(2,1)} copy(bf16[256,2048]{0,1:T(8,128)(2,1)S(1)} %bitcast.41) | data formatting | bytes 2097152 | tf_op jit(solution)/shard_map/reshape | solution.py:40
  (1 shorter events, 0.0 us)
Async XLA Ops:
  0.0 38.3 %copy-start = (bf16[256,2048]{1,0:T(8,128)(2,1)S(1)}, bf16[256,2048]{1,0:T(8,128)(2,1)}, u32[]{:S(2)}) copy-start(bf16[256,2048]{1,0:T(8,128)(2,1)} %param.3) | copy-start | bytes 3145732
  0.0 1.6 %copy-start.1 = (bf16[256,2048]{1,0:T(8,128)(2,1)S(1)}, bf16[256,2048]{1,0:T(8,128)(2,1)}, u32[]{:S(2)}) copy-start(bf16[256,2048]{1,0:T(8,128)(2,1)} %param.5) | copy-start | bytes 3145732
  2.9 21.4 %all-to-all-start = ((f16[16,128,128]{2,1,0:T(8,128)(2,1)}), f16[16,128,128]{2,1,0:T(8,128)(2,1)S(1)}, u32[]{:S(2)}, u32[]{:S(2)}) async-start(f16[16,128,128]{2,1,0:T(8,128)(2,1)} %convolution_convert_fusion), calls=%async_computation | async-start | bytes 1048576 | tf_op jit(solution)/shard_map/all_to_all | solution.py:18
  33.7 18.6 %all-to-all-start.1 = ((bf16[16,128,128]{2,1,0:T(8,128)(2,1)}), bf16[16,128,128]{2,1,0:T(8,128)(2,1)S(1)}, u32[]{:S(2)}, u32[]{:S(2)}) async-start(bf16[16,128,128]{2,1,0:T(8,128)(2,1)} %constant_dynamic-update-slice_fusion), calls=%async_computation.1 | async-start | bytes 1048576 | tf_op jit(solution)/shard_map/all_to_all | solution.py:27

commit v5 on v1

--- a/solution.py
+++ b/solution.py
@@ -13,14 +13,12 @@
     q_blk = queries.reshape(tok, HEADS, DK)
     k_blk = keys.reshape(tok, HEADS, DK)
     v_blk = values.reshape(tok, HEADS, DK)
-    local_state = jnp.einsum("thd,the->hde", k_blk, v_blk, preferred_element_type=jnp.float32)
-    flat = local_state.reshape(HEADS * DK, DK).astype(jnp.bfloat16)
+    local_state = jnp.einsum("the,thd->hed", v_blk, k_blk, preferred_element_type=jnp.float32)
+    flat = local_state.reshape(HEADS * DK, DK).astype(jnp.float16)
     received = lax.all_to_all(flat, "seq", split_axis=0, concat_axis=0, tiled=True)
     received = received.reshape(sources, HEADS * DK // sources, DK)
-    row_index = lax.broadcasted_iota(jnp.int32, (sources, sources), 0)
-    col_index = lax.broadcasted_iota(jnp.int32, (sources, sources), 1)
-    lower = (col_index < row_index).astype(jnp.bfloat16)
-    earlier = jnp.einsum("cb,brd->crd", lower, received, preferred_element_type=jnp.float32)
+    widened = received.astype(jnp.float32)
+    earlier = jnp.cumsum(widened, axis=0) - widened
     summed = lax.all_to_all(
         earlier.astype(jnp.bfloat16), "seq", split_axis=0, concat_axis=0, tiled=True
     )
@@ -31,7 +29,7 @@
     scores = jnp.einsum("thd,shd->hts", q_blk, k_blk, preferred_element_type=jnp.float32)
     scores = jnp.where(causal[None], scores, jnp.float32(0.0)).astype(jnp.bfloat16)
     intra = jnp.einsum("hts,she->the", scores, v_blk, preferred_element_type=jnp.float32)
-    inter = jnp.einsum("thd,hde->the", q_blk, carried, preferred_element_type=jnp.float32)
+    inter = jnp.einsum("thd,hed->the", q_blk, carried, preferred_element_type=jnp.float32)
     scale = 1.0 / jnp.sqrt(jnp.float32(DK * tok * sources))
     attended = ((intra + inter) * scale).astype(jnp.bfloat16)
     return attended.reshape(tok, HEADS * DK)

time: 47.7 us -> 47 us (0.985)
  local copies, waits for them, and re-layouts: 4.29 us -> 3.06 us
  other arithmetic: 0.03 us -> 0.96 us
    dot_general x1 -> x0, local copies, waits for them, and re-layouts: 1.23 us -> none  [on_device(): jnp.einsum('cb,brd->crd', lower, received, preferred_element_type=jnp.flo...]
    another operation x0 -> x1, other arithmetic: none -> 0.93 us  [on_device(): earlier = jnp.cumsum(widened, axis=0) - widened]
    dot_general x3 -> x2, matrix products: 2.86 us -> 2.45 us  [the longest x1 2.03 us: on_device(): jnp.einsum('thd,hed->the', q_blk, carried, preferred_element_type=jnp.flo...]
  transfers between devices with their start and end apart: 1 -> 1, of which waited for: 1 -> 1; matrix products, arithmetic and copies ran while one was open for 8% -> 9% of each run, Pallas kernels for 0% -> 0%
where the time goes in v5:
time: 47 us; the launch traced here: 46.2 us
  blocking collectives  21.2 us (45%)
  waiting for transfers between devices  10.1 us (21%)
  matrix products  6.36 us (14%)
  starting transfers between devices  4.5 us (10%)
  local copies, waits for them, and re-layouts  3.06 us (7%)
  other arithmetic  0.96 us (2%)
    all_to_all x1, blocking collectives, on_device(): lax.all_to_all(flat, 'seq', split_axis=0, concat_axis=0, tiled=True)  21.2 us
    all_to_all x1, waiting for transfers between devices, on_device(): lax.all_to_all(earlier.astype(jnp.bfloat16), 'seq', split_axis=0, concat_...  10.1 us
    all_to_all x1, starting transfers between devices, on_device(): lax.all_to_all(earlier.astype(jnp.bfloat16), 'seq', split_axis=0, concat_...  4.5 us
    dot_general x1, matrix products, on_device(): jnp.einsum('hts,she->the', scores, v_blk, preferred_element_type=jnp.floa...  3.91 us
    dot_general x1, matrix products, on_device(): jnp.einsum('thd,hed->the', q_blk, carried, preferred_element_type=jnp.flo...  2.03 us
    reshape x1, local copies, waits for them, and re-layouts, on_device(): v_blk = values.reshape(tok, HEADS, DK)  1.62 us
    reshape x1, local copies, waits for them, and re-layouts, on_device(): return attended.reshape(tok, HEADS * DK)  1.42 us
  transfers between devices with their start and end apart: 1, of which 1 were waited for; matrix products, arithmetic and copies ran while one was open for 9% of the time, Pallas kernels for 0%

profile of v5, /device:TPU:1, one launch (start us, length us, event | category | flops | bytes accessed | tf_op | source)
XLA Modules:
  0.0 46.2 jit_solution(17315377739852409016)
XLA Ops:
  0.0 0.0 copy-start
  0.0 0.0 copy-start.1
  0.0 1.6 %copy.10 = bf16[256,2048]{0,1:T(8,128)(2,1)S(1)} copy(bf16[256,2048]{1,0:T(8,128)(2,1)} %param.5) | data formatting | bytes 2097152 | tf_op jit(solution)/shard_map/reshape | solution.py:15
  1.6 0.0 copy-done.1
  1.6 0.4 convolution_convert_fusion
  2.1 21.2 %all_to_all.11 = f16[16,128,128]{2,1,0:T(8,128)(2,1)S(1)} all-to-all(f16[16,128,128]{2,1,0:T(8,128)(2,1)S(1)} %convolution_convert_fusion), channel_id=1, replica_groups=mesh['groups'=2,'seq'=16] {'seq'}, dimensions={0} | all-to-all | bytes 1048576 | tf_op jit(solution)/shard_map/all_to_all | solution.py:18
  23.3 0.9 %fusion.7 = bf16[16,128,128]{2,1,0:T(8,128)(2,1)} fusion(f16[16,128,128]{2,1,0:T(8,128)(2,1)S(1)} %all_to_all.11), kind=kOutput, calls=%fused_computation.9 | output fusion | flops 4980736 | bytes 1048576 | tf_op jit(solution)/shard_map/jit(cumsum)/reduce_window_sum | solution.py:21
  24.2 4.5 %all-to-all-start.1 = ((bf16[16,128,128]{2,1,0:T(8,128)(2,1)}), bf16[16,128,128]{2,1,0:T(8,128)(2,1)S(1)}, u32[]{:S(2)}, u32[]{:S(2)}) async-start(bf16[16,128,128]{2,1,0:T(8,128)(2,1)} %fusion.7), calls=%async_computation.1 | async-start | bytes 1048576 | tf_op jit(solution)/shard_map/all_to_all | solution.py:22
  28.7 0.0 copy-done
  28.7 3.9 %fusion.2 = f32[16,256,128]{1,2,0:T(8,128)} fusion(bf16[256,16,128]{0,2,1:T(8,128)(2,1)S(1)} %bitcast.42, pred[256,256]{1,0:T(8,128)(4,1)S(1)} %iota_compare_fusion, bf16[256,2048]{1,0:T(8,128)(2,1)} %param.4, bf16[256,2048]{1,0:T(8,128)(2,1)S(1)} %copy-done), kind=kOutput, calls=%fused_computation.4 | convolution fusion | flops 538968064 | bytes 5308416 | tf_op jit(solution)/shard_map/hts,she->the/dot_general | solution.py:31
  32.6 10.1 %all-to-all-done.1 = bf16[16,128,128]{2,1,0:T(8,128)(2,1)S(1)} async-done(((bf16[16,128,128]{2,1,0:T(8,128)(2,1)}), bf16[16,128,128]{2,1,0:T(8,128)(2,1)S(1)}, u32[]{:S(2)}, u32[]{:S(2)}) %all-to-all-start.1) | async-done | bytes 524320 | tf_op jit(solution)/shard_map/all_to_all | solution.py:22
  42.8 2.0 %fusion.1 = bf16[256,16,128]{0,2,1:T(8,128)(2,1)S(1)} fusion(f32[16,256,128]{1,2,0:T(8,128)} %fusion.2, bf16[16,128,128]{2,1,0:T(8,128)(2,1)S(1)} %all-to-all-done.1, bf16[256,2048]{1,0:T(8,128)(2,1)S(1)} %copy-done), kind=kOutput, calls=%fused_computation.3 | convolution fusion | flops 135790592 | bytes 4718592 | tf_op jit(solution)/shard_map/thd,hed->the/dot_general | solution.py:32
  44.8 1.4 %copy.8 = bf16[256,2048]{1,0:T(8,128)(2,1)} copy(bf16[256,2048]{0,1:T(8,128)(2,1)S(1)} %bitcast.43) | data formatting | bytes 2097152 | tf_op jit(solution)/shard_map/reshape | solution.py:35
  (1 shorter events, 0.0 us)
Async XLA Ops:
  0.0 28.7 %copy-start = (bf16[256,2048]{1,0:T(8,128)(2,1)S(1)}, bf16[256,2048]{1,0:T(8,128)(2,1)}, u32[]{:S(2)}) copy-start(bf16[256,2048]{1,0:T(8,128)(2,1)} %param.3) | copy-start | bytes 3145732
  0.0 1.6 %copy-start.1 = (bf16[256,2048]{1,0:T(8,128)(2,1)S(1)}, bf16[256,2048]{1,0:T(8,128)(2,1)}, u32[]{:S(2)}) copy-start(bf16[256,2048]{1,0:T(8,128)(2,1)} %param.4) | copy-start | bytes 3145732
  24.2 18.6 %all-to-all-start.1 = ((bf16[16,128,128]{2,1,0:T(8,128)(2,1)}), bf16[16,128,128]{2,1,0:T(8,128)(2,1)S(1)}, u32[]{:S(2)}, u32[]{:S(2)}) async-start(bf16[16,128,128]{2,1,0:T(8,128)(2,1)} %fusion.7), calls=%async_computation.1 | async-start | bytes 1048576 | tf_op jit(solution)/shard_map/all_to_all | solution.py:22

commit v6 on v3

v6 whole, which is shorter than its diff:
```python
import functools

import jax
import numpy as np
import jax.numpy as jnp
from jax import lax
from jax.experimental import pallas as pl
from jax.experimental.pallas import tpu as pltpu
from jax.sharding import PartitionSpec as P

HEADS = 16
DK = 128
GROUP = 8


def intra_kernel(q_ref, k_ref, v_ref, o_ref):
    tok = q_ref.shape[0]
    rows = lax.broadcasted_iota(jnp.int32, (tok, tok), 0)
    cols_i = lax.broadcasted_iota(jnp.int32, (tok, tok), 1)
    causal = cols_i <= rows
    for j in range(GROUP):
        cols = slice(j * DK, (j + 1) * DK)
        s = lax.dot_general(
            q_ref[:, cols], k_ref[:, cols], (((1,), (1,)), ((), ())),
            preferred_element_type=jnp.float32,
        )
        s = jnp.where(causal, s, jnp.float32(0.0)).astype(jnp.bfloat16)
        o_ref[:, cols] = jnp.dot(s, v_ref[:, cols], preferred_element_type=jnp.float32)


def final_kernel(scale, q_ref, p_ref, intra_ref, o_ref):
    base = pl.program_id(0) * (GROUP * DK)
    for j in range(GROUP):
        cols = slice(j * DK, (j + 1) * DK)
        start = pl.multiple_of(base + j * DK, DK)
        inter = lax.dot_general(
            q_ref[:, cols], p_ref[pl.ds(start, DK), :], (((1,), (1,)), ((), ())),
            preferred_element_type=jnp.float32,
        )
        o_ref[:, cols] = ((intra_ref[:, cols] + inter) * scale).astype(o_ref.dtype)


def intra_block(queries, keys, values):
    tok = queries.shape[0]
    spec = pl.BlockSpec((tok, GROUP * DK), lambda i: (0, i))
    return pl.pallas_call(
        intra_kernel,
        grid=(HEADS // GROUP,),
        in_specs=[spec] * 3,
        out_specs=spec,
        out_shape=jax.ShapeDtypeStruct((tok, HEADS * DK), jnp.float32),
        cost_estimate=pl.CostEstimate(
            flops=4 * tok * tok * DK * HEADS, transcendentals=0,
            bytes_accessed=3 * tok * HEADS * DK * 2 + tok * HEADS * DK * 4,
        ),
    )(queries, keys, values)


def combine(queries, carried_t, intra, scale):
    tok = queries.shape[0]
    spec = pl.BlockSpec((tok, GROUP * DK), lambda i: (0, i))
    return pl.pallas_call(
        functools.partial(final_kernel, scale),
        grid=(HEADS // GROUP,),
        in_specs=[spec, pl.BlockSpec(memory_space=pltpu.VMEM), spec],
        out_specs=spec,
        out_shape=jax.ShapeDtypeStruct((tok, HEADS * DK), jnp.bfloat16),
        cost_estimate=pl.CostEstimate(
            flops=2 * tok * DK * DK * HEADS, transcendentals=0,
            bytes_accessed=2 * tok * HEADS * DK * 2 + tok * HEADS * DK * 4 + HEADS * DK * DK * 2,
        ),
    )(queries, carried_t, intra)


def on_device(queries, keys, values):
    tok = queries.shape[0]
    sources = lax.axis_size("seq")
    q_blk = queries.reshape(tok, HEADS, DK)
    k_blk = keys.reshape(tok, HEADS, DK)
    v_blk = values.reshape(tok, HEADS, DK)
    local_state = jnp.einsum("the,thd->hed", v_blk, k_blk, preferred_element_type=jnp.float32)
    flat = local_state.reshape(HEADS * DK, DK).astype(jnp.float16)
    received = lax.all_to_all(flat, "seq", split_axis=0, concat_axis=0, tiled=True)
    received = received.reshape(sources, HEADS * DK // sources, DK)
    widened = received.astype(jnp.float32)
    earlier = jnp.cumsum(widened, axis=0) - widened
    summed = lax.all_to_all(
        earlier.astype(jnp.bfloat16), "seq", split_axis=0, concat_axis=0, tiled=True
    )
    carried_t = summed.reshape(HEADS * DK, DK)
    intra = intra_block(queries, keys, values)
    scale = float(np.float32(1.0) / np.sqrt(np.float32(DK * tok * sources)))
    return combine(queries, carried_t, intra, scale)

def solution(mesh):
    placed = (P(("groups", "seq"), None), P(("groups", "seq"), None), P(("groups", "seq"), None))
    return jax.shard_map(
        on_device, mesh=mesh, in_specs=placed, out_specs=P(("groups", "seq"), None), check_vma=False
    )
```

time: 52.7 us -> 47.4 us (0.90)
  Pallas kernels: 13.6 us -> 7.32 us
  waiting for transfers between devices: 8.75 us -> 9.87 us
  local copies, waits for them, and re-layouts: 1.72 us -> 2.36 us
    pallas_call x3 -> x2, Pallas kernels: 13.6 us -> 7.32 us  [the longest x1 4.2 us: intra_block(): pl.pallas_call(intra_kernel, grid=(HEADS // GROUP,), in_specs=[spec] * 3,...]
    reshape x0 -> x1, local copies, waits for them, and re-layouts: none -> 1.56 us  [on_device(): v_blk = values.reshape(tok, HEADS, DK)]
    convert_element_type x1 -> x0, other arithmetic: 1.29 us -> none  [on_device(): flat = local_states(keys, values).astype(jnp.float16)]
    all_to_all x1, waiting for transfers between devices: 8.75 us -> 9.87 us  [on_device(): lax.all_to_all(earlier.astype(jnp.bfloat16), 'seq', split_axis=0, concat_...]
    another operation x0 -> x1, other arithmetic: none -> 0.93 us  [on_device(): earlier = jnp.cumsum(widened, axis=0) - widened]
    convert_element_type x1 -> x0, local copies, waits for them, and re-layouts: 0.93 us -> none  [on_device(): earlier.astype(jnp.bfloat16)]
  transfers between devices with their start and end apart: 1 -> 1, of which waited for: 1 -> 1; matrix products, arithmetic and copies ran while one was open for 0% -> 0% of each run, Pallas kernels for 10% -> 9%
where the time goes in v6:
time: 47.4 us; the launch traced here: 46.6 us
  blocking collectives  21.2 us (45%)
  waiting for transfers between devices  9.87 us (21%)
  Pallas kernels  7.32 us (15%)
  starting transfers between devices  4.5 us (9%)
  local copies, waits for them, and re-layouts  2.36 us (5%)
  other arithmetic  0.93 us (2%)
    all_to_all x1, blocking collectives, on_device(): lax.all_to_all(flat, 'seq', split_axis=0, concat_axis=0, tiled=True)  21.2 us
    all_to_all x1, waiting for transfers between devices, on_device(): lax.all_to_all(earlier.astype(jnp.bfloat16), 'seq', split_axis=0, concat_...  9.87 us
    all_to_all x1, starting transfers between devices, on_device(): lax.all_to_all(earlier.astype(jnp.bfloat16), 'seq', split_axis=0, concat_...  4.5 us
    pallas_call x1, Pallas kernels, intra_block(): pl.pallas_call(intra_kernel, grid=(HEADS // GROUP,), in_specs=[spec] * 3,...  4.2 us
    pallas_call x1, Pallas kernels, combine(): pl.pallas_call(functools.partial(final_kernel, scale), grid=(HEADS // GRO...  3.12 us
    reshape x1, local copies, waits for them, and re-layouts, on_device(): v_blk = values.reshape(tok, HEADS, DK)  1.56 us
  transfers between devices with their start and end apart: 1, of which 1 were waited for; matrix products, arithmetic and copies ran while one was open for 0% of the time, Pallas kernels for 9%

profile of v6, /device:TPU:1, one launch (start us, length us, event | category | flops | bytes accessed | tf_op | source)
XLA Modules:
  0.0 46.6 jit_solution(7989332105968340239)
XLA Ops:
  0.0 0.0 copy-start
  0.0 1.6 %copy.6 = bf16[256,2048]{0,1:T(8,128)(2,1)S(1)} copy(bf16[256,2048]{1,0:T(8,128)(2,1)} %v_ref.1) | data formatting | bytes 2097152 | tf_op jit(solution)/shard_map/reshape | solution.py:80
  1.6 0.0 copy-done
  1.6 0.4 convolution_convert_fusion
  2.0 21.2 %all_to_all.11 = f16[16,128,128]{2,1,0:T(8,128)(2,1)S(1)} all-to-all(f16[16,128,128]{2,1,0:T(8,128)(2,1)S(1)} %convolution_convert_fusion), channel_id=1, replica_groups=mesh['groups'=2,'seq'=16] {'seq'}, dimensions={0} | all-to-all | bytes 1048576 | tf_op jit(solution)/shard_map/all_to_all | solution.py:83
  23.2 0.9 %fusion.4 = bf16[16,128,128]{2,1,0:T(8,128)(2,1)} fusion(f16[16,128,128]{2,1,0:T(8,128)(2,1)S(1)} %all_to_all.11), kind=kOutput, calls=%fused_computation.4 | output fusion | flops 4980736 | bytes 1048576 | tf_op jit(solution)/shard_map/jit(cumsum)/reduce_window_sum | solution.py:86
  24.1 4.5 %all-to-all-start.1 = ((bf16[16,128,128]{2,1,0:T(8,128)(2,1)}), bf16[16,128,128]{2,1,0:T(8,128)(2,1)S(1)}, u32[]{:S(2)}, u32[]{:S(2)}) async-start(bf16[16,128,128]{2,1,0:T(8,128)(2,1)} %fusion.4), calls=%async_computation.1 | async-start | bytes 1048576 | tf_op jit(solution)/shard_map/all_to_all | solution.py:87
  28.6 4.2 %shard_map.37.intra_ref = f32[256,2048]{1,0:T(8,128)} custom-call(bf16[256,2048]{1,0:T(8,128)(2,1)} %q_ref.3, bf16[256,2048]{1,0:T(8,128)(2,1)} %k_ref.1, bf16[256,2048]{1,0:T(8,128)(2,1)} %v_ref.1), custom_call_target="tpu_custom_call" | custom-call | flops 536870912 | bytes 5242880 | tf_op jit(solution)/shard_map/pallas_call | solution.py:46
  32.8 9.9 %all-to-all-done.1 = bf16[16,128,128]{2,1,0:T(8,128)(2,1)S(1)} async-done(((bf16[16,128,128]{2,1,0:T(8,128)(2,1)}), bf16[16,128,128]{2,1,0:T(8,128)(2,1)S(1)}, u32[]{:S(2)}, u32[]{:S(2)}) %all-to-all-start.1) | async-done | bytes 524320 | tf_op jit(solution)/shard_map/all_to_all | solution.py:87
  42.7 0.0 copy-start.1
  42.7 0.8 %copy-done.1 = bf16[16,128,128]{2,1,0:T(8,128)(2,1)} copy-done((bf16[16,128,128]{2,1,0:T(8,128)(2,1)}, bf16[16,128,128]{2,1,0:T(8,128)(2,1)S(1)}, u32[]{:S(2)}) %copy-start.1) | copy-done | bytes 524312
  43.5 3.1 %shard_map.38 = bf16[256,2048]{1,0:T(8,128)(2,1)} custom-call(bf16[256,2048]{1,0:T(8,128)(2,1)} %q_ref.3, bf16[2048,128]{1,0:T(8,128)(2,1)} %bitcast.11, f32[256,2048]{1,0:T(8,128)} %shard_map.37.intra_ref), custom_call_target="tpu_custom_call" | custom-call | flops 134217728 | bytes 4718592 | tf_op jit(solution)/shard_map/pallas_call | solution.py:62
Async XLA Ops:
  0.0 1.6 %copy-start = (bf16[256,2048]{1,0:T(8,128)(2,1)S(1)}, bf16[256,2048]{1,0:T(8,128)(2,1)}, u32[]{:S(2)}) copy-start(bf16[256,2048]{1,0:T(8,128)(2,1)} %k_ref.1) | copy-start | bytes 3145732
  24.1 18.6 %all-to-all-start.1 = ((bf16[16,128,128]{2,1,0:T(8,128)(2,1)}), bf16[16,128,128]{2,1,0:T(8,128)(2,1)S(1)}, u32[]{:S(2)}, u32[]{:S(2)}) async-start(bf16[16,128,128]{2,1,0:T(8,128)(2,1)} %fusion.4), calls=%async_computation.1 | async-start | bytes 1048576 | tf_op jit(solution)/shard_map/all_to_all | solution.py:87
  42.7 0.8 %copy-start.1 = (bf16[16,128,128]{2,1,0:T(8,128)(2,1)}, bf16[16,128,128]{2,1,0:T(8,128)(2,1)S(1)}, u32[]{:S(2)}) copy-start(bf16[16,128,128]{2,1,0:T(8,128)(2,1)S(1)} %all-to-all-done.1) | copy-start | bytes 1572868

commit v7 on v5

v7 whole, which is shorter than its diff:
```python
import math

import jax
import jax.numpy as jnp
import numpy as np
from jax import lax
from jax.sharding import Mesh
from jax.sharding import PartitionSpec as P

HEADS = 16
DK = 128
LIMIT = 6.0
F16_MAX = 65504.0


def swap_cores(x):
    return lax.ppermute(x, "core", [(0, 1), (1, 0)])


def on_device(queries, keys, values):
    tok = queries.shape[0]
    chips = lax.axis_size("chip")
    core = lax.axis_index("core")
    sources = chips * lax.axis_size("core")
    q_blk = queries.reshape(tok, HEADS, DK)
    k_blk = keys.reshape(tok, HEADS, DK)
    v_blk = values.reshape(tok, HEADS, DK)
    local_state = jnp.einsum("the,thd->hed", v_blk, k_blk, preferred_element_type=jnp.float32)
    flat = local_state.reshape(HEADS * DK, DK)
    half = HEADS * DK // 2
    own = lax.dynamic_slice_in_dim(flat, core * half, half)
    other = lax.dynamic_slice_in_dim(flat, (1 - core) * half, half)
    partner = swap_cores(other)
    chip_sum = own + partner
    received = lax.all_to_all(chip_sum.astype(jnp.float16), "chip", split_axis=0, concat_axis=0, tiled=True)
    received = received.reshape(chips, half // chips, DK).astype(jnp.float32)
    earlier = jnp.cumsum(received, axis=0) - received
    bound = (chips - 1) * 2 * tok * LIMIT * LIMIT
    shift = max(0, math.ceil(math.log2(bound / F16_MAX)))
    down = np.float32(2.0 ** -shift)
    back = lax.all_to_all((earlier * down).astype(jnp.float16), "chip", split_axis=0, concat_axis=0, tiled=True)
    chip_prefix = back.reshape(half, DK).astype(jnp.float32) * np.float32(2.0 ** shift)
    first = core == 0
    kept = (chip_prefix + jnp.where(first, jnp.float32(0.0), partner)).astype(jnp.bfloat16)
    sent = (chip_prefix + jnp.where(first, own, jnp.float32(0.0))).astype(jnp.bfloat16)
    got = swap_cores(sent)
    low = jnp.where(first, kept, got)
    high = jnp.where(first, got, kept)
    carried = jnp.concatenate([low, high], axis=0).reshape(HEADS, DK, DK)
    rows = lax.broadcasted_iota(jnp.int32, (tok, tok), 0)
    cols = lax.broadcasted_iota(jnp.int32, (tok, tok), 1)
    causal = cols <= rows
    scores = jnp.einsum("thd,shd->hts", q_blk, k_blk, preferred_element_type=jnp.float32)
    scores = jnp.where(causal[None], scores, jnp.float32(0.0)).astype(jnp.bfloat16)
    intra = jnp.einsum("hts,she->the", scores, v_blk, preferred_element_type=jnp.float32)
    inter = jnp.einsum("thd,hed->the", q_blk, carried, preferred_element_type=jnp.float32)
    scale = 1.0 / jnp.sqrt(jnp.float32(DK * tok * sources))
    attended = ((intra + inter) * scale).astype(jnp.bfloat16)
    return attended.reshape(tok, HEADS * DK)


def solution(mesh):
    devices = mesh.devices
    split = Mesh(devices.reshape(devices.shape[0], devices.shape[1] // 2, 2), ("groups", "chip", "core"))
    spec = P(("groups", "chip", "core"), None)
    return jax.shard_map(
        on_device, mesh=split, in_specs=(spec, spec, spec), out_specs=spec, check_vma=False
    )
```

time: 47 us -> 45.6 us (0.970)
  blocking collectives: 21.2 us -> 14.2 us
  starting transfers between devices: 4.5 us -> 7.27 us
  other arithmetic: 0.96 us -> 3.41 us
  local copies, waits for them, and re-layouts: 3.06 us -> 4.19 us
  waiting for transfers between devices: 10.1 us -> 9.35 us
    all_to_all x1, blocking collectives: 21.2 us -> 14.2 us  [on_device(): lax.all_to_all(chip_sum.astype(jnp.float16), 'chip', split_axis=0, concat...]
    all_to_all x1, waiting for transfers between devices: 10.1 us -> 7.15 us  [on_device(): lax.all_to_all((earlier * down).astype(jnp.float16), 'chip', split_axis=0...]
    ppermute x0 -> x2, starting transfers between devices: none -> 2.81 us  [swap_cores(): return lax.ppermute(x, 'core', [(0, 1), (1, 0)])]
    ppermute x0 -> x2, waiting for transfers between devices: none -> 2.2 us  [swap_cores(): return lax.ppermute(x, 'core', [(0, 1), (1, 0)])]
    dot_general x1, matrix products: 0.42 us -> 2.03 us  [on_device(): jnp.einsum('the,thd->hed', v_blk, k_blk, preferred_element_type=jnp.float32)]
    dot_general x1, matrix products: 2.03 us -> 0.48 us  [on_device(): jnp.einsum('thd,hed->the', q_blk, carried, preferred_element_type=jnp.flo...]
    select_n x0 -> x2, other arithmetic: none -> 1.33 us  [the longest x1 1.3 us: on_device(): low = jnp.where(first, kept, got)]
    convert_element_type x0 -> x2, other arithmetic: none -> 1.17 us  [the longest x1 1.1 us: on_device(): chip_sum.astype(jnp.float16)]
  transfers between devices with their start and end apart: 1 -> 3, of which waited for: 1 -> 2; matrix products, arithmetic and copies ran while one was open for 9% -> 9% of each run, Pallas kernels for 0% -> 0%
where the time goes in v7:
time: 45.6 us; the launch traced here: 45.2 us
  blocking collectives  14.2 us (31%)
  waiting for transfers between devices  9.35 us (21%)
  starting transfers between devices  7.27 us (16%)
  matrix products  6.73 us (15%)
  local copies, waits for them, and re-layouts  4.19 us (9%)
  other arithmetic  3.41 us (7%)
    all_to_all x1, blocking collectives, on_device(): lax.all_to_all(chip_sum.astype(jnp.float16), 'chip', split_axis=0, concat...  14.2 us
    all_to_all x1, waiting for transfers between devices, on_device(): lax.all_to_all((earlier * down).astype(jnp.float16), 'chip', split_axis=0...  7.15 us
    all_to_all x1, starting transfers between devices, on_device(): lax.all_to_all((earlier * down).astype(jnp.float16), 'chip', split_axis=0...  4.45 us
    dot_general x1, matrix products, on_device(): jnp.einsum('hts,she->the', scores, v_blk, preferred_element_type=jnp.floa...  4.22 us
    ppermute x2, starting transfers between devices, swap_cores(): return lax.ppermute(x, 'core', [(0, 1), (1, 0)])  2.81 us
    ppermute x2, waiting for transfers between devices, swap_cores(): return lax.ppermute(x, 'core', [(0, 1), (1, 0)])  2.2 us
    dot_general x1, matrix products, on_device(): jnp.einsum('the,thd->hed', v_blk, k_blk, preferred_element_type=jnp.float32)  2.03 us
    reshape x1, local copies, waits for them, and re-layouts, on_device(): v_blk = values.reshape(tok, HEADS, DK)  1.56 us
  transfers between devices with their start and end apart: 3, of which 2 were waited for; matrix products, arithmetic and copies ran while one was open for 9% of the time, Pallas kernels for 0%

profile of v7, /device:TPU:1, one launch (start us, length us, event | category | flops | bytes accessed | tf_op | source)
XLA Modules:
  0.0 45.2 jit_solution(8108064988552842390)
XLA Ops:
  0.0 0.0 copy-start
  0.0 1.6 %copy.10 = bf16[256,2048]{0,1:T(8,128)(2,1)S(1)} copy(bf16[256,2048]{1,0:T(8,128)(2,1)} %param.5) | data formatting | bytes 2097152 | tf_op jit(solution)/shard_map/reshape | solution.py:27
  1.6 0.0 copy-start.1
  1.6 2.0 %fusion.7 = f32[16,128,128]{2,1,0:T(8,128)S(1)} fusion(bf16[256,16,128]{0,2,1:T(8,128)(2,1)S(1)} %bitcast.55, bf16[256,2048]{1,0:T(8,128)(2,1)} %param.4), kind=kOutput, calls=%fused_computation.9 | convolution fusion | flops 134217728 | bytes 3145728 | tf_op jit(solution)/shard_map/the,thd->hed/dot_general | solution.py:28
  3.6 0.8 %constant_dynamic-slice_fusion = f32[1024,128]{1,0:T(8,128)} fusion(f32[2048,128]{1,0:T(8,128)S(1)} %bitcast.52, s32[]{:T(128)S(6)} %select_n.37), kind=kLoop, calls=%fused_computation.28 | loop fusion | bytes 1048580 | tf_op jit(solution)/shard_map/dynamic_slice | solution.py:32
  4.4 0.0 copy-done.1
  4.5 0.1 collective-permute-start
  4.5 2.2 %collective-permute-done = f32[1024,128]{1,0:T(8,128)} collective-permute-done((f32[1024,128]{1,0:T(8,128)}, f32[1024,128]{1,0:T(8,128)}, u32[]{:S(2)}, u32[]{:S(2)}) %collective-permute-start) | collective-permute-done | bytes 524320 | tf_op jit(solution)/shard_map/ppermute | solution.py:17
  6.7 1.1 %add_convert_fusion = f16[1024,128]{1,0:T(8,128)(2,1)S(1)} fusion(f32[1024,128]{1,0:T(8,128)} %collective-permute-done, f32[2048,128]{1,0:T(8,128)S(1)} %bitcast.53, s32[]{:T(128)S(6)} %select_n.36), kind=kLoop, calls=%fused_computation.24 | loop fusion | flops 262144 | bytes 1310724 | tf_op jit(solution)/shard_map/convert_element_type | solution.py:35
  7.8 14.2 %all_to_all.14 = f16[8,128,128]{2,1,0:T(8,128)(2,1)S(1)} all-to-all(f16[8,128,128]{2,1,0:T(8,128)(2,1)S(1)} %bitcast.59), channel_id=1, replica_groups=mesh['groups'=2,'chip'=8,'core'=2] {'chip'}, dimensions={0} | all-to-all | bytes 524288 | tf_op jit(solution)/shard_map/all_to_all | solution.py:35
  22.0 0.8 %fusion.4 = f16[8,128,128]{2,1,0:T(8,128)(2,1)} fusion(f16[8,128,128]{2,1,0:T(8,128)(2,1)S(1)} %all_to_all.14), kind=kOutput, calls=%fused_computation.7 | output fusion | flops 1441792 | bytes 524288 | tf_op jit(solution)/shard_map/jit(cumsum)/reduce_window_sum | solution.py:37
  22.8 4.5 %all-to-all-start.1 = ((f16[8,128,128]{2,1,0:T(8,128)(2,1)}), f16[8,128,128]{2,1,0:T(8,128)(2,1)S(1)}, u32[]{:S(2)}, u32[]{:S(2)}) async-start(f16[8,128,128]{2,1,0:T(8,128)(2,1)} %fusion.4), calls=%async_computation.1 | async-start | bytes 524288 | tf_op jit(solution)/shard_map/all_to_all | solution.py:41
  27.2 7.2 %all-to-all-done.1 = f16[8,128,128]{2,1,0:T(8,128)(2,1)S(1)} async-done(((f16[8,128,128]{2,1,0:T(8,128)(2,1)}), f16[8,128,128]{2,1,0:T(8,128)(2,1)S(1)}, u32[]{:S(2)}, u32[]{:S(2)}) %all-to-all-start.1) | async-done | bytes 262176 | tf_op jit(solution)/shard_map/all_to_all | solution.py:41
  34.5 0.1 fusion.19
  34.5 2.8 %collective-permute-start.1 = (bf16[1024,128]{1,0:T(8,128)(2,1)S(1)}, bf16[1024,128]{1,0:T(8,128)(2,1)S(1)}, u32[]{:S(2)}, u32[]{:S(2)}) collective-permute-start(bf16[1024,128]{1,0:T(8,128)(2,1)S(1)} %fusion.19), channel_id=1, source_target_pairs={{0,1},{1,0},{2,3},{3,2},{4,5},{5,4},{6,7},{7,6},{8,9},{9,8},{10,11... | collective-permute-start | bytes 786440 | tf_op jit(solution)/shard_map/ppermute | solution.py:17
  37.3 0.0 copy-done
  37.3 4.2 %fusion.2 = f32[16,256,128]{1,2,0:T(8,128)} fusion(bf16[256,16,128]{0,2,1:T(8,128)(2,1)} %bitcast.56, pred[256,256]{1,0:T(8,128)(4,1)S(1)} %iota_compare_fusion, bf16[256,2048]{1,0:T(8,128)(2,1)} %param.4, bf16[256,2048]{1,0:T(8,128)(2,1)S(1)} %copy-done), kind=kOutput, calls=%fused_computation.4 | convolution fusion | flops 538968064 | bytes 5308416 | tf_op jit(solution)/shard_map/hts,she->the/dot_general | solution.py:55
  41.5 0.0 copy-start.2
  41.5 0.0 collective-permute-done.1
  41.5 1.3 %broadcast_select_fusion.1 = (bf16[1024,128]{1,0:T(8,128)(2,1)S(1)}, bf16[1024,128]{1,0:T(8,128)(2,1)S(1)}) fusion(bf16[1024,128]{1,0:T(8,128)(2,1)S(1)} %collective-permute-done.1, pred[]{:T(512)S(6)} %eq.3, f32[1024,128]{1,0:T(8,128)} %collective-permute-done, f32[8,128,128]{2,1,0:T(8,128)S(1)} %convert_multiply_fusion), kind=kLoop, calls=%fused_computation.27 | loop fusion | flops 524288 | bytes 1835009 | tf_op jit(solution)/shard_map/jit(_where)/select_n | solution.py:47
  42.9 0.4 copy-done.2
  43.3 0.5 %fusion.1 = bf16[256,16,128]{0,2,1:T(8,128)(2,1)S(1)} fusion(f32[16,256,128]{1,2,0:T(8,128)S(1)} %copy-done.2, bf16[16,128,128]{2,1,0:T(8,128)(2,1)S(1)} %bitcast.58, bf16[256,2048]{1,0:T(8,128)(2,1)S(1)} %copy-done), kind=kOutput, calls=%fused_computation.3 | convolution fusion | flops 135790592 | bytes 4718592 | tf_op jit(solution)/shard_map/thd,hed->the/dot_general | solution.py:56
  43.8 1.4 %copy.8 = bf16[256,2048]{1,0:T(8,128)(2,1)} copy(bf16[256,2048]{0,1:T(8,128)(2,1)S(1)} %bitcast.57) | data formatting | bytes 2097152 | tf_op jit(solution)/shard_map/reshape | solution.py:59
  (4 shorter events, 0.1 us)
Async XLA Ops:
  0.0 37.3 %copy-start = (bf16[256,2048]{1,0:T(8,128)(2,1)S(1)}, bf16[256,2048]{1,0:T(8,128)(2,1)}, u32[]{:S(2)}) copy-start(bf16[256,2048]{1,0:T(8,128)(2,1)} %param.3) | copy-start | bytes 3145732
  1.6 2.9 %copy-start.1 = (bf16[256,2048]{0,1:T(8,128)(2,1)}, bf16[256,2048]{0,1:T(8,128)(2,1)S(1)}, u32[]{:S(2)}) copy-start(bf16[256,2048]{0,1:T(8,128)(2,1)S(1)} %copy.10) | copy-start | bytes 3145732
  4.5 2.3 %collective-permute-start = (f32[1024,128]{1,0:T(8,128)}, f32[1024,128]{1,0:T(8,128)}, u32[]{:S(2)}, u32[]{:S(2)}) collective-permute-start(f32[1024,128]{1,0:T(8,128)} %constant_dynamic-slice_fusion), channel_id=1, source_target_pairs={{0,1},{1,0},{2,3},{3,2},{4,5},{5,4},{6,7},{7,6},{8,9},{9,8},{10,11... | collective-permute-start | bytes 1572872 | tf_op jit(solution)/shard_map/ppermute | solution.py:17
  22.8 11.6 %all-to-all-start.1 = ((f16[8,128,128]{2,1,0:T(8,128)(2,1)}), f16[8,128,128]{2,1,0:T(8,128)(2,1)S(1)}, u32[]{:S(2)}, u32[]{:S(2)}) async-start(f16[8,128,128]{2,1,0:T(8,128)(2,1)} %fusion.4), calls=%async_computation.1 | async-start | bytes 524288 | tf_op jit(solution)/shard_map/all_to_all | solution.py:41
  34.5 7.0 %collective-permute-start.1 = (bf16[1024,128]{1,0:T(8,128)(2,1)S(1)}, bf16[1024,128]{1,0:T(8,128)(2,1)S(1)}, u32[]{:S(2)}, u32[]{:S(2)}) collective-permute-start(bf16[1024,128]{1,0:T(8,128)(2,1)S(1)} %fusion.19), channel_id=1, source_target_pairs={{0,1},{1,0},{2,3},{3,2},{4,5},{5,4},{6,7},{7,6},{8,9},{9,8},{10,11... | collective-permute-start | bytes 786440 | tf_op jit(solution)/shard_map/ppermute | solution.py:17
  41.5 1.7 %copy-start.2 = (f32[16,256,128]{1,2,0:T(8,128)S(1)}, f32[16,256,128]{1,2,0:T(8,128)}, u32[]{:S(2)}) copy-start(f32[16,256,128]{1,2,0:T(8,128)} %fusion.2) | copy-start | bytes 6291460

commit v8 on v7

--- a/solution.py
+++ b/solution.py
@@ -43,16 +43,17 @@
     first = core == 0
     kept = (chip_prefix + jnp.where(first, jnp.float32(0.0), partner)).astype(jnp.bfloat16)
     sent = (chip_prefix + jnp.where(first, own, jnp.float32(0.0))).astype(jnp.bfloat16)
-    got = swap_cores(sent)
-    low = jnp.where(first, kept, got)
-    high = jnp.where(first, got, kept)
-    carried = jnp.concatenate([low, high], axis=0).reshape(HEADS, DK, DK)
     rows = lax.broadcasted_iota(jnp.int32, (tok, tok), 0)
     cols = lax.broadcasted_iota(jnp.int32, (tok, tok), 1)
     causal = cols <= rows
     scores = jnp.einsum("thd,shd->hts", q_blk, k_blk, preferred_element_type=jnp.float32)
     scores = jnp.where(causal[None], scores, jnp.float32(0.0)).astype(jnp.bfloat16)
     intra = jnp.einsum("hts,she->the", scores, v_blk, preferred_element_type=jnp.float32)
+    sent, intra = lax.optimization_barrier((sent, intra))
+    got = swap_cores(sent)
+    low = jnp.where(first, kept, got)
+    high = jnp.where(first, got, kept)
+    carried = jnp.concatenate([low, high], axis=0).reshape(HEADS, DK, DK)
     inter = jnp.einsum("thd,hed->the", q_blk, carried, preferred_element_type=jnp.float32)
     scale = 1.0 / jnp.sqrt(jnp.float32(DK * tok * sources))
     attended = ((intra + inter) * scale).astype(jnp.bfloat16)

time: 45.6 us -> 43.2 us (0.947)
  blocking collectives: 14.2 us -> 0 us
  starting transfers between devices: 7.27 us -> 13.9 us
  waiting for transfers between devices: 9.35 us -> 14.4 us
  matrix products: 6.73 us -> 6.04 us
  other arithmetic: 3.41 us -> 3.97 us
    all_to_all x1 -> x0, blocking collectives: 14.2 us -> none  [on_device(): lax.all_to_all(chip_sum.astype(jnp.float16), 'chip', split_axis=0, concat...]
    all_to_all x0 -> x1, waiting for transfers between devices: none -> 7.7 us  [on_device(): lax.all_to_all(chip_sum.astype(jnp.float16), 'chip', split_axis=0, concat...]
    all_to_all x0 -> x1, starting transfers between devices: none -> 6.66 us  [on_device(): lax.all_to_all(chip_sum.astype(jnp.float16), 'chip', split_axis=0, concat...]
    all_to_all x1, waiting for transfers between devices: 7.15 us -> 3.31 us  [on_device(): lax.all_to_all((earlier * down).astype(jnp.float16), 'chip', split_axis=0...]
    ppermute x2, waiting for transfers between devices: 2.2 us -> 3.36 us  [swap_cores(): return lax.ppermute(x, 'core', [(0, 1), (1, 0)])]
    convert_element_type x1, other arithmetic: 1.1 us -> 1.8 us  [on_device(): chip_sum.astype(jnp.float16)]
    convert_element_type x0 -> x1, local copies, waits for them, and re-layouts: none -> 0.53 us  [on_device(): attended = ((intra + inter) * scale).astype(jnp.bfloat16)]
  transfers between devices with their start and end apart: 3 -> 4, of which waited for: 2 -> 4; matrix products, arithmetic and copies ran while one was open for 9% -> 9% of each run, Pallas kernels for 0% -> 0%
where the time goes in v8:
time: 43.2 us; the launch traced here: 42.8 us
  waiting for transfers between devices  14.4 us (33%)
  starting transfers between devices  13.9 us (32%)
  matrix products  6.04 us (14%)
  local copies, waits for them, and re-layouts  4.36 us (10%)
  other arithmetic  3.97 us (9%)
    all_to_all x1, waiting for transfers between devices, on_device(): lax.all_to_all(chip_sum.astype(jnp.float16), 'chip', split_axis=0, concat...  7.7 us
    all_to_all x1, starting transfers between devices, on_device(): lax.all_to_all(chip_sum.astype(jnp.float16), 'chip', split_axis=0, concat...  6.66 us
    all_to_all x1, starting transfers between devices, on_device(): lax.all_to_all((earlier * down).astype(jnp.float16), 'chip', split_axis=0...  4.45 us
    dot_general x1, matrix products, on_device(): jnp.einsum('hts,she->the', scores, v_blk, preferred_element_type=jnp.floa...  3.83 us
    ppermute x2, waiting for transfers between devices, swap_cores(): return lax.ppermute(x, 'core', [(0, 1), (1, 0)])  3.36 us
    all_to_all x1, waiting for transfers between devices, on_device(): lax.all_to_all((earlier * down).astype(jnp.float16), 'chip', split_axis=0...  3.31 us
    ppermute x2, starting transfers between devices, swap_cores(): return lax.ppermute(x, 'core', [(0, 1), (1, 0)])  2.81 us
    convert_element_type x1, other arithmetic, on_device(): chip_sum.astype(jnp.float16)  1.8 us
  transfers between devices with their start and end apart: 4, of which 4 were waited for; matrix products, arithmetic and copies ran while one was open for 9% of the time, Pallas kernels for 0%

profile of v8, /device:TPU:1, one launch (start us, length us, event | category | flops | bytes accessed | tf_op | source)
XLA Modules:
  0.0 42.8 jit_solution(10835292801187562474)
XLA Ops:
  0.0 0.0 copy-start
  0.0 1.6 %copy.18 = bf16[256,2048]{0,1:T(8,128)(2,1)S(1)} copy(bf16[256,2048]{1,0:T(8,128)(2,1)} %param.4) | data formatting | bytes 2097152 | tf_op jit(solution)/shard_map/reshape | solution.py:26
  1.6 1.7 %fusion.9 = f32[16,128,128]{2,1,0:T(8,128)S(1)} fusion(bf16[256,16,128]{0,2,1:T(8,128)(2,1)S(1)} %bitcast.53, bf16[256,2048]{1,0:T(8,128)(2,1)} %param.5), kind=kOutput, calls=%fused_computation.11 | convolution fusion | flops 134217728 | bytes 3145728 | tf_op jit(solution)/shard_map/the,thd->hed/dot_general | solution.py:28
  3.3 0.8 %constant_dynamic-slice_fusion = f32[1024,128]{1,0:T(8,128)} fusion(f32[2048,128]{1,0:T(8,128)S(1)} %bitcast.50, s32[]{:T(128)S(6)} %select_n.35), kind=kLoop, calls=%fused_computation.29 | loop fusion | bytes 1048580 | tf_op jit(solution)/shard_map/dynamic_slice | solution.py:32
  4.1 0.1 collective-permute-start
  4.2 2.2 %collective-permute-done = f32[1024,128]{1,0:T(8,128)} collective-permute-done((f32[1024,128]{1,0:T(8,128)}, f32[1024,128]{1,0:T(8,128)}, u32[]{:S(2)}, u32[]{:S(2)}) %collective-permute-start) | collective-permute-done | bytes 524320 | tf_op jit(solution)/shard_map/ppermute | solution.py:17
  6.4 1.8 %add_convert_fusion = f16[1024,128]{1,0:T(8,128)(2,1)} fusion(f32[1024,128]{1,0:T(8,128)} %collective-permute-done, f32[2048,128]{1,0:T(8,128)S(1)} %bitcast.51, s32[]{:T(128)S(6)} %select_n.34), kind=kLoop, calls=%fused_computation.25 | loop fusion | flops 262144 | bytes 1310724 | tf_op jit(solution)/shard_map/convert_element_type | solution.py:35
  8.2 6.7 %all-to-all-start = ((f16[8,128,128]{2,1,0:T(8,128)(2,1)}), f16[8,128,128]{2,1,0:T(8,128)(2,1)S(1)}, u32[]{:S(2)}, u32[]{:S(2)}) async-start(f16[8,128,128]{2,1,0:T(8,128)(2,1)} %bitcast.1), calls=%async_computation | async-start | bytes 524288 | tf_op jit(solution)/shard_map/all_to_all | solution.py:35
  14.8 7.7 %all-to-all-done = f16[8,128,128]{2,1,0:T(8,128)(2,1)S(1)} async-done(((f16[8,128,128]{2,1,0:T(8,128)(2,1)}), f16[8,128,128]{2,1,0:T(8,128)(2,1)S(1)}, u32[]{:S(2)}, u32[]{:S(2)}) %all-to-all-start) | async-done | bytes 262176 | tf_op jit(solution)/shard_map/all_to_all | solution.py:35
  22.5 0.8 %fusion.5 = f16[8,128,128]{2,1,0:T(8,128)(2,1)} fusion(f16[8,128,128]{2,1,0:T(8,128)(2,1)S(1)} %all-to-all-done), kind=kOutput, calls=%fused_computation.8 | output fusion | flops 1441792 | bytes 524288 | tf_op jit(solution)/shard_map/jit(cumsum)/reduce_window_sum | solution.py:37
  23.3 4.5 %all-to-all-start.1 = ((f16[8,128,128]{2,1,0:T(8,128)(2,1)}), f16[8,128,128]{2,1,0:T(8,128)(2,1)S(1)}, u32[]{:S(2)}, u32[]{:S(2)}) async-start(f16[8,128,128]{2,1,0:T(8,128)(2,1)} %fusion.5), calls=%async_computation.1 | async-start | bytes 524288 | tf_op jit(solution)/shard_map/all_to_all | solution.py:41
  27.8 0.0 copy-done
  27.8 3.8 %fusion.3 = f32[256,16,128]{2,0,1:T(8,128)} fusion(bf16[256,16,128]{0,2,1:T(8,128)(2,1)S(1)} %bitcast.54, pred[256,256]{1,0:T(8,128)(4,1)S(1)} %iota_compare_fusion, bf16[256,2048]{1,0:T(8,128)(2,1)S(1)} %copy-done, bf16[256,2048]{1,0:T(8,128)(2,1)} %param.5), kind=kOutput, calls=%fused_computation.5 | convolution fusion | flops 538968064 | bytes 5308416 | tf_op jit(solution)/shard_map/hts,she->the/dot_general | solution.py:51
  31.7 3.3 %all-to-all-done.1 = f16[8,128,128]{2,1,0:T(8,128)(2,1)S(1)} async-done(((f16[8,128,128]{2,1,0:T(8,128)(2,1)}), f16[8,128,128]{2,1,0:T(8,128)(2,1)S(1)}, u32[]{:S(2)}, u32[]{:S(2)}) %all-to-all-start.1) | async-done | bytes 262176 | tf_op jit(solution)/shard_map/all_to_all | solution.py:41
  35.0 0.1 fusion.17
  35.1 0.0 copy-start.1
  35.1 2.8 %collective-permute-start.1 = (bf16[1024,128]{1,0:T(8,128)(2,1)S(1)}, bf16[1024,128]{1,0:T(8,128)(2,1)S(1)}, u32[]{:S(2)}, u32[]{:S(2)}) collective-permute-start(bf16[1024,128]{1,0:T(8,128)(2,1)S(1)} %fusion.17), channel_id=1, source_target_pairs={{0,1},{1,0},{2,3},{3,2},{4,5},{5,4},{6,7},{7,6},{8,9},{9,8},{10,11... | collective-permute-start | bytes 786440 | tf_op jit(solution)/shard_map/ppermute | solution.py:17
  37.9 1.2 %collective-permute-done.1 = bf16[1024,128]{1,0:T(8,128)(2,1)S(1)} collective-permute-done((bf16[1024,128]{1,0:T(8,128)(2,1)S(1)}, bf16[1024,128]{1,0:T(8,128)(2,1)S(1)}, u32[]{:S(2)}, u32[]{:S(2)}) %collective-permute-start.1) | collective-permute-done | bytes 262176 | tf_op jit(solution)/shard_map/ppermute | solution.py:17
  39.0 1.1 %broadcast_select_fusion.1 = (bf16[1024,128]{1,0:T(8,128)(2,1)S(1)}, bf16[1024,128]{1,0:T(8,128)(2,1)S(1)}) fusion(bf16[1024,128]{1,0:T(8,128)(2,1)S(1)} %collective-permute-done.1, pred[]{:T(512)S(6)} %eq.3, f32[1024,128]{1,0:T(8,128)} %collective-permute-done, f32[8,128,128]{2,1,0:T(8,128)S(1)} %convert_multiply_fusion), kind=kLoop, calls=%fused_computation.28 | loop fusion | flops 524288 | bytes 1835009 | tf_op jit(solution)/shard_map/jit(_where)/select_n | solution.py:54
  40.3 0.0 copy-done.1
  40.3 0.5 %fusion.1 = bf16[256,16,128]{2,0,1:T(8,128)(2,1)S(1)} fusion(f32[256,16,128]{2,0,1:T(8,128)S(1)} %copy-done.1, bf16[16,128,128]{2,1,0:T(8,128)(2,1)S(1)} %bitcast.56, bf16[256,2048]{1,0:T(8,128)(2,1)S(1)} %copy-done), kind=kOutput, calls=%fused_computation.3 | convolution fusion | flops 135790592 | bytes 4718592 | tf_op jit(solution)/shard_map/thd,hed->the/dot_general | solution.py:57
  40.8 0.5 %copy.14 = bf16[256,16,128]{0,2,1:T(8,128)(2,1)S(1)} copy(bf16[256,16,128]{2,0,1:T(8,128)(2,1)S(1)} %fusion.1) | data formatting | bytes 2097152 | tf_op jit(solution)/shard_map/convert_element_type | solution.py:59
  41.3 1.4 %copy.15 = bf16[256,2048]{1,0:T(8,128)(2,1)} copy(bf16[256,2048]{0,1:T(8,128)(2,1)S(1)} %bitcast.55) | data formatting | bytes 2097152 | tf_op jit(solution)/shard_map/reshape | solution.py:60
  (4 shorter events, 0.1 us)
Async XLA Ops:
  0.0 27.8 %copy-start = (bf16[256,2048]{1,0:T(8,128)(2,1)S(1)}, bf16[256,2048]{1,0:T(8,128)(2,1)}, u32[]{:S(2)}) copy-start(bf16[256,2048]{1,0:T(8,128)(2,1)} %param.3) | copy-start | bytes 3145732
  4.1 2.3 %collective-permute-start = (f32[1024,128]{1,0:T(8,128)}, f32[1024,128]{1,0:T(8,128)}, u32[]{:S(2)}, u32[]{:S(2)}) collective-permute-start(f32[1024,128]{1,0:T(8,128)} %constant_dynamic-slice_fusion), channel_id=1, source_target_pairs={{0,1},{1,0},{2,3},{3,2},{4,5},{5,4},{6,7},{7,6},{8,9},{9,8},{10,11... | collective-permute-start | bytes 1572872 | tf_op jit(solution)/shard_map/ppermute | solution.py:17
  8.2 14.4 %all-to-all-start = ((f16[8,128,128]{2,1,0:T(8,128)(2,1)}), f16[8,128,128]{2,1,0:T(8,128)(2,1)S(1)}, u32[]{:S(2)}, u32[]{:S(2)}) async-start(f16[8,128,128]{2,1,0:T(8,128)(2,1)} %bitcast.1), calls=%async_computation | async-start | bytes 524288 | tf_op jit(solution)/shard_map/all_to_all | solution.py:35
  23.3 11.6 %all-to-all-start.1 = ((f16[8,128,128]{2,1,0:T(8,128)(2,1)}), f16[8,128,128]{2,1,0:T(8,128)(2,1)S(1)}, u32[]{:S(2)}, u32[]{:S(2)}) async-start(f16[8,128,128]{2,1,0:T(8,128)(2,1)} %fusion.5), calls=%async_computation.1 | async-start | bytes 524288 | tf_op jit(solution)/shard_map/all_to_all | solution.py:41
  35.1 5.2 %copy-start.1 = (f32[256,16,128]{2,0,1:T(8,128)S(1)}, f32[256,16,128]{2,0,1:T(8,128)}, u32[]{:S(2)}) copy-start(f32[256,16,128]{2,0,1:T(8,128)} %fusion.3) | copy-start | bytes 6291460
  35.1 3.9 %collective-permute-start.1 = (bf16[1024,128]{1,0:T(8,128)(2,1)S(1)}, bf16[1024,128]{1,0:T(8,128)(2,1)S(1)}, u32[]{:S(2)}, u32[]{:S(2)}) collective-permute-start(bf16[1024,128]{1,0:T(8,128)(2,1)S(1)} %fusion.17), channel_id=1, source_target_pairs={{0,1},{1,0},{2,3},{3,2},{4,5},{5,4},{6,7},{7,6},{8,9},{9,8},{10,11... | collective-permute-start | bytes 786440 | tf_op jit(solution)/shard_map/ppermute | solution.py:17

commit v9 on v8

--- a/solution.py
+++ b/solution.py
@@ -25,12 +25,16 @@
     q_blk = queries.reshape(tok, HEADS, DK)
     k_blk = keys.reshape(tok, HEADS, DK)
     v_blk = values.reshape(tok, HEADS, DK)
-    local_state = jnp.einsum("the,thd->hed", v_blk, k_blk, preferred_element_type=jnp.float32)
-    flat = local_state.reshape(HEADS * DK, DK)
     half = HEADS * DK // 2
-    own = lax.dynamic_slice_in_dim(flat, core * half, half)
-    other = lax.dynamic_slice_in_dim(flat, (1 - core) * half, half)
-    partner = swap_cores(other)
+
+    def half_state(index):
+        k_half = lax.dynamic_slice_in_dim(keys, index * half, half, axis=1).reshape(tok, HEADS // 2, DK)
+        v_half = lax.dynamic_slice_in_dim(values, index * half, half, axis=1).reshape(tok, HEADS // 2, DK)
+        state = jnp.einsum("the,thd->hed", v_half, k_half, preferred_element_type=jnp.float32)
+        return state.reshape(half, DK)
+
+    partner = swap_cores(half_state(1 - core))
+    own = half_state(core)
     chip_sum = own + partner
     received = lax.all_to_all(chip_sum.astype(jnp.float16), "chip", split_axis=0, concat_axis=0, tiled=True)
     received = received.reshape(chips, half // chips, DK).astype(jnp.float32)

time: 43.2 us -> 47.6 us (1.10)
  local copies, waits for them, and re-layouts: 4.36 us -> 9.14 us
  waiting for transfers between devices: 14.4 us -> 13.1 us
  matrix products: 6.04 us -> 6.76 us
    dynamic_slice x1 -> x4, local copies, waits for them, and re-layouts: 0.84 us -> 5.61 us  [the longest x3 4.73 us: half_state(): lax.dynamic_slice_in_dim(values, index * half, half, axis=1)]
    ppermute x2, waiting for transfers between devices: 3.36 us -> 1.16 us  [swap_cores(): return lax.ppermute(x, 'core', [(0, 1), (1, 0)])]
    unnamed x4 -> x5, local copies, waits for them, and re-layouts: 0.01 us -> 1.57 us
    reshape x1 -> x0, local copies, waits for them, and re-layouts: 1.56 us -> none  [on_device(): k_blk = keys.reshape(tok, HEADS, DK)]
    dot_general x1 -> x2, matrix products: 1.7 us -> 2.44 us  [half_state(): jnp.einsum('the,thd->hed', v_half, k_half, preferred_element_type=jnp.flo...]
    all_to_all x1, waiting for transfers between devices: 7.7 us -> 8.22 us  [on_device(): lax.all_to_all(chip_sum.astype(jnp.float16), 'chip', split_axis=0, concat...]
  transfers between devices with their start and end apart: 4 -> 4, of which waited for: 4 -> 3; matrix products, arithmetic and copies ran while one was open for 9% -> 14% of each run, Pallas kernels for 0% -> 0%
where the time goes in v9:
time: 47.6 us; the launch traced here: 47 us
  starting transfers between devices  13.9 us (29%)
  waiting for transfers between devices  13.1 us (28%)
  local copies, waits for them, and re-layouts  9.14 us (19%)
  matrix products  6.76 us (14%)
  other arithmetic  3.96 us (8%)
    all_to_all x1, waiting for transfers between devices, on_device(): lax.all_to_all(chip_sum.astype(jnp.float16), 'chip', split_axis=0, concat...  8.22 us
    all_to_all x1, starting transfers between devices, on_device(): lax.all_to_all(chip_sum.astype(jnp.float16), 'chip', split_axis=0, concat...  6.97 us
    dynamic_slice x3, local copies, waits for them, and re-layouts, half_state(): lax.dynamic_slice_in_dim(values, index * half, half, axis=1)  4.73 us
    all_to_all x1, starting transfers between devices, on_device(): lax.all_to_all((earlier * down).astype(jnp.float16), 'chip', split_axis=0...  4.49 us
    dot_general x1, matrix products, on_device(): jnp.einsum('hts,she->the', scores, v_blk, preferred_element_type=jnp.floa...  3.82 us
    all_to_all x1, waiting for transfers between devices, on_device(): lax.all_to_all((earlier * down).astype(jnp.float16), 'chip', split_axis=0...  3.74 us
    dot_general x2, matrix products, half_state(): jnp.einsum('the,thd->hed', v_half, k_half, preferred_element_type=jnp.flo...  2.44 us
    ppermute x2, starting transfers between devices, swap_cores(): return lax.ppermute(x, 'core', [(0, 1), (1, 0)])  2.39 us
  transfers between devices with their start and end apart: 4, of which 3 were waited for; matrix products, arithmetic and copies ran while one was open for 14% of the time, Pallas kernels for 0%

profile of v9, /device:TPU:1, one launch (start us, length us, event | category | flops | bytes accessed | tf_op | source)
XLA Modules:
  0.0 47.0 jit_solution(9226614410389100723)
XLA Ops:
  0.0 0.0 copy-start
  0.0 1.6 %copy.10 = bf16[256,2048]{0,1:T(8,128)(2,1)S(1)} copy(bf16[256,2048]{1,0:T(8,128)(2,1)} %param.4) | data formatting | bytes 2097152 | tf_op args[1]
  1.6 0.9 %constant_dynamic-slice_fusion.2 = (bf16[256,1024]{0,1:T(8,128)(2,1)}, bf16[256,1024]{0,1:T(8,128)(2,1)S(1)}) fusion(bf16[256,2048]{0,1:T(8,128)(2,1)S(1)} %copy.10, s32[]{:T(128)S(6)} %select_n.36, s32[]{:T(128)S(6)} %select_n.37), kind=kLoop, calls=%fused_computation.30 | loop fusion | bytes 2097160 | tf_op jit(solution)/shard_map/dynamic_slice | solution.py:31
  2.5 2.2 %constant_dynamic-slice_fusion.3 = (bf16[256,1024]{1,0:T(8,128)(2,1)}, bf16[256,1024]{1,0:T(8,128)(2,1)}) fusion(bf16[256,2048]{1,0:T(8,128)(2,1)} %param.5, s32[]{:T(128)S(6)} %select_n.36, s32[]{:T(128)S(6)} %select_n.37), kind=kLoop, calls=%fused_computation.31 | loop fusion | bytes 2097160 | tf_op jit(solution)/shard_map/dynamic_slice | solution.py:32
  4.7 1.2 %copy.12 = bf16[256,1024]{0,1:T(8,128)(2,1)S(1)} copy(bf16[256,1024]{1,0:T(8,128)(2,1)} %get-tuple-element.14) | data formatting | bytes 1048576 | tf_op jit(solution)/shard_map/dynamic_slice | solution.py:32
  5.9 1.1 %fusion.21 = f32[8,128,128]{2,1,0:T(8,128)} fusion(bf16[256,8,128]{0,2,1:T(8,128)(2,1)S(1)} %bitcast.63, bf16[256,8,128]{0,2,1:T(8,128)(2,1)S(1)} %bitcast.65), kind=kOutput, calls=%fused_computation.34 | convolution fusion | flops 67108864 | bytes 1572864 | tf_op jit(solution)/shard_map/the,thd->hed/dot_general | solution.py:33
  7.0 0.1 collective-permute-start
  7.1 1.2 %copy.9 = bf16[256,1024]{0,1:T(8,128)(2,1)S(1)} copy(bf16[256,1024]{1,0:T(8,128)(2,1)} %get-tuple-element.13) | data formatting | bytes 1048576 | tf_op jit(solution)/shard_map/dynamic_slice | solution.py:32
  8.3 1.3 %fusion.20 = f32[8,128,128]{2,1,0:T(8,128)S(1)} fusion(bf16[256,8,128]{0,2,1:T(8,128)(2,1)S(1)} %bitcast.61, bf16[256,8,128]{0,2,1:T(8,128)(2,1)} %bitcast.64), kind=kOutput, calls=%fused_computation.33 | convolution fusion | flops 67108864 | bytes 1572864 | tf_op jit(solution)/shard_map/the,thd->hed/dot_general | solution.py:33
  9.7 0.0 collective-permute-done
  9.7 1.8 %fusion.16 = f16[1024,128]{1,0:T(8,128)(2,1)} fusion(f32[1024,128]{1,0:T(8,128)} %collective-permute-done, f32[8,128,128]{2,1,0:T(8,128)S(1)} %fusion.20), kind=kLoop, calls=%fused_computation.22 | loop fusion | flops 262144 | bytes 1310720 | tf_op jit(solution)/shard_map/convert_element_type | solution.py:39
  11.5 7.0 %all-to-all-start = ((f16[8,128,128]{2,1,0:T(8,128)(2,1)}), f16[8,128,128]{2,1,0:T(8,128)(2,1)S(1)}, u32[]{:S(2)}, u32[]{:S(2)}) async-start(f16[8,128,128]{2,1,0:T(8,128)(2,1)} %bitcast.6), calls=%async_computation | async-start | bytes 524288 | tf_op jit(solution)/shard_map/all_to_all | solution.py:39
  18.5 8.2 %all-to-all-done = f16[8,128,128]{2,1,0:T(8,128)(2,1)S(1)} async-done(((f16[8,128,128]{2,1,0:T(8,128)(2,1)}), f16[8,128,128]{2,1,0:T(8,128)(2,1)S(1)}, u32[]{:S(2)}, u32[]{:S(2)}) %all-to-all-start) | async-done | bytes 262176 | tf_op jit(solution)/shard_map/all_to_all | solution.py:39
  26.7 0.8 %fusion.5 = f16[8,128,128]{2,1,0:T(8,128)(2,1)} fusion(f16[8,128,128]{2,1,0:T(8,128)(2,1)S(1)} %all-to-all-done), kind=kOutput, calls=%fused_computation.8 | output fusion | flops 1441792 | bytes 524288 | tf_op jit(solution)/shard_map/jit(cumsum)/reduce_window_sum | solution.py:41
  27.5 4.5 %all-to-all-start.1 = ((f16[8,128,128]{2,1,0:T(8,128)(2,1)}), f16[8,128,128]{2,1,0:T(8,128)(2,1)S(1)}, u32[]{:S(2)}, u32[]{:S(2)}) async-start(f16[8,128,128]{2,1,0:T(8,128)(2,1)} %fusion.5), calls=%async_computation.1 | async-start | bytes 524288 | tf_op jit(solution)/shard_map/all_to_all | solution.py:45
  32.0 0.0 copy-done
  32.0 3.8 %fusion.3 = f32[256,16,128]{2,0,1:T(8,128)} fusion(bf16[256,16,128]{0,2,1:T(8,128)(2,1)S(1)} %bitcast.60, pred[256,256]{1,0:T(8,128)(4,1)S(1)} %iota_compare_fusion, bf16[256,2048]{1,0:T(8,128)(2,1)} %param.5, bf16[256,2048]{1,0:T(8,128)(2,1)S(1)} %copy-done), kind=kOutput, calls=%fused_computation.5 | convolution fusion | flops 538968064 | bytes 5308416 | tf_op jit(solution)/shard_map/hts,she->the/dot_general | solution.py:55
  35.9 3.7 %all-to-all-done.1 = f16[8,128,128]{2,1,0:T(8,128)(2,1)S(1)} async-done(((f16[8,128,128]{2,1,0:T(8,128)(2,1)}), f16[8,128,128]{2,1,0:T(8,128)(2,1)S(1)}, u32[]{:S(2)}, u32[]{:S(2)}) %all-to-all-start.1) | async-done | bytes 262176 | tf_op jit(solution)/shard_map/all_to_all | solution.py:45
  39.6 0.1 fusion.14
  39.7 0.0 copy-start.1
  39.7 2.3 %collective-permute-start.1 = (bf16[1024,128]{1,0:T(8,128)(2,1)S(1)}, bf16[1024,128]{1,0:T(8,128)(2,1)S(1)}, u32[]{:S(2)}, u32[]{:S(2)}) collective-permute-start(bf16[1024,128]{1,0:T(8,128)(2,1)S(1)} %fusion.14), channel_id=1, source_target_pairs={{0,1},{1,0},{2,3},{3,2},{4,5},{5,4},{6,7},{7,6},{8,9},{9,8},{10,11... | collective-permute-start | bytes 786440 | tf_op jit(solution)/shard_map/ppermute | solution.py:17
  42.1 1.2 %collective-permute-done.1 = bf16[1024,128]{1,0:T(8,128)(2,1)S(1)} collective-permute-done((bf16[1024,128]{1,0:T(8,128)(2,1)S(1)}, bf16[1024,128]{1,0:T(8,128)(2,1)S(1)}, u32[]{:S(2)}, u32[]{:S(2)}) %collective-permute-start.1) | collective-permute-done | bytes 262176 | tf_op jit(solution)/shard_map/ppermute | solution.py:17
  43.2 1.1 %broadcast_select_fusion.1 = (bf16[1024,128]{1,0:T(8,128)(2,1)S(1)}, bf16[1024,128]{1,0:T(8,128)(2,1)S(1)}) fusion(bf16[1024,128]{1,0:T(8,128)(2,1)S(1)} %collective-permute-done.1, pred[]{:T(512)S(6)} %eq.3, f32[1024,128]{1,0:T(8,128)} %collective-permute-done, f32[8,128,128]{2,1,0:T(8,128)S(1)} %convert_multiply_fusion), kind=kLoop, calls=%fused_computation.27 | loop fusion | flops 524288 | bytes 1835009 | tf_op jit(solution)/shard_map/jit(_where)/select_n | solution.py:58
  44.5 0.0 copy-done.1
  44.5 0.5 %fusion.1 = bf16[256,16,128]{2,0,1:T(8,128)(2,1)S(1)} fusion(f32[256,16,128]{2,0,1:T(8,128)S(1)} %copy-done.1, bf16[16,128,128]{2,1,0:T(8,128)(2,1)S(1)} %bitcast.62, bf16[256,2048]{1,0:T(8,128)(2,1)S(1)} %copy-done), kind=kOutput, calls=%fused_computation.3 | convolution fusion | flops 135790592 | bytes 4718592 | tf_op jit(solution)/shard_map/thd,hed->the/dot_general | solution.py:61
  45.0 0.5 %copy.18 = bf16[256,16,128]{0,2,1:T(8,128)(2,1)S(1)} copy(bf16[256,16,128]{2,0,1:T(8,128)(2,1)S(1)} %fusion.1) | data formatting | bytes 2097152 | tf_op jit(solution)/shard_map/convert_element_type | solution.py:63
  45.5 1.4 %copy.19 = bf16[256,2048]{1,0:T(8,128)(2,1)} copy(bf16[256,2048]{0,1:T(8,128)(2,1)S(1)} %bitcast.59) | data formatting | bytes 2097152 | tf_op jit(solution)/shard_map/reshape | solution.py:64
  (4 shorter events, 0.1 us)
Async XLA Ops:
  0.0 32.0 %copy-start = (bf16[256,2048]{1,0:T(8,128)(2,1)S(1)}, bf16[256,2048]{1,0:T(8,128)(2,1)}, u32[]{:S(2)}) copy-start(bf16[256,2048]{1,0:T(8,128)(2,1)} %param.3) | copy-start | bytes 3145732
  7.0 2.6 %collective-permute-start = (f32[1024,128]{1,0:T(8,128)}, f32[1024,128]{1,0:T(8,128)}, u32[]{:S(2)}, u32[]{:S(2)}) collective-permute-start(f32[1024,128]{1,0:T(8,128)} %bitcast.5), channel_id=1, source_target_pairs={{0,1},{1,0},{2,3},{3,2},{4,5},{5,4},{6,7},{7,6},{8,9},{9,8},{10,11... | collective-permute-start | bytes 1572872 | tf_op jit(solution)/shard_map/ppermute | solution.py:17
  11.5 15.2 %all-to-all-start = ((f16[8,128,128]{2,1,0:T(8,128)(2,1)}), f16[8,128,128]{2,1,0:T(8,128)(2,1)S(1)}, u32[]{:S(2)}, u32[]{:S(2)}) async-start(f16[8,128,128]{2,1,0:T(8,128)(2,1)} %bitcast.6), calls=%async_computation | async-start | bytes 524288 | tf_op jit(solution)/shard_map/all_to_all | solution.py:39
  27.5 12.1 %all-to-all-start.1 = ((f16[8,128,128]{2,1,0:T(8,128)(2,1)}), f16[8,128,128]{2,1,0:T(8,128)(2,1)S(1)}, u32[]{:S(2)}, u32[]{:S(2)}) async-start(f16[8,128,128]{2,1,0:T(8,128)(2,1)} %fusion.5), calls=%async_computation.1 | async-start | bytes 524288 | tf_op jit(solution)/shard_map/all_to_all | solution.py:45
  39.7 4.7 %copy-start.1 = (f32[256,16,128]{2,0,1:T(8,128)S(1)}, f32[256,16,128]{2,0,1:T(8,128)}, u32[]{:S(2)}) copy-start(f32[256,16,128]{2,0,1:T(8,128)} %fusion.3) | copy-start | bytes 6291460
  39.7 3.5 %collective-permute-start.1 = (bf16[1024,128]{1,0:T(8,128)(2,1)S(1)}, bf16[1024,128]{1,0:T(8,128)(2,1)S(1)}, u32[]{:S(2)}, u32[]{:S(2)}) collective-permute-start(bf16[1024,128]{1,0:T(8,128)(2,1)S(1)} %fusion.14), channel_id=1, source_target_pairs={{0,1},{1,0},{2,3},{3,2},{4,5},{5,4},{6,7},{7,6},{8,9},{9,8},{10,11... | collective-permute-start | bytes 786440 | tf_op jit(solution)/shard_map/ppermute | solution.py:17

commit v10 on v8

--- a/solution.py
+++ b/solution.py
@@ -28,9 +28,9 @@
     local_state = jnp.einsum("the,thd->hed", v_blk, k_blk, preferred_element_type=jnp.float32)
     flat = local_state.reshape(HEADS * DK, DK)
     half = HEADS * DK // 2
+    partner_all = swap_cores(flat.astype(jnp.float16))
     own = lax.dynamic_slice_in_dim(flat, core * half, half)
-    other = lax.dynamic_slice_in_dim(flat, (1 - core) * half, half)
-    partner = swap_cores(other)
+    partner = lax.dynamic_slice_in_dim(partner_all, core * half, half).astype(jnp.float32)
     chip_sum = own + partner
     received = lax.all_to_all(chip_sum.astype(jnp.float16), "chip", split_axis=0, concat_axis=0, tiled=True)
     received = received.reshape(chips, half // chips, DK).astype(jnp.float32)

time: 43.2 us -> 43.4 us (level)
  local copies, waits for them, and re-layouts: 4.36 us -> 3.53 us
  other arithmetic: 3.97 us -> 4.67 us
    convert_element_type x0 -> x1, other arithmetic: none -> 0.86 us  [on_device(): partner_all = swap_cores(flat.astype(jnp.float16))]
    dynamic_slice x1 -> x0, local copies, waits for them, and re-layouts: 0.84 us -> none  [on_device(): other = lax.dynamic_slice_in_dim(flat, (1 - core) * half, half)]
where the time goes in v10:
time: 43.4 us; the launch traced here: 42.6 us
  waiting for transfers between devices  14.4 us (33%)
  starting transfers between devices  13.9 us (32%)
  matrix products  6.03 us (14%)
  other arithmetic  4.67 us (11%)
  local copies, waits for them, and re-layouts  3.53 us (8%)
    all_to_all x1, waiting for transfers between devices, on_device(): lax.all_to_all(chip_sum.astype(jnp.float16), 'chip', split_axis=0, concat...  7.7 us
    all_to_all x1, starting transfers between devices, on_device(): lax.all_to_all(chip_sum.astype(jnp.float16), 'chip', split_axis=0, concat...  6.66 us
    all_to_all x1, starting transfers between devices, on_device(): lax.all_to_all((earlier * down).astype(jnp.float16), 'chip', split_axis=0...  4.45 us
    dot_general x1, matrix products, on_device(): jnp.einsum('hts,she->the', scores, v_blk, preferred_element_type=jnp.floa...  3.83 us
    ppermute x2, waiting for transfers between devices, swap_cores(): return lax.ppermute(x, 'core', [(0, 1), (1, 0)])  3.36 us
    all_to_all x1, waiting for transfers between devices, on_device(): lax.all_to_all((earlier * down).astype(jnp.float16), 'chip', split_axis=0...  3.31 us
    ppermute x2, starting transfers between devices, swap_cores(): return lax.ppermute(x, 'core', [(0, 1), (1, 0)])  2.81 us
    convert_element_type x1, other arithmetic, on_device(): chip_sum.astype(jnp.float16)  1.72 us
  transfers between devices with their start and end apart: 4, of which 4 were waited for; matrix products, arithmetic and copies ran while one was open for 9% of the time, Pallas kernels for 0%

profile of v10, /device:TPU:1, one launch (start us, length us, event | category | flops | bytes accessed | tf_op | source)
XLA Modules:
  0.0 42.6 jit_solution(16165621768285002081)
XLA Ops:
  0.0 0.0 copy-start
  0.0 1.6 %copy.18 = bf16[256,2048]{0,1:T(8,128)(2,1)S(1)} copy(bf16[256,2048]{1,0:T(8,128)(2,1)} %param.4) | data formatting | bytes 2097152 | tf_op jit(solution)/shard_map/reshape | solution.py:26
  1.6 1.7 %fusion.9 = f32[16,128,128]{2,1,0:T(8,128)S(1)} fusion(bf16[256,16,128]{0,2,1:T(8,128)(2,1)S(1)} %bitcast.54, bf16[256,2048]{1,0:T(8,128)(2,1)} %param.5), kind=kOutput, calls=%fused_computation.11 | convolution fusion | flops 134217728 | bytes 3145728 | tf_op jit(solution)/shard_map/the,thd->hed/dot_general | solution.py:28
  3.3 0.9 %bitcast_convert_fusion = f16[2048,128]{1,0:T(8,128)(2,1)} fusion(f32[16,128,128]{2,1,0:T(8,128)S(1)} %fusion.9), kind=kLoop, calls=%fused_computation.31 | loop fusion | flops 262144 | bytes 1572864 | tf_op jit(solution)/shard_map/convert_element_type | solution.py:31
  4.1 0.1 collective-permute-start
  4.2 2.2 %collective-permute-done = f16[2048,128]{1,0:T(8,128)(2,1)} collective-permute-done((f16[2048,128]{1,0:T(8,128)(2,1)}, f16[2048,128]{1,0:T(8,128)(2,1)}, u32[]{:S(2)}, u32[]{:S(2)}) %collective-permute-start) | collective-permute-done | bytes 524320 | tf_op jit(solution)/shard_map/ppermute | solution.py:17
  6.4 1.7 %fusion.17 = f16[1024,128]{1,0:T(8,128)(2,1)} fusion(f32[2048,128]{1,0:T(8,128)S(1)} %bitcast.52, s32[]{:T(128)S(6)} %select_n.32, f16[2048,128]{1,0:T(8,128)(2,1)} %collective-permute-done), kind=kLoop, calls=%fused_computation.20 | loop fusion | flops 393216 | bytes 1048580 | tf_op jit(solution)/shard_map/convert_element_type | solution.py:35
  8.1 6.7 %all-to-all-start = ((f16[8,128,128]{2,1,0:T(8,128)(2,1)}), f16[8,128,128]{2,1,0:T(8,128)(2,1)S(1)}, u32[]{:S(2)}, u32[]{:S(2)}) async-start(f16[8,128,128]{2,1,0:T(8,128)(2,1)} %bitcast.58), calls=%async_computation | async-start | bytes 524288 | tf_op jit(solution)/shard_map/all_to_all | solution.py:35
  14.8 7.7 %all-to-all-done = f16[8,128,128]{2,1,0:T(8,128)(2,1)S(1)} async-done(((f16[8,128,128]{2,1,0:T(8,128)(2,1)}), f16[8,128,128]{2,1,0:T(8,128)(2,1)S(1)}, u32[]{:S(2)}, u32[]{:S(2)}) %all-to-all-start) | async-done | bytes 262176 | tf_op jit(solution)/shard_map/all_to_all | solution.py:35
  22.5 0.8 %fusion.5 = f16[8,128,128]{2,1,0:T(8,128)(2,1)} fusion(f16[8,128,128]{2,1,0:T(8,128)(2,1)S(1)} %all-to-all-done), kind=kOutput, calls=%fused_computation.8 | output fusion | flops 1441792 | bytes 524288 | tf_op jit(solution)/shard_map/jit(cumsum)/reduce_window_sum | solution.py:37
  23.3 4.5 %all-to-all-start.1 = ((f16[8,128,128]{2,1,0:T(8,128)(2,1)}), f16[8,128,128]{2,1,0:T(8,128)(2,1)S(1)}, u32[]{:S(2)}, u32[]{:S(2)}) async-start(f16[8,128,128]{2,1,0:T(8,128)(2,1)} %fusion.5), calls=%async_computation.1 | async-start | bytes 524288 | tf_op jit(solution)/shard_map/all_to_all | solution.py:41
  27.8 0.0 copy-done
  27.8 3.8 %fusion.3 = f32[256,16,128]{2,0,1:T(8,128)} fusion(bf16[256,16,128]{0,2,1:T(8,128)(2,1)S(1)} %bitcast.55, pred[256,256]{1,0:T(8,128)(4,1)S(1)} %iota_compare_fusion, bf16[256,2048]{1,0:T(8,128)(2,1)S(1)} %copy-done, bf16[256,2048]{1,0:T(8,128)(2,1)} %param.5), kind=kOutput, calls=%fused_computation.5 | convolution fusion | flops 538968064 | bytes 5308416 | tf_op jit(solution)/shard_map/hts,she->the/dot_general | solution.py:51
  31.6 3.3 %all-to-all-done.1 = f16[8,128,128]{2,1,0:T(8,128)(2,1)S(1)} async-done(((f16[8,128,128]{2,1,0:T(8,128)(2,1)}), f16[8,128,128]{2,1,0:T(8,128)(2,1)S(1)}, u32[]{:S(2)}, u32[]{:S(2)}) %all-to-all-start.1) | async-done | bytes 262176 | tf_op jit(solution)/shard_map/all_to_all | solution.py:41
  35.0 0.0 copy-start.1
  35.0 0.1 fusion.20
  35.1 2.8 %collective-permute-start.1 = (bf16[1024,128]{1,0:T(8,128)(2,1)S(1)}, bf16[1024,128]{1,0:T(8,128)(2,1)S(1)}, u32[]{:S(2)}, u32[]{:S(2)}) collective-permute-start(bf16[1024,128]{1,0:T(8,128)(2,1)S(1)} %fusion.20), channel_id=1, source_target_pairs={{0,1},{1,0},{2,3},{3,2},{4,5},{5,4},{6,7},{7,6},{8,9},{9,8},{10,11... | collective-permute-start | bytes 786440 | tf_op jit(solution)/shard_map/ppermute | solution.py:17
  37.8 1.2 %collective-permute-done.1 = bf16[1024,128]{1,0:T(8,128)(2,1)S(1)} collective-permute-done((bf16[1024,128]{1,0:T(8,128)(2,1)S(1)}, bf16[1024,128]{1,0:T(8,128)(2,1)S(1)}, u32[]{:S(2)}, u32[]{:S(2)}) %collective-permute-start.1) | collective-permute-done | bytes 262176 | tf_op jit(solution)/shard_map/ppermute | solution.py:17
  39.0 1.1 %broadcast_select_fusion.1 = (bf16[1024,128]{1,0:T(8,128)(2,1)S(1)}, bf16[1024,128]{1,0:T(8,128)(2,1)S(1)}) fusion(bf16[1024,128]{1,0:T(8,128)(2,1)S(1)} %collective-permute-done.1, pred[]{:T(512)S(6)} %eq.3, f16[2048,128]{1,0:T(8,128)(2,1)} %collective-permute-done, s32[]{:T(128)S(6)} %select_n.32, f32[8,128,128]{2,1,0:T(8,128)S(1)} %convert_multiply_fusion), kind=kLoop, calls=%fused_computation.30 | loop fusion | flops 786432 | bytes 1572869 | tf_op jit(solution)/shard_map/jit(_where)/select_n | solution.py:54
  40.1 0.0 copy-done.1
  40.1 0.5 %fusion.1 = bf16[256,16,128]{2,0,1:T(8,128)(2,1)S(1)} fusion(f32[256,16,128]{2,0,1:T(8,128)S(1)} %copy-done.1, bf16[16,128,128]{2,1,0:T(8,128)(2,1)S(1)} %bitcast.57, bf16[256,2048]{1,0:T(8,128)(2,1)S(1)} %copy-done), kind=kOutput, calls=%fused_computation.3 | convolution fusion | flops 135790592 | bytes 4718592 | tf_op jit(solution)/shard_map/thd,hed->the/dot_general | solution.py:57
  40.6 0.5 %copy.14 = bf16[256,16,128]{0,2,1:T(8,128)(2,1)S(1)} copy(bf16[256,16,128]{2,0,1:T(8,128)(2,1)S(1)} %fusion.1) | data formatting | bytes 2097152 | tf_op jit(solution)/shard_map/convert_element_type | solution.py:59
  41.2 1.4 %copy.15 = bf16[256,2048]{1,0:T(8,128)(2,1)} copy(bf16[256,2048]{0,1:T(8,128)(2,1)S(1)} %bitcast.56) | data formatting | bytes 2097152 | tf_op jit(solution)/shard_map/reshape | solution.py:60
  (3 shorter events, 0.1 us)
Async XLA Ops:
  0.0 27.8 %copy-start = (bf16[256,2048]{1,0:T(8,128)(2,1)S(1)}, bf16[256,2048]{1,0:T(8,128)(2,1)}, u32[]{:S(2)}) copy-start(bf16[256,2048]{1,0:T(8,128)(2,1)} %param.3) | copy-start | bytes 3145732
  4.1 2.3 %collective-permute-start = (f16[2048,128]{1,0:T(8,128)(2,1)}, f16[2048,128]{1,0:T(8,128)(2,1)}, u32[]{:S(2)}, u32[]{:S(2)}) collective-permute-start(f16[2048,128]{1,0:T(8,128)(2,1)} %bitcast_convert_fusion), channel_id=1, source_target_pairs={{0,1},{1,0},{2,3},{3,2},{4,5},{5,4},{6,7},{7,6},{8,9},{9,8},{10,11... | collective-permute-start | bytes 1572872 | tf_op jit(solution)/shard_map/ppermute | solution.py:17
  8.1 14.4 %all-to-all-start = ((f16[8,128,128]{2,1,0:T(8,128)(2,1)}), f16[8,128,128]{2,1,0:T(8,128)(2,1)S(1)}, u32[]{:S(2)}, u32[]{:S(2)}) async-start(f16[8,128,128]{2,1,0:T(8,128)(2,1)} %bitcast.58), calls=%async_computation | async-start | bytes 524288 | tf_op jit(solution)/shard_map/all_to_all | solution.py:35
  23.3 11.6 %all-to-all-start.1 = ((f16[8,128,128]{2,1,0:T(8,128)(2,1)}), f16[8,128,128]{2,1,0:T(8,128)(2,1)S(1)}, u32[]{:S(2)}, u32[]{:S(2)}) async-start(f16[8,128,128]{2,1,0:T(8,128)(2,1)} %fusion.5), calls=%async_computation.1 | async-start | bytes 524288 | tf_op jit(solution)/shard_map/all_to_all | solution.py:41
  35.0 5.1 %copy-start.1 = (f32[256,16,128]{2,0,1:T(8,128)S(1)}, f32[256,16,128]{2,0,1:T(8,128)}, u32[]{:S(2)}) copy-start(f32[256,16,128]{2,0,1:T(8,128)} %fusion.3) | copy-start | bytes 6291460
  35.1 3.9 %collective-permute-start.1 = (bf16[1024,128]{1,0:T(8,128)(2,1)S(1)}, bf16[1024,128]{1,0:T(8,128)(2,1)S(1)}, u32[]{:S(2)}, u32[]{:S(2)}) collective-permute-start(bf16[1024,128]{1,0:T(8,128)(2,1)S(1)} %fusion.20), channel_id=1, source_target_pairs={{0,1},{1,0},{2,3},{3,2},{4,5},{5,4},{6,7},{7,6},{8,9},{9,8},{10,11... | collective-permute-start | bytes 786440 | tf_op jit(solution)/shard_map/ppermute | solution.py:17

commit v11 on v10

--- a/solution.py
+++ b/solution.py
@@ -26,10 +26,10 @@
     k_blk = keys.reshape(tok, HEADS, DK)
     v_blk = values.reshape(tok, HEADS, DK)
     local_state = jnp.einsum("the,thd->hed", v_blk, k_blk, preferred_element_type=jnp.float32)
-    flat = local_state.reshape(HEADS * DK, DK)
+    flat = local_state.reshape(HEADS * DK, DK).astype(jnp.float16)
     half = HEADS * DK // 2
-    partner_all = swap_cores(flat.astype(jnp.float16))
-    own = lax.dynamic_slice_in_dim(flat, core * half, half)
+    partner_all = swap_cores(flat)
+    own = lax.dynamic_slice_in_dim(flat, core * half, half).astype(jnp.float32)
     partner = lax.dynamic_slice_in_dim(partner_all, core * half, half).astype(jnp.float32)
     chip_sum = own + partner
     received = lax.all_to_all(chip_sum.astype(jnp.float16), "chip", split_axis=0, concat_axis=0, tiled=True)

time: 43.4 us -> 40.3 us (0.929)
  other arithmetic: 4.67 us -> 1.93 us
    select_n x1, other arithmetic: 1.09 us -> 0.14 us  [on_device(): low = jnp.where(first, kept, got)]
    convert_element_type x1, other arithmetic: 1.72 us -> 0.79 us  [on_device(): chip_sum.astype(jnp.float16)]
    convert_element_type x1 -> x0, other arithmetic: 0.86 us -> none  [on_device(): partner_all = swap_cores(flat.astype(jnp.float16))]
  transfers between devices with their start and end apart: 4 -> 4, of which waited for: 4 -> 4; matrix products, arithmetic and copies ran while one was open for 9% -> 10% of each run, Pallas kernels for 0% -> 0%
where the time goes in v11:
time: 40.3 us; the launch traced here: 39.6 us
  starting transfers between devices  14 us (35%)
  waiting for transfers between devices  14 us (35%)
  matrix products  6.04 us (15%)
  local copies, waits for them, and re-layouts  3.53 us (9%)
  other arithmetic  1.93 us (5%)
    all_to_all x1, waiting for transfers between devices, on_device(): lax.all_to_all(chip_sum.astype(jnp.float16), 'chip', split_axis=0, concat...  7.7 us
    all_to_all x1, starting transfers between devices, on_device(): lax.all_to_all(chip_sum.astype(jnp.float16), 'chip', split_axis=0, concat...  6.66 us
    all_to_all x1, starting transfers between devices, on_device(): lax.all_to_all((earlier * down).astype(jnp.float16), 'chip', split_axis=0...  4.45 us
    dot_general x1, matrix products, on_device(): jnp.einsum('hts,she->the', scores, v_blk, preferred_element_type=jnp.floa...  3.83 us
    all_to_all x1, waiting for transfers between devices, on_device(): lax.all_to_all((earlier * down).astype(jnp.float16), 'chip', split_axis=0...  3.31 us
    ppermute x2, waiting for transfers between devices, swap_cores(): return lax.ppermute(x, 'core', [(0, 1), (1, 0)])  3.01 us
    ppermute x2, starting transfers between devices, swap_cores(): return lax.ppermute(x, 'core', [(0, 1), (1, 0)])  2.88 us
    dot_general x1, matrix products, on_device(): jnp.einsum('the,thd->hed', v_blk, k_blk, preferred_element_type=jnp.float32)  1.71 us
  transfers between devices with their start and end apart: 4, of which 4 were waited for; matrix products, arithmetic and copies ran while one was open for 10% of the time, Pallas kernels for 0%

profile of v11, /device:TPU:1, one launch (start us, length us, event | category | flops | bytes accessed | tf_op | source)
XLA Modules:
  0.0 39.6 jit_solution(12770264564079964932)
XLA Ops:
  0.0 0.0 copy-start
  0.0 1.6 %copy.18 = bf16[256,2048]{0,1:T(8,128)(2,1)S(1)} copy(bf16[256,2048]{1,0:T(8,128)(2,1)} %param.4) | data formatting | bytes 2097152 | tf_op jit(solution)/shard_map/reshape | solution.py:26
  1.6 1.7 %convolution_convert_fusion = f16[16,128,128]{2,1,0:T(8,128)(2,1)S(1)} fusion(bf16[256,16,128]{0,2,1:T(8,128)(2,1)S(1)} %bitcast.49, bf16[256,2048]{1,0:T(8,128)(2,1)} %param.5), kind=kOutput, calls=%fused_computation.6 | convolution fusion | flops 134479872 | bytes 2621440 | tf_op jit(solution)/shard_map/the,thd->hed/dot_general | solution.py:28
  3.3 0.1 collective-permute-start
  3.4 1.9 %collective-permute-done = f16[2048,128]{1,0:T(8,128)(2,1)S(1)} collective-permute-done((f16[2048,128]{1,0:T(8,128)(2,1)S(1)}, f16[2048,128]{1,0:T(8,128)(2,1)S(1)}, u32[]{:S(2)}, u32[]{:S(2)}) %collective-permute-start) | collective-permute-done | bytes 524320 | tf_op jit(solution)/shard_map/ppermute | solution.py:17
  5.3 0.8 %fusion.18 = f16[1024,128]{1,0:T(8,128)(2,1)} fusion(f16[2048,128]{1,0:T(8,128)(2,1)S(1)} %collective-permute-done, s32[]{:T(128)S(6)} %select_n.32, f16[2048,128]{1,0:T(8,128)(2,1)S(1)} %bitcast.53), kind=kLoop, calls=%fused_computation.23 | loop fusion | flops 524288 | bytes 786436 | tf_op jit(solution)/shard_map/convert_element_type | solution.py:35
  6.1 6.7 %all-to-all-start = ((f16[8,128,128]{2,1,0:T(8,128)(2,1)}), f16[8,128,128]{2,1,0:T(8,128)(2,1)S(1)}, u32[]{:S(2)}, u32[]{:S(2)}) async-start(f16[8,128,128]{2,1,0:T(8,128)(2,1)} %bitcast.1), calls=%async_computation | async-start | bytes 524288 | tf_op jit(solution)/shard_map/all_to_all | solution.py:35
  12.7 7.7 %all-to-all-done = f16[8,128,128]{2,1,0:T(8,128)(2,1)S(1)} async-done(((f16[8,128,128]{2,1,0:T(8,128)(2,1)}), f16[8,128,128]{2,1,0:T(8,128)(2,1)S(1)}, u32[]{:S(2)}, u32[]{:S(2)}) %all-to-all-start) | async-done | bytes 262176 | tf_op jit(solution)/shard_map/all_to_all | solution.py:35
  20.4 0.8 %fusion.5 = f16[8,128,128]{2,1,0:T(8,128)(2,1)} fusion(f16[8,128,128]{2,1,0:T(8,128)(2,1)S(1)} %all-to-all-done), kind=kOutput, calls=%fused_computation.9 | output fusion | flops 1441792 | bytes 524288 | tf_op jit(solution)/shard_map/jit(cumsum)/reduce_window_sum | solution.py:37
  21.2 4.5 %all-to-all-start.1 = ((f16[8,128,128]{2,1,0:T(8,128)(2,1)}), f16[8,128,128]{2,1,0:T(8,128)(2,1)S(1)}, u32[]{:S(2)}, u32[]{:S(2)}) async-start(f16[8,128,128]{2,1,0:T(8,128)(2,1)} %fusion.5), calls=%async_computation.1 | async-start | bytes 524288 | tf_op jit(solution)/shard_map/all_to_all | solution.py:41
  25.7 0.0 copy-done
  25.7 3.8 %fusion.3 = f32[256,16,128]{2,0,1:T(8,128)} fusion(bf16[256,16,128]{0,2,1:T(8,128)(2,1)S(1)} %bitcast.50, pred[256,256]{1,0:T(8,128)(4,1)S(1)} %iota_compare_fusion, bf16[256,2048]{1,0:T(8,128)(2,1)S(1)} %copy-done, bf16[256,2048]{1,0:T(8,128)(2,1)} %param.5), kind=kOutput, calls=%fused_computation.5 | convolution fusion | flops 538968064 | bytes 5308416 | tf_op jit(solution)/shard_map/hts,she->the/dot_general | solution.py:51
  29.5 3.3 %all-to-all-done.1 = f16[8,128,128]{2,1,0:T(8,128)(2,1)S(1)} async-done(((f16[8,128,128]{2,1,0:T(8,128)(2,1)}), f16[8,128,128]{2,1,0:T(8,128)(2,1)S(1)}, u32[]{:S(2)}, u32[]{:S(2)}) %all-to-all-start.1) | async-done | bytes 262176 | tf_op jit(solution)/shard_map/all_to_all | solution.py:41
  32.9 0.0 copy-start.1
  32.9 0.1 fusion.17
  33.0 2.8 %collective-permute-start.1 = (bf16[1024,128]{1,0:T(8,128)(2,1)S(1)}, bf16[1024,128]{1,0:T(8,128)(2,1)S(1)}, u32[]{:S(2)}, u32[]{:S(2)}) collective-permute-start(bf16[1024,128]{1,0:T(8,128)(2,1)S(1)} %fusion.17), channel_id=1, source_target_pairs={{0,1},{1,0},{2,3},{3,2},{4,5},{5,4},{6,7},{7,6},{8,9},{9,8},{10,11... | collective-permute-start | bytes 786440 | tf_op jit(solution)/shard_map/ppermute | solution.py:17
  35.8 1.2 %collective-permute-done.1 = bf16[1024,128]{1,0:T(8,128)(2,1)S(1)} collective-permute-done((bf16[1024,128]{1,0:T(8,128)(2,1)S(1)}, bf16[1024,128]{1,0:T(8,128)(2,1)S(1)}, u32[]{:S(2)}, u32[]{:S(2)}) %collective-permute-start.1) | collective-permute-done | bytes 262176 | tf_op jit(solution)/shard_map/ppermute | solution.py:17
  36.9 0.1 broadcast_select_fusion.1
  37.1 0.0 copy-done.1
  37.1 0.5 %fusion.1 = bf16[256,16,128]{2,0,1:T(8,128)(2,1)S(1)} fusion(f32[256,16,128]{2,0,1:T(8,128)S(1)} %copy-done.1, bf16[16,128,128]{2,1,0:T(8,128)(2,1)S(1)} %bitcast.55, bf16[256,2048]{1,0:T(8,128)(2,1)S(1)} %copy-done), kind=kOutput, calls=%fused_computation.3 | convolution fusion | flops 135790592 | bytes 4718592 | tf_op jit(solution)/shard_map/thd,hed->the/dot_general | solution.py:57
  37.6 0.5 %copy.14 = bf16[256,16,128]{0,2,1:T(8,128)(2,1)S(1)} copy(bf16[256,16,128]{2,0,1:T(8,128)(2,1)S(1)} %fusion.1) | data formatting | bytes 2097152 | tf_op jit(solution)/shard_map/convert_element_type | solution.py:59
  38.2 1.4 %copy.15 = bf16[256,2048]{1,0:T(8,128)(2,1)} copy(bf16[256,2048]{0,1:T(8,128)(2,1)S(1)} %bitcast.51) | data formatting | bytes 2097152 | tf_op jit(solution)/shard_map/reshape | solution.py:60
  (3 shorter events, 0.1 us)
Async XLA Ops:
  0.0 25.7 %copy-start = (bf16[256,2048]{1,0:T(8,128)(2,1)S(1)}, bf16[256,2048]{1,0:T(8,128)(2,1)}, u32[]{:S(2)}) copy-start(bf16[256,2048]{1,0:T(8,128)(2,1)} %param.3) | copy-start | bytes 3145732
  3.3 2.0 %collective-permute-start = (f16[2048,128]{1,0:T(8,128)(2,1)S(1)}, f16[2048,128]{1,0:T(8,128)(2,1)S(1)}, u32[]{:S(2)}, u32[]{:S(2)}) collective-permute-start(f16[2048,128]{1,0:T(8,128)(2,1)S(1)} %bitcast.52), channel_id=1, source_target_pairs={{0,1},{1,0},{2,3},{3,2},{4,5},{5,4},{6,7},{7,6},{8,9},{9,8},{10,11... | collective-permute-start | bytes 1572872 | tf_op jit(solution)/shard_map/ppermute | solution.py:17
  6.1 14.4 %all-to-all-start = ((f16[8,128,128]{2,1,0:T(8,128)(2,1)}), f16[8,128,128]{2,1,0:T(8,128)(2,1)S(1)}, u32[]{:S(2)}, u32[]{:S(2)}) async-start(f16[8,128,128]{2,1,0:T(8,128)(2,1)} %bitcast.1), calls=%async_computation | async-start | bytes 524288 | tf_op jit(solution)/shard_map/all_to_all | solution.py:35
  21.2 11.6 %all-to-all-start.1 = ((f16[8,128,128]{2,1,0:T(8,128)(2,1)}), f16[8,128,128]{2,1,0:T(8,128)(2,1)S(1)}, u32[]{:S(2)}, u32[]{:S(2)}) async-start(f16[8,128,128]{2,1,0:T(8,128)(2,1)} %fusion.5), calls=%async_computation.1 | async-start | bytes 524288 | tf_op jit(solution)/shard_map/all_to_all | solution.py:41
  32.9 4.3 %copy-start.1 = (f32[256,16,128]{2,0,1:T(8,128)S(1)}, f32[256,16,128]{2,0,1:T(8,128)}, u32[]{:S(2)}) copy-start(f32[256,16,128]{2,0,1:T(8,128)} %fusion.3) | copy-start | bytes 6291460
  33.0 3.9 %collective-permute-start.1 = (bf16[1024,128]{1,0:T(8,128)(2,1)S(1)}, bf16[1024,128]{1,0:T(8,128)(2,1)S(1)}, u32[]{:S(2)}, u32[]{:S(2)}) collective-permute-start(bf16[1024,128]{1,0:T(8,128)(2,1)S(1)} %fusion.17), channel_id=1, source_target_pairs={{0,1},{1,0},{2,3},{3,2},{4,5},{5,4},{6,7},{7,6},{8,9},{9,8},{10,11... | collective-permute-start | bytes 786440 | tf_op jit(solution)/shard_map/ppermute | solution.py:17

commit v12 on v11

--- a/solution.py
+++ b/solution.py
@@ -28,9 +28,11 @@
     local_state = jnp.einsum("the,thd->hed", v_blk, k_blk, preferred_element_type=jnp.float32)
     flat = local_state.reshape(HEADS * DK, DK).astype(jnp.float16)
     half = HEADS * DK // 2
-    partner_all = swap_cores(flat)
-    own = lax.dynamic_slice_in_dim(flat, core * half, half).astype(jnp.float32)
-    partner = lax.dynamic_slice_in_dim(partner_all, core * half, half).astype(jnp.float32)
+    to_second = lax.ppermute(flat[half:], "core", [(0, 1)])
+    to_first = lax.ppermute(flat[:half], "core", [(1, 0)])
+    first = core == 0
+    own = jnp.where(first, flat[:half], flat[half:]).astype(jnp.float32)
+    partner = (to_first + to_second).astype(jnp.float32)
     chip_sum = own + partner
     received = lax.all_to_all(chip_sum.astype(jnp.float16), "chip", split_axis=0, concat_axis=0, tiled=True)
     received = received.reshape(chips, half // chips, DK).astype(jnp.float32)
@@ -40,7 +42,6 @@
     down = np.float32(2.0 ** -shift)
     back = lax.all_to_all((earlier * down).astype(jnp.float16), "chip", split_axis=0, concat_axis=0, tiled=True)
     chip_prefix = back.reshape(half, DK).astype(jnp.float32) * np.float32(2.0 ** shift)
-    first = core == 0
     kept = (chip_prefix + jnp.where(first, jnp.float32(0.0), partner)).astype(jnp.bfloat16)
     sent = (chip_prefix + jnp.where(first, own, jnp.float32(0.0))).astype(jnp.bfloat16)
     rows = lax.broadcasted_iota(jnp.int32, (tok, tok), 0)

time: 40.3 us -> 42.7 us (1.060)
  blocking collectives: 0 us -> 14.8 us
  waiting for transfers between devices: 14 us -> 6.88 us
  starting transfers between devices: 14 us -> 10.3 us
  matrix products: 6.04 us -> 4.81 us
  other arithmetic: 1.93 us -> 1.44 us
    all_to_all x0 -> x1, blocking collectives: none -> 14.8 us  [on_device(): lax.all_to_all(chip_sum.astype(jnp.float16), 'chip', split_axis=0, concat...]
    all_to_all x1 -> x0, waiting for transfers between devices: 7.7 us -> none  [on_device(): lax.all_to_all(chip_sum.astype(jnp.float16), 'chip', split_axis=0, concat...]
    all_to_all x1 -> x0, starting transfers between devices: 6.66 us -> none  [on_device(): lax.all_to_all(chip_sum.astype(jnp.float16), 'chip', split_axis=0, concat...]
    ppermute x0 -> x2, starting transfers between devices: none -> 3.27 us  [the longest x1 1.98 us: on_device(): to_first = lax.ppermute(flat[:half], 'core', [(1, 0)])]
    ppermute x0 -> x2, waiting for transfers between devices: none -> 2.12 us  [the longest x1 2.11 us: on_device(): to_second = lax.ppermute(flat[half:], 'core', [(0, 1)])]
    ppermute x2 -> x1, waiting for transfers between devices: 3.01 us -> 1.16 us  [swap_cores(): return lax.ppermute(x, 'core', [(0, 1), (1, 0)])]
    dot_general x1, matrix products: 1.71 us -> 0.49 us  [on_device(): jnp.einsum('the,thd->hed', v_blk, k_blk, preferred_element_type=jnp.float32)]
    convert_element_type x1, other arithmetic: 0.79 us -> 0.19 us  [on_device(): chip_sum.astype(jnp.float16)]
  transfers between devices with their start and end apart: 4 -> 4, of which waited for: 4 -> 3; matrix products, arithmetic and copies ran while one was open for 10% -> 9% of each run, Pallas kernels for 0% -> 0%
where the time goes in v12:
time: 42.7 us; the launch traced here: 42.1 us
  blocking collectives  14.8 us (35%)
  starting transfers between devices  10.3 us (24%)
  waiting for transfers between devices  6.88 us (16%)
  matrix products  4.81 us (11%)
  local copies, waits for them, and re-layouts  3.72 us (9%)
  other arithmetic  1.44 us (3%)
    all_to_all x1, blocking collectives, on_device(): lax.all_to_all(chip_sum.astype(jnp.float16), 'chip', split_axis=0, concat...  14.8 us
    all_to_all x1, starting transfers between devices, on_device(): lax.all_to_all((earlier * down).astype(jnp.float16), 'chip', split_axis=0...  4.6 us
    dot_general x1, matrix products, on_device(): jnp.einsum('hts,she->the', scores, v_blk, preferred_element_type=jnp.floa...  3.82 us
    all_to_all x1, waiting for transfers between devices, on_device(): lax.all_to_all((earlier * down).astype(jnp.float16), 'chip', split_axis=0...  3.6 us
    ppermute x1, starting transfers between devices, swap_cores(): return lax.ppermute(x, 'core', [(0, 1), (1, 0)])  2.48 us
    ppermute x1, waiting for transfers between devices, on_device(): to_second = lax.ppermute(flat[half:], 'core', [(0, 1)])  2.11 us
    ppermute x1, starting transfers between devices, on_device(): to_first = lax.ppermute(flat[:half], 'core', [(1, 0)])  1.98 us
    reshape x1, local copies, waits for them, and re-layouts, on_device(): k_blk = keys.reshape(tok, HEADS, DK)  1.62 us
  transfers between devices with their start and end apart: 4, of which 3 were waited for; matrix products, arithmetic and copies ran while one was open for 9% of the time, Pallas kernels for 0%

profile of v12, /device:TPU:1, one launch (start us, length us, event | category | flops | bytes accessed | tf_op | source)
XLA Modules:
  0.0 42.1 jit_solution(7605880304398276751)
XLA Ops:
  0.0 0.0 copy-start
  0.0 0.0 copy-start.2
  0.0 1.6 %copy.18 = bf16[256,2048]{0,1:T(8,128)(2,1)S(1)} copy(bf16[256,2048]{1,0:T(8,128)(2,1)} %param.4) | data formatting | bytes 2097152 | tf_op jit(solution)/shard_map/reshape | solution.py:26
  1.6 0.0 copy-done.2
  1.6 0.5 %convolution_convert_fusion = f16[16,128,128]{2,1,0:T(8,128)(2,1)S(1)} fusion(bf16[256,16,128]{0,2,1:T(8,128)(2,1)S(1)} %bitcast.51, bf16[256,2048]{1,0:T(8,128)(2,1)S(1)} %copy-done.2), kind=kOutput, calls=%fused_computation.6 | convolution fusion | flops 134479872 | bytes 2621440 | tf_op jit(solution)/shard_map/the,thd->hed/dot_general | solution.py:28
  2.1 0.1 fusion.24
  2.3 2.0 %collective-permute-start = (f16[1024,128]{1,0:T(8,128)(2,1)S(1)}, f16[1024,128]{1,0:T(8,128)(2,1)S(1)}, u32[]{:S(2)}, u32[]{:S(2)}) collective-permute-start(f16[1024,128]{1,0:T(8,128)(2,1)S(1)} %bitcast.55), channel_id=1, source_target_pairs={{1,0},{3,2},{5,4},{7,6},{9,8},{11,10},{13,12},{15,14},{17,16},{19,... | collective-permute-start | bytes 786440 | tf_op jit(solution)/shard_map/ppermute | solution.py:32
  4.3 1.3 %collective-permute-start.1 = (f16[1024,128]{1,0:T(8,128)(2,1)S(1)}, f16[1024,128]{1,0:T(8,128)(2,1)S(1)}, u32[]{:S(2)}, u32[]{:S(2)}) collective-permute-start(f16[1024,128]{1,0:T(8,128)(2,1)S(1)} %bitcast.54), channel_id=1, source_target_pairs={{0,1},{2,3},{4,5},{6,7},{8,9},{10,11},{12,13},{14,15},{16,17},{18,... | collective-permute-start | bytes 786440 | tf_op jit(solution)/shard_map/ppermute | solution.py:31
  5.6 0.0 collective-permute-done
  5.6 2.1 %collective-permute-done.1 = f16[1024,128]{1,0:T(8,128)(2,1)S(1)} collective-permute-done((f16[1024,128]{1,0:T(8,128)(2,1)S(1)}, f16[1024,128]{1,0:T(8,128)(2,1)S(1)}, u32[]{:S(2)}, u32[]{:S(2)}) %collective-permute-start.1) | collective-permute-done | bytes 262176 | tf_op jit(solution)/shard_map/ppermute | solution.py:31
  7.7 0.2 fusion.18
  7.9 14.8 %all_to_all.14 = f16[8,128,128]{2,1,0:T(8,128)(2,1)S(1)} all-to-all(f16[8,128,128]{2,1,0:T(8,128)(2,1)S(1)} %bitcast.57), channel_id=1, replica_groups=mesh['groups'=2,'chip'=8,'core'=2] {'chip'}, dimensions={0} | all-to-all | bytes 524288 | tf_op jit(solution)/shard_map/all_to_all | solution.py:37
  22.7 0.8 %fusion.5 = f16[8,128,128]{2,1,0:T(8,128)(2,1)} fusion(f16[8,128,128]{2,1,0:T(8,128)(2,1)S(1)} %all_to_all.14), kind=kOutput, calls=%fused_computation.9 | output fusion | flops 1441792 | bytes 524288 | tf_op jit(solution)/shard_map/jit(cumsum)/reduce_window_sum | solution.py:39
  23.5 4.6 %all-to-all-start.1 = ((f16[8,128,128]{2,1,0:T(8,128)(2,1)}), f16[8,128,128]{2,1,0:T(8,128)(2,1)S(1)}, u32[]{:S(2)}, u32[]{:S(2)}) async-start(f16[8,128,128]{2,1,0:T(8,128)(2,1)} %fusion.5), calls=%async_computation.1 | async-start | bytes 524288 | tf_op jit(solution)/shard_map/all_to_all | solution.py:43
  28.1 0.0 copy-done
  28.1 3.8 %fusion.3 = f32[256,16,128]{2,0,1:T(8,128)} fusion(bf16[256,16,128]{0,2,1:T(8,128)(2,1)S(1)} %bitcast.52, pred[256,256]{1,0:T(8,128)(4,1)S(1)} %iota_compare_fusion, bf16[256,2048]{1,0:T(8,128)(2,1)S(1)} %copy-done, bf16[256,2048]{1,0:T(8,128)(2,1)} %param.5), kind=kOutput, calls=%fused_computation.5 | convolution fusion | flops 538968064 | bytes 5308416 | tf_op jit(solution)/shard_map/hts,she->the/dot_general | solution.py:52
  31.9 3.6 %all-to-all-done.1 = f16[8,128,128]{2,1,0:T(8,128)(2,1)S(1)} async-done(((f16[8,128,128]{2,1,0:T(8,128)(2,1)}), f16[8,128,128]{2,1,0:T(8,128)(2,1)S(1)}, u32[]{:S(2)}, u32[]{:S(2)}) %all-to-all-start.1) | async-done | bytes 262176 | tf_op jit(solution)/shard_map/all_to_all | solution.py:43
  35.6 0.1 fusion.17
  35.7 0.0 copy-start.1
  35.7 2.5 %collective-permute-start.2 = (bf16[1024,128]{1,0:T(8,128)(2,1)S(1)}, bf16[1024,128]{1,0:T(8,128)(2,1)S(1)}, u32[]{:S(2)}, u32[]{:S(2)}) collective-permute-start(bf16[1024,128]{1,0:T(8,128)(2,1)S(1)} %fusion.17), channel_id=1, source_target_pairs={{0,1},{1,0},{2,3},{3,2},{4,5},{5,4},{6,7},{7,6},{8,9},{9,8},{10,11... | collective-permute-start | bytes 786440 | tf_op jit(solution)/shard_map/ppermute | solution.py:17
  38.2 1.2 %collective-permute-done.2 = bf16[1024,128]{1,0:T(8,128)(2,1)S(1)} collective-permute-done((bf16[1024,128]{1,0:T(8,128)(2,1)S(1)}, bf16[1024,128]{1,0:T(8,128)(2,1)S(1)}, u32[]{:S(2)}, u32[]{:S(2)}) %collective-permute-start.2) | collective-permute-done | bytes 262176 | tf_op jit(solution)/shard_map/ppermute | solution.py:17
  39.4 0.2 broadcast_select_fusion.1
  39.6 0.0 copy-done.1
  39.6 0.5 %fusion.1 = bf16[256,16,128]{2,0,1:T(8,128)(2,1)S(1)} fusion(f32[256,16,128]{2,0,1:T(8,128)S(1)} %copy-done.1, bf16[16,128,128]{2,1,0:T(8,128)(2,1)S(1)} %bitcast.56, bf16[256,2048]{1,0:T(8,128)(2,1)S(1)} %copy-done), kind=kOutput, calls=%fused_computation.3 | convolution fusion | flops 135790592 | bytes 4718592 | tf_op jit(solution)/shard_map/thd,hed->the/dot_general | solution.py:58
  40.1 0.5 %copy.14 = bf16[256,16,128]{0,2,1:T(8,128)(2,1)S(1)} copy(bf16[256,16,128]{2,0,1:T(8,128)(2,1)S(1)} %fusion.1) | data formatting | bytes 2097152 | tf_op jit(solution)/shard_map/convert_element_type | solution.py:60
  40.7 1.4 %copy.15 = bf16[256,2048]{1,0:T(8,128)(2,1)} copy(bf16[256,2048]{0,1:T(8,128)(2,1)S(1)} %bitcast.53) | data formatting | bytes 2097152 | tf_op jit(solution)/shard_map/reshape | solution.py:61
  (4 shorter events, 0.1 us)
Async XLA Ops:
  0.0 28.1 %copy-start = (bf16[256,2048]{1,0:T(8,128)(2,1)S(1)}, bf16[256,2048]{1,0:T(8,128)(2,1)}, u32[]{:S(2)}) copy-start(bf16[256,2048]{1,0:T(8,128)(2,1)} %param.3) | copy-start | bytes 3145732
  0.0 1.6 %copy-start.2 = (bf16[256,2048]{1,0:T(8,128)(2,1)S(1)}, bf16[256,2048]{1,0:T(8,128)(2,1)}, u32[]{:S(2)}) copy-start(bf16[256,2048]{1,0:T(8,128)(2,1)} %param.5) | copy-start | bytes 3145732
  2.3 3.3 %collective-permute-start = (f16[1024,128]{1,0:T(8,128)(2,1)S(1)}, f16[1024,128]{1,0:T(8,128)(2,1)S(1)}, u32[]{:S(2)}, u32[]{:S(2)}) collective-permute-start(f16[1024,128]{1,0:T(8,128)(2,1)S(1)} %bitcast.55), channel_id=1, source_target_pairs={{1,0},{3,2},{5,4},{7,6},{9,8},{11,10},{13,12},{15,14},{17,16},{19,... | collective-permute-start | bytes 786440 | tf_op jit(solution)/shard_map/ppermute | solution.py:32
  4.3 3.4 %collective-permute-start.1 = (f16[1024,128]{1,0:T(8,128)(2,1)S(1)}, f16[1024,128]{1,0:T(8,128)(2,1)S(1)}, u32[]{:S(2)}, u32[]{:S(2)}) collective-permute-start(f16[1024,128]{1,0:T(8,128)(2,1)S(1)} %bitcast.54), channel_id=1, source_target_pairs={{0,1},{2,3},{4,5},{6,7},{8,9},{10,11},{12,13},{14,15},{16,17},{18,... | collective-permute-start | bytes 786440 | tf_op jit(solution)/shard_map/ppermute | solution.py:31
  23.5 12.1 %all-to-all-start.1 = ((f16[8,128,128]{2,1,0:T(8,128)(2,1)}), f16[8,128,128]{2,1,0:T(8,128)(2,1)S(1)}, u32[]{:S(2)}, u32[]{:S(2)}) async-start(f16[8,128,128]{2,1,0:T(8,128)(2,1)} %fusion.5), calls=%async_computation.1 | async-start | bytes 524288 | tf_op jit(solution)/shard_map/all_to_all | solution.py:43
  35.7 3.9 %copy-start.1 = (f32[256,16,128]{2,0,1:T(8,128)S(1)}, f32[256,16,128]{2,0,1:T(8,128)}, u32[]{:S(2)}) copy-start(f32[256,16,128]{2,0,1:T(8,128)} %fusion.3) | copy-start | bytes 6291460
  35.7 3.6 %collective-permute-start.2 = (bf16[1024,128]{1,0:T(8,128)(2,1)S(1)}, bf16[1024,128]{1,0:T(8,128)(2,1)S(1)}, u32[]{:S(2)}, u32[]{:S(2)}) collective-permute-start(bf16[1024,128]{1,0:T(8,128)(2,1)S(1)} %fusion.17), channel_id=1, source_target_pairs={{0,1},{1,0},{2,3},{3,2},{4,5},{5,4},{6,7},{7,6},{8,9},{9,8},{10,11... | collective-permute-start | bytes 786440 | tf_op jit(solution)/shard_map/ppermute | solution.py:17

commit v13 on v11

--- a/solution.py
+++ b/solution.py
@@ -4,6 +4,7 @@
 import jax.numpy as jnp
 import numpy as np
 from jax import lax
+from jax.experimental.layout import Layout, with_layout_constraint
 from jax.sharding import Mesh
 from jax.sharding import PartitionSpec as P
 
@@ -48,15 +49,16 @@
     causal = cols <= rows
     scores = jnp.einsum("thd,shd->hts", q_blk, k_blk, preferred_element_type=jnp.float32)
     scores = jnp.where(causal[None], scores, jnp.float32(0.0)).astype(jnp.bfloat16)
-    intra = jnp.einsum("hts,she->the", scores, v_blk, preferred_element_type=jnp.float32)
+    intra = jnp.einsum("hts,she->hte", scores, v_blk, preferred_element_type=jnp.float32)
+    intra = with_layout_constraint(intra, Layout(major_to_minor=(0, 2, 1)))
     sent, intra = lax.optimization_barrier((sent, intra))
     got = swap_cores(sent)
     low = jnp.where(first, kept, got)
     high = jnp.where(first, got, kept)
     carried = jnp.concatenate([low, high], axis=0).reshape(HEADS, DK, DK)
-    inter = jnp.einsum("thd,hed->the", q_blk, carried, preferred_element_type=jnp.float32)
+    inter = jnp.einsum("thd,hed->hte", q_blk, carried, preferred_element_type=jnp.float32)
     scale = 1.0 / jnp.sqrt(jnp.float32(DK * tok * sources))
-    attended = ((intra + inter) * scale).astype(jnp.bfloat16)
+    attended = jnp.transpose(((intra + inter) * scale).astype(jnp.bfloat16), (1, 0, 2))
     return attended.reshape(tok, HEADS * DK)
 
 

time: 40.3 us -> 44.1 us (1.094)
  other arithmetic: 1.93 us -> 5.03 us
  matrix products: 6.04 us -> 4.37 us
  waiting for transfers between devices: 14 us -> 15.5 us
  local copies, waits for them, and re-layouts: 3.53 us -> 4.48 us
    reshape x0 -> x1, local copies, waits for them, and re-layouts: none -> 1.48 us  [on_device(): v_blk = values.reshape(tok, HEADS, DK)]
    dot_general x2, matrix products: 4.33 us -> 3.13 us  [the longest x1 2.68 us: on_device(): jnp.einsum('hts,she->hte', scores, v_blk, preferred_element_type=jnp.floa...]
    all_to_all x1, waiting for transfers between devices: 3.31 us -> 4.46 us  [on_device(): lax.all_to_all((earlier * down).astype(jnp.float16), 'chip', split_axis=0...]
    convert_element_type x1, other arithmetic: 0.08 us -> 1.2 us  [on_device(): (chip_prefix + jnp.where(first, own, jnp.float32(0.0))).astype(jnp.bfloat16)]
    convert_element_type x1, other arithmetic: 0.79 us -> 1.82 us  [on_device(): chip_sum.astype(jnp.float16)]
    select_n x1, other arithmetic: 0.14 us -> 1.09 us  [on_device(): low = jnp.where(first, kept, got)]
    convert_element_type x1 -> x0, local copies, waits for them, and re-layouts: 0.53 us -> none  [on_device(): attended = ((intra + inter) * scale).astype(jnp.bfloat16)]
    dot_general x1, matrix products: 1.71 us -> 1.24 us  [on_device(): jnp.einsum('the,thd->hed', v_blk, k_blk, preferred_element_type=jnp.float32)]
  transfers between devices with their start and end apart: 4 -> 4, of which waited for: 4 -> 4; matrix products, arithmetic and copies ran while one was open for 10% -> 6% of each run, Pallas kernels for 0% -> 0%
where the time goes in v13:
time: 44.1 us; the launch traced here: 43.4 us
  waiting for transfers between devices  15.5 us (35%)
  starting transfers between devices  13.9 us (32%)
  other arithmetic  5.03 us (11%)
  local copies, waits for them, and re-layouts  4.48 us (10%)
  matrix products  4.37 us (10%)
    all_to_all x1, waiting for transfers between devices, on_device(): lax.all_to_all(chip_sum.astype(jnp.float16), 'chip', split_axis=0, concat...  7.7 us
    all_to_all x1, starting transfers between devices, on_device(): lax.all_to_all(chip_sum.astype(jnp.float16), 'chip', split_axis=0, concat...  6.65 us
    all_to_all x1, waiting for transfers between devices, on_device(): lax.all_to_all((earlier * down).astype(jnp.float16), 'chip', split_axis=0...  4.46 us
    all_to_all x1, starting transfers between devices, on_device(): lax.all_to_all((earlier * down).astype(jnp.float16), 'chip', split_axis=0...  4.45 us
    ppermute x2, waiting for transfers between devices, swap_cores(): return lax.ppermute(x, 'core', [(0, 1), (1, 0)])  3.36 us
    ppermute x2, starting transfers between devices, swap_cores(): return lax.ppermute(x, 'core', [(0, 1), (1, 0)])  2.81 us
    dot_general x1, matrix products, on_device(): jnp.einsum('hts,she->hte', scores, v_blk, preferred_element_type=jnp.floa...  2.68 us
    convert_element_type x1, other arithmetic, on_device(): chip_sum.astype(jnp.float16)  1.82 us
  transfers between devices with their start and end apart: 4, of which 4 were waited for; matrix products, arithmetic and copies ran while one was open for 6% of the time, Pallas kernels for 0%

profile of v13, /device:TPU:1, one launch (start us, length us, event | category | flops | bytes accessed | tf_op | source)
XLA Modules:
  0.0 43.4 jit_solution(13949956609992094327)
XLA Ops:
  0.0 0.0 copy-start
  0.0 1.6 %copy.11 = bf16[256,2048]{0,1:T(8,128)(2,1)S(1)} copy(bf16[256,2048]{1,0:T(8,128)(2,1)} %param.4) | data formatting | bytes 2097152 | tf_op jit(solution)/shard_map/reshape | solution.py:27
  1.6 1.5 %copy.10 = bf16[256,2048]{0,1:T(8,128)(2,1)S(1)} copy(bf16[256,2048]{1,0:T(8,128)(2,1)} %param.5) | data formatting | bytes 2097152 | tf_op jit(solution)/shard_map/reshape | solution.py:28
  3.1 1.2 %convolution_convert_fusion = f16[16,128,128]{2,1,0:T(8,128)(2,1)} fusion(bf16[256,16,128]{0,2,1:T(8,128)(2,1)S(1)} %bitcast.42, bf16[256,16,128]{0,2,1:T(8,128)(2,1)S(1)} %bitcast.40), kind=kOutput, calls=%fused_computation.5 | convolution fusion | flops 134479872 | bytes 2621440 | tf_op jit(solution)/shard_map/the,thd->hed/dot_general | solution.py:29
  4.3 0.1 collective-permute-start
  4.4 2.2 %collective-permute-done = f16[2048,128]{1,0:T(8,128)(2,1)} collective-permute-done((f16[2048,128]{1,0:T(8,128)(2,1)}, f16[2048,128]{1,0:T(8,128)(2,1)}, u32[]{:S(2)}, u32[]{:S(2)}) %collective-permute-start) | collective-permute-done | bytes 524320 | tf_op jit(solution)/shard_map/ppermute | solution.py:18
  6.6 1.8 %fusion.13 = f16[1024,128]{1,0:T(8,128)(2,1)} fusion(f16[2048,128]{1,0:T(8,128)(2,1)} %collective-permute-done, s32[]{:T(128)S(6)} %select_n.32, f16[2048,128]{1,0:T(8,128)(2,1)} %bitcast), kind=kLoop, calls=%fused_computation.18 | loop fusion | flops 524288 | bytes 786436 | tf_op jit(solution)/shard_map/convert_element_type | solution.py:36
  8.4 6.7 %all-to-all-start = ((f16[8,128,128]{2,1,0:T(8,128)(2,1)}), f16[8,128,128]{2,1,0:T(8,128)(2,1)S(1)}, u32[]{:S(2)}, u32[]{:S(2)}) async-start(f16[8,128,128]{2,1,0:T(8,128)(2,1)} %bitcast.46), calls=%async_computation | async-start | bytes 524288 | tf_op jit(solution)/shard_map/all_to_all | solution.py:36
  15.0 7.7 %all-to-all-done = f16[8,128,128]{2,1,0:T(8,128)(2,1)S(1)} async-done(((f16[8,128,128]{2,1,0:T(8,128)(2,1)}), f16[8,128,128]{2,1,0:T(8,128)(2,1)S(1)}, u32[]{:S(2)}, u32[]{:S(2)}) %all-to-all-start) | async-done | bytes 262176 | tf_op jit(solution)/shard_map/all_to_all | solution.py:36
  22.7 0.8 %fusion.4 = f16[8,128,128]{2,1,0:T(8,128)(2,1)} fusion(f16[8,128,128]{2,1,0:T(8,128)(2,1)S(1)} %all-to-all-done), kind=kOutput, calls=%fused_computation.8 | output fusion | flops 1441792 | bytes 524288 | tf_op jit(solution)/shard_map/jit(cumsum)/reduce_window_sum | solution.py:38
  23.5 4.5 %all-to-all-start.1 = ((f16[8,128,128]{2,1,0:T(8,128)(2,1)}), f16[8,128,128]{2,1,0:T(8,128)(2,1)S(1)}, u32[]{:S(2)}, u32[]{:S(2)}) async-start(f16[8,128,128]{2,1,0:T(8,128)(2,1)} %fusion.4), calls=%async_computation.1 | async-start | bytes 524288 | tf_op jit(solution)/shard_map/all_to_all | solution.py:42
  28.0 0.0 copy-done
  28.0 2.7 %fusion.2 = f32[16,256,128]{1,2,0:T(8,128)} fusion(bf16[256,16,128]{0,2,1:T(8,128)(2,1)S(1)} %bitcast.43, bf16[256,16,128]{0,2,1:T(8,128)(2,1)S(1)} %bitcast.41, pred[256,256]{1,0:T(8,128)(4,1)S(1)} %iota_compare_fusion, bf16[256,2048]{1,0:T(8,128)(2,1)S(1)} %copy-done), kind=kOutput, calls=%fused_computation.4 | convolution fusion | flops 538968064 | bytes 5308416 | tf_op jit(solution)/shard_map/hts,she->hte/dot_general | solution.py:52
  30.7 4.5 %all-to-all-done.1 = f16[8,128,128]{2,1,0:T(8,128)(2,1)S(1)} async-done(((f16[8,128,128]{2,1,0:T(8,128)(2,1)}), f16[8,128,128]{2,1,0:T(8,128)(2,1)S(1)}, u32[]{:S(2)}, u32[]{:S(2)}) %all-to-all-start.1) | async-done | bytes 262176 | tf_op jit(solution)/shard_map/all_to_all | solution.py:42
  35.2 0.0 copy-start.1
  35.2 1.2 %fusion.12 = bf16[1024,128]{1,0:T(8,128)(2,1)S(1)} fusion(f32[8,128,128]{2,1,0:T(8,128)S(1)} %convert_multiply_fusion, pred[]{:T(512)S(6)} %eq.3, f16[2048,128]{1,0:T(8,128)(2,1)} %bitcast, s32[]{:T(128)S(6)} %select_n.32), kind=kLoop, calls=%fused_computation.17 | loop fusion | flops 524288 | bytes 1048581 | tf_op jit(solution)/shard_map/convert_element_type | solution.py:46
  36.4 2.8 %collective-permute-start.1 = (bf16[1024,128]{1,0:T(8,128)(2,1)S(1)}, bf16[1024,128]{1,0:T(8,128)(2,1)S(1)}, u32[]{:S(2)}, u32[]{:S(2)}) collective-permute-start(bf16[1024,128]{1,0:T(8,128)(2,1)S(1)} %fusion.12), channel_id=1, source_target_pairs={{0,1},{1,0},{2,3},{3,2},{4,5},{5,4},{6,7},{7,6},{8,9},{9,8},{10,11... | collective-permute-start | bytes 786440 | tf_op jit(solution)/shard_map/ppermute | solution.py:18
  39.2 1.2 %collective-permute-done.1 = bf16[1024,128]{1,0:T(8,128)(2,1)S(1)} collective-permute-done((bf16[1024,128]{1,0:T(8,128)(2,1)S(1)}, bf16[1024,128]{1,0:T(8,128)(2,1)S(1)}, u32[]{:S(2)}, u32[]{:S(2)}) %collective-permute-start.1) | collective-permute-done | bytes 262176 | tf_op jit(solution)/shard_map/ppermute | solution.py:18
  40.4 1.1 %broadcast_select_fusion.1 = (bf16[1024,128]{1,0:T(8,128)(2,1)S(1)}, bf16[1024,128]{1,0:T(8,128)(2,1)S(1)}) fusion(bf16[1024,128]{1,0:T(8,128)(2,1)S(1)} %collective-permute-done.1, pred[]{:T(512)S(6)} %eq.3, f16[2048,128]{1,0:T(8,128)(2,1)} %collective-permute-done, s32[]{:T(128)S(6)} %select_n.32, f32[8,128,128]{2,1,0:T(8,128)S(1)} %convert_multiply_fusion), kind=kLoop, calls=%fused_computation.26 | loop fusion | flops 786432 | bytes 1572869 | tf_op jit(solution)/shard_map/jit(_where)/select_n | solution.py:56
  41.5 0.0 copy-done.1
  41.5 0.5 %fusion.1 = bf16[16,256,128]{1,2,0:T(8,128)(2,1)S(1)} fusion(f32[16,256,128]{1,2,0:T(8,128)S(1)} %copy-done.1, bf16[16,128,128]{2,1,0:T(8,128)(2,1)S(1)} %bitcast.45, bf16[256,2048]{1,0:T(8,128)(2,1)S(1)} %copy-done), kind=kOutput, calls=%fused_computation.3 | convolution fusion | flops 135790592 | bytes 4718592 | tf_op jit(solution)/shard_map/thd,hed->hte/dot_general | solution.py:59
  42.0 1.4 %copy.8 = bf16[256,2048]{1,0:T(8,128)(2,1)} copy(bf16[256,2048]{0,1:T(8,128)(2,1)S(1)} %bitcast.44) | data formatting | bytes 2097152 | tf_op jit(solution)/shard_map/reshape | solution.py:62
  (3 shorter events, 0.1 us)
Async XLA Ops:
  0.0 28.0 %copy-start = (bf16[256,2048]{1,0:T(8,128)(2,1)S(1)}, bf16[256,2048]{1,0:T(8,128)(2,1)}, u32[]{:S(2)}) copy-start(bf16[256,2048]{1,0:T(8,128)(2,1)} %param.3) | copy-start | bytes 3145732
  4.3 2.3 %collective-permute-start = (f16[2048,128]{1,0:T(8,128)(2,1)}, f16[2048,128]{1,0:T(8,128)(2,1)}, u32[]{:S(2)}, u32[]{:S(2)}) collective-permute-start(f16[2048,128]{1,0:T(8,128)(2,1)} %bitcast), channel_id=1, source_target_pairs={{0,1},{1,0},{2,3},{3,2},{4,5},{5,4},{6,7},{7,6},{8,9},{9,8},{10,11... | collective-permute-start | bytes 1572872 | tf_op jit(solution)/shard_map/ppermute | solution.py:18
  8.4 14.4 %all-to-all-start = ((f16[8,128,128]{2,1,0:T(8,128)(2,1)}), f16[8,128,128]{2,1,0:T(8,128)(2,1)S(1)}, u32[]{:S(2)}, u32[]{:S(2)}) async-start(f16[8,128,128]{2,1,0:T(8,128)(2,1)} %bitcast.46), calls=%async_computation | async-start | bytes 524288 | tf_op jit(solution)/shard_map/all_to_all | solution.py:36
  23.5 11.6 %all-to-all-start.1 = ((f16[8,128,128]{2,1,0:T(8,128)(2,1)}), f16[8,128,128]{2,1,0:T(8,128)(2,1)S(1)}, u32[]{:S(2)}, u32[]{:S(2)}) async-start(f16[8,128,128]{2,1,0:T(8,128)(2,1)} %fusion.4), calls=%async_computation.1 | async-start | bytes 524288 | tf_op jit(solution)/shard_map/all_to_all | solution.py:42
  35.2 6.3 %copy-start.1 = (f32[16,256,128]{1,2,0:T(8,128)S(1)}, f32[16,256,128]{1,2,0:T(8,128)}, u32[]{:S(2)}) copy-start(f32[16,256,128]{1,2,0:T(8,128)} %fusion.2) | copy-start | bytes 6291460
  36.4 3.9 %collective-permute-start.1 = (bf16[1024,128]{1,0:T(8,128)(2,1)S(1)}, bf16[1024,128]{1,0:T(8,128)(2,1)S(1)}, u32[]{:S(2)}, u32[]{:S(2)}) collective-permute-start(bf16[1024,128]{1,0:T(8,128)(2,1)S(1)} %fusion.12), channel_id=1, source_target_pairs={{0,1},{1,0},{2,3},{3,2},{4,5},{5,4},{6,7},{7,6},{8,9},{9,8},{10,11... | collective-permute-start | bytes 786440 | tf_op jit(solution)/shard_map/ppermute | solution.py:18

commit v14 on v12

--- a/solution.py
+++ b/solution.py
@@ -28,11 +28,10 @@
     local_state = jnp.einsum("the,thd->hed", v_blk, k_blk, preferred_element_type=jnp.float32)
     flat = local_state.reshape(HEADS * DK, DK).astype(jnp.float16)
     half = HEADS * DK // 2
-    to_second = lax.ppermute(flat[half:], "core", [(0, 1)])
-    to_first = lax.ppermute(flat[:half], "core", [(1, 0)])
     first = core == 0
-    own = jnp.where(first, flat[:half], flat[half:]).astype(jnp.float32)
-    partner = (to_first + to_second).astype(jnp.float32)
+    low, high = flat[:half], flat[half:]
+    partner = swap_cores(jnp.where(first, high, low)).astype(jnp.float32)
+    own = jnp.where(first, low, high).astype(jnp.float32)
     chip_sum = own + partner
     received = lax.all_to_all(chip_sum.astype(jnp.float16), "chip", split_axis=0, concat_axis=0, tiled=True)
     received = received.reshape(chips, half // chips, DK).astype(jnp.float32)
@@ -52,9 +51,7 @@
     intra = jnp.einsum("hts,she->the", scores, v_blk, preferred_element_type=jnp.float32)
     sent, intra = lax.optimization_barrier((sent, intra))
     got = swap_cores(sent)
-    low = jnp.where(first, kept, got)
-    high = jnp.where(first, got, kept)
-    carried = jnp.concatenate([low, high], axis=0).reshape(HEADS, DK, DK)
+    carried = jnp.concatenate([jnp.where(first, kept, got), jnp.where(first, got, kept)], axis=0).reshape(HEADS, DK, DK)
     inter = jnp.einsum("thd,hed->the", q_blk, carried, preferred_element_type=jnp.float32)
     scale = 1.0 / jnp.sqrt(jnp.float32(DK * tok * sources))
     attended = ((intra + inter) * scale).astype(jnp.bfloat16)

time: 42.7 us -> 38 us (0.89)
  starting transfers between devices: 10.3 us -> 7.33 us
  waiting for transfers between devices: 6.88 us -> 5.95 us
  blocking collectives: 14.8 us -> 14.2 us
    ppermute x2 -> x0, starting transfers between devices: 3.27 us -> none  [the longest x1 1.98 us: on_device(): to_first = lax.ppermute(flat[:half], 'core', [(1, 0)])]
    ppermute x2 -> x0, waiting for transfers between devices: 2.12 us -> none  [the longest x1 2.11 us: on_device(): to_second = lax.ppermute(flat[half:], 'core', [(0, 1)])]
    ppermute x1 -> x2, waiting for transfers between devices: 1.16 us -> 2.64 us  [swap_cores(): return lax.ppermute(x, 'core', [(0, 1), (1, 0)])]
    all_to_all x1, blocking collectives: 14.8 us -> 14.2 us  [on_device(): lax.all_to_all(chip_sum.astype(jnp.float16), 'chip', split_axis=0, concat...]
    ppermute x1 -> x2, starting transfers between devices: 2.48 us -> 2.88 us  [swap_cores(): return lax.ppermute(x, 'core', [(0, 1), (1, 0)])]
  transfers between devices with their start and end apart: 4 -> 3, of which waited for: 3 -> 3; matrix products, arithmetic and copies ran while one was open for 9% -> 10% of each run, Pallas kernels for 0% -> 0%
where the time goes in v14:
time: 38 us; the launch traced here: 37.4 us
  blocking collectives  14.2 us (37%)
  starting transfers between devices  7.33 us (19%)
  waiting for transfers between devices  5.95 us (16%)
  matrix products  4.82 us (13%)
  local copies, waits for them, and re-layouts  3.59 us (9%)
  other arithmetic  1.42 us (4%)
    all_to_all x1, blocking collectives, on_device(): lax.all_to_all(chip_sum.astype(jnp.float16), 'chip', split_axis=0, concat...  14.2 us
    all_to_all x1, starting transfers between devices, on_device(): lax.all_to_all((earlier * down).astype(jnp.float16), 'chip', split_axis=0...  4.45 us
    dot_general x1, matrix products, on_device(): jnp.einsum('hts,she->the', scores, v_blk, preferred_element_type=jnp.floa...  3.83 us
    all_to_all x1, waiting for transfers between devices, on_device(): lax.all_to_all((earlier * down).astype(jnp.float16), 'chip', split_axis=0...  3.31 us
    ppermute x2, starting transfers between devices, swap_cores(): return lax.ppermute(x, 'core', [(0, 1), (1, 0)])  2.88 us
    ppermute x2, waiting for transfers between devices, swap_cores(): return lax.ppermute(x, 'core', [(0, 1), (1, 0)])  2.64 us
    reshape x1, local copies, waits for them, and re-layouts, on_device(): k_blk = keys.reshape(tok, HEADS, DK)  1.62 us
    reshape x1, local copies, waits for them, and re-layouts, on_device(): return attended.reshape(tok, HEADS * DK)  1.42 us
  transfers between devices with their start and end apart: 3, of which 3 were waited for; matrix products, arithmetic and copies ran while one was open for 10% of the time, Pallas kernels for 0%

profile of v14, /device:TPU:1, one launch (start us, length us, event | category | flops | bytes accessed | tf_op | source)
XLA Modules:
  0.0 37.4 jit_solution(10418356067431273791)
XLA Ops:
  0.0 0.0 copy-start
  0.0 0.0 copy-start.2
  0.0 1.6 %copy.18 = bf16[256,2048]{0,1:T(8,128)(2,1)S(1)} copy(bf16[256,2048]{1,0:T(8,128)(2,1)} %param.4) | data formatting | bytes 2097152 | tf_op jit(solution)/shard_map/reshape | solution.py:26
  1.6 0.0 copy-done.2
  1.7 0.5 %convolution_convert_fusion = f16[16,128,128]{2,1,0:T(8,128)(2,1)S(1)} fusion(bf16[256,16,128]{0,2,1:T(8,128)(2,1)S(1)} %bitcast.53, bf16[256,2048]{1,0:T(8,128)(2,1)S(1)} %copy-done.2), kind=kOutput, calls=%fused_computation.6 | convolution fusion | flops 134479872 | bytes 2621440 | tf_op jit(solution)/shard_map/the,thd->hed/dot_general | solution.py:28
  2.1 0.2 broadcast_select_fusion.3
  2.3 0.1 collective-permute-start
  2.4 1.5 %collective-permute-done = f16[1024,128]{1,0:T(8,128)(2,1)S(1)} collective-permute-done((f16[1024,128]{1,0:T(8,128)(2,1)S(1)}, f16[1024,128]{1,0:T(8,128)(2,1)S(1)}, u32[]{:S(2)}, u32[]{:S(2)}) %collective-permute-start) | collective-permute-done | bytes 262176 | tf_op jit(solution)/shard_map/ppermute | solution.py:17
  3.9 0.1 fusion.18
  4.0 14.2 %all_to_all.14 = f16[8,128,128]{2,1,0:T(8,128)(2,1)S(1)} all-to-all(f16[8,128,128]{2,1,0:T(8,128)(2,1)S(1)} %bitcast.57), channel_id=1, replica_groups=mesh['groups'=2,'chip'=8,'core'=2] {'chip'}, dimensions={0} | all-to-all | bytes 524288 | tf_op jit(solution)/shard_map/all_to_all | solution.py:36
  18.2 0.8 %fusion.5 = f16[8,128,128]{2,1,0:T(8,128)(2,1)} fusion(f16[8,128,128]{2,1,0:T(8,128)(2,1)S(1)} %all_to_all.14), kind=kOutput, calls=%fused_computation.9 | output fusion | flops 1441792 | bytes 524288 | tf_op jit(solution)/shard_map/jit(cumsum)/reduce_window_sum | solution.py:38
  19.0 4.5 %all-to-all-start.1 = ((f16[8,128,128]{2,1,0:T(8,128)(2,1)}), f16[8,128,128]{2,1,0:T(8,128)(2,1)S(1)}, u32[]{:S(2)}, u32[]{:S(2)}) async-start(f16[8,128,128]{2,1,0:T(8,128)(2,1)} %fusion.5), calls=%async_computation.1 | async-start | bytes 524288 | tf_op jit(solution)/shard_map/all_to_all | solution.py:42
  23.5 0.0 copy-done
  23.5 3.8 %fusion.3 = f32[256,16,128]{2,0,1:T(8,128)} fusion(bf16[256,16,128]{0,2,1:T(8,128)(2,1)S(1)} %bitcast.54, pred[256,256]{1,0:T(8,128)(4,1)S(1)} %iota_compare_fusion, bf16[256,2048]{1,0:T(8,128)(2,1)S(1)} %copy-done, bf16[256,2048]{1,0:T(8,128)(2,1)} %param.5), kind=kOutput, calls=%fused_computation.5 | convolution fusion | flops 538968064 | bytes 5308416 | tf_op jit(solution)/shard_map/hts,she->the/dot_general | solution.py:51
  27.3 3.3 %all-to-all-done.1 = f16[8,128,128]{2,1,0:T(8,128)(2,1)S(1)} async-done(((f16[8,128,128]{2,1,0:T(8,128)(2,1)}), f16[8,128,128]{2,1,0:T(8,128)(2,1)S(1)}, u32[]{:S(2)}, u32[]{:S(2)}) %all-to-all-start.1) | async-done | bytes 262176 | tf_op jit(solution)/shard_map/all_to_all | solution.py:42
  30.6 0.0 copy-start.1
  30.7 0.1 fusion.20
  30.8 2.8 %collective-permute-start.1 = (bf16[1024,128]{1,0:T(8,128)(2,1)S(1)}, bf16[1024,128]{1,0:T(8,128)(2,1)S(1)}, u32[]{:S(2)}, u32[]{:S(2)}) collective-permute-start(bf16[1024,128]{1,0:T(8,128)(2,1)S(1)} %fusion.20), channel_id=1, source_target_pairs={{0,1},{1,0},{2,3},{3,2},{4,5},{5,4},{6,7},{7,6},{8,9},{9,8},{10,11... | collective-permute-start | bytes 786440 | tf_op jit(solution)/shard_map/ppermute | solution.py:17
  33.5 1.2 %collective-permute-done.1 = bf16[1024,128]{1,0:T(8,128)(2,1)S(1)} collective-permute-done((bf16[1024,128]{1,0:T(8,128)(2,1)S(1)}, bf16[1024,128]{1,0:T(8,128)(2,1)S(1)}, u32[]{:S(2)}, u32[]{:S(2)}) %collective-permute-start.1) | collective-permute-done | bytes 262176 | tf_op jit(solution)/shard_map/ppermute | solution.py:17
  34.7 0.1 broadcast_select_fusion.1
  34.9 0.0 copy-done.1
  34.9 0.5 %fusion.1 = bf16[256,16,128]{2,0,1:T(8,128)(2,1)S(1)} fusion(f32[256,16,128]{2,0,1:T(8,128)S(1)} %copy-done.1, bf16[16,128,128]{2,1,0:T(8,128)(2,1)S(1)} %bitcast.56, bf16[256,2048]{1,0:T(8,128)(2,1)S(1)} %copy-done), kind=kOutput, calls=%fused_computation.3 | convolution fusion | flops 135790592 | bytes 4718592 | tf_op jit(solution)/shard_map/thd,hed->the/dot_general | solution.py:55
  35.4 0.5 %copy.14 = bf16[256,16,128]{0,2,1:T(8,128)(2,1)S(1)} copy(bf16[256,16,128]{2,0,1:T(8,128)(2,1)S(1)} %fusion.1) | data formatting | bytes 2097152 | tf_op jit(solution)/shard_map/convert_element_type | solution.py:57
  36.0 1.4 %copy.15 = bf16[256,2048]{1,0:T(8,128)(2,1)} copy(bf16[256,2048]{0,1:T(8,128)(2,1)S(1)} %bitcast.55) | data formatting | bytes 2097152 | tf_op jit(solution)/shard_map/reshape | solution.py:58
  (3 shorter events, 0.1 us)
Async XLA Ops:
  0.0 23.5 %copy-start = (bf16[256,2048]{1,0:T(8,128)(2,1)S(1)}, bf16[256,2048]{1,0:T(8,128)(2,1)}, u32[]{:S(2)}) copy-start(bf16[256,2048]{1,0:T(8,128)(2,1)} %param.3) | copy-start | bytes 3145732
  0.0 1.6 %copy-start.2 = (bf16[256,2048]{1,0:T(8,128)(2,1)S(1)}, bf16[256,2048]{1,0:T(8,128)(2,1)}, u32[]{:S(2)}) copy-start(bf16[256,2048]{1,0:T(8,128)(2,1)} %param.5) | copy-start | bytes 3145732
  2.3 1.6 %collective-permute-start = (f16[1024,128]{1,0:T(8,128)(2,1)S(1)}, f16[1024,128]{1,0:T(8,128)(2,1)S(1)}, u32[]{:S(2)}, u32[]{:S(2)}) collective-permute-start(f16[1024,128]{1,0:T(8,128)(2,1)S(1)} %bitcast.58), channel_id=1, source_target_pairs={{0,1},{1,0},{2,3},{3,2},{4,5},{5,4},{6,7},{7,6},{8,9},{9,8},{10,11... | collective-permute-start | bytes 786440 | tf_op jit(solution)/shard_map/ppermute | solution.py:17
  19.0 11.6 %all-to-all-start.1 = ((f16[8,128,128]{2,1,0:T(8,128)(2,1)}), f16[8,128,128]{2,1,0:T(8,128)(2,1)S(1)}, u32[]{:S(2)}, u32[]{:S(2)}) async-start(f16[8,128,128]{2,1,0:T(8,128)(2,1)} %fusion.5), calls=%async_computation.1 | async-start | bytes 524288 | tf_op jit(solution)/shard_map/all_to_all | solution.py:42
  30.6 4.3 %copy-start.1 = (f32[256,16,128]{2,0,1:T(8,128)S(1)}, f32[256,16,128]{2,0,1:T(8,128)}, u32[]{:S(2)}) copy-start(f32[256,16,128]{2,0,1:T(8,128)} %fusion.3) | copy-start | bytes 6291460
  30.8 3.9 %collective-permute-start.1 = (bf16[1024,128]{1,0:T(8,128)(2,1)S(1)}, bf16[1024,128]{1,0:T(8,128)(2,1)S(1)}, u32[]{:S(2)}, u32[]{:S(2)}) collective-permute-start(bf16[1024,128]{1,0:T(8,128)(2,1)S(1)} %fusion.20), channel_id=1, source_target_pairs={{0,1},{1,0},{2,3},{3,2},{4,5},{5,4},{6,7},{7,6},{8,9},{9,8},{10,11... | collective-permute-start | bytes 786440 | tf_op jit(solution)/shard_map/ppermute | solution.py:17

commit v15 on v14

--- a/solution.py
+++ b/solution.py
@@ -1,9 +1,12 @@
+import functools
 import math
 
 import jax
 import jax.numpy as jnp
 import numpy as np
 from jax import lax
+from jax.experimental import pallas as pl
+from jax.experimental.pallas import tpu as pltpu
 from jax.sharding import Mesh
 from jax.sharding import PartitionSpec as P
 
@@ -11,6 +14,31 @@
 DK = 128
 LIMIT = 6.0
 F16_MAX = 65504.0
+
+
+def combine_kernel(scale, q_ref, p_ref, intra_ref, o_ref):
+    for h in range(HEADS):
+        cols = slice(h * DK, (h + 1) * DK)
+        inter = lax.dot_general(
+            q_ref[:, cols], p_ref[h * DK:(h + 1) * DK, :], (((1,), (1,)), ((), ())),
+            preferred_element_type=jnp.float32,
+        )
+        o_ref[:, cols] = ((intra_ref[h] + inter) * scale).astype(o_ref.dtype)
+
+
+def combine(queries, carried_t, intra, scale):
+    tok = queries.shape[0]
+    whole = pl.BlockSpec(memory_space=pltpu.VMEM)
+    return pl.pallas_call(
+        functools.partial(combine_kernel, scale),
+        in_specs=[whole] * 3,
+        out_specs=whole,
+        out_shape=jax.ShapeDtypeStruct((tok, HEADS * DK), jnp.bfloat16),
+        cost_estimate=pl.CostEstimate(
+            flops=2 * tok * DK * DK * HEADS, transcendentals=0,
+            bytes_accessed=2 * tok * HEADS * DK * 2 + tok * HEADS * DK * 4 + HEADS * DK * DK * 2,
+        ),
+    )(queries, carried_t, intra)
 
 
 def swap_cores(x):
@@ -48,15 +76,12 @@
     causal = cols <= rows
     scores = jnp.einsum("thd,shd->hts", q_blk, k_blk, preferred_element_type=jnp.float32)
     scores = jnp.where(causal[None], scores, jnp.float32(0.0)).astype(jnp.bfloat16)
-    intra = jnp.einsum("hts,she->the", scores, v_blk, preferred_element_type=jnp.float32)
+    intra = jnp.einsum("hts,she->hte", scores, v_blk, preferred_element_type=jnp.float32)
     sent, intra = lax.optimization_barrier((sent, intra))
     got = swap_cores(sent)
-    carried = jnp.concatenate([jnp.where(first, kept, got), jnp.where(first, got, kept)], axis=0).reshape(HEADS, DK, DK)
-    inter = jnp.einsum("thd,hed->the", q_blk, carried, preferred_element_type=jnp.float32)
-    scale = 1.0 / jnp.sqrt(jnp.float32(DK * tok * sources))
-    attended = ((intra + inter) * scale).astype(jnp.bfloat16)
-    return attended.reshape(tok, HEADS * DK)
-
+    carried_t = jnp.concatenate([jnp.where(first, kept, got), jnp.where(first, got, kept)], axis=0)
+    scale = float(np.float32(1.0) / np.sqrt(np.float32(DK * tok * sources)))
+    return combine(queries, carried_t, intra, scale)
 
 def solution(mesh):
     devices = mesh.devices

time: 38 us -> 39.8 us (1.047)
  Pallas kernels: 0 us -> 3.53 us
  local copies, waits for them, and re-layouts: 3.59 us -> 1.57 us
  other arithmetic: 1.42 us -> 2.19 us
  matrix products: 4.82 us -> 4.29 us
    pallas_call x0 -> x1, Pallas kernels: none -> 3.53 us  [combine(): pl.pallas_call(functools.partial(combine_kernel, scale), in_specs=[whole]...]
    reshape x1 -> x0, local copies, waits for them, and re-layouts: 1.42 us -> none  [on_device(): return attended.reshape(tok, HEADS * DK)]
    concatenate x1, other arithmetic: 0.04 us -> 0.83 us  [on_device(): jnp.concatenate([jnp.where(first, kept, got), jnp.where(first, got, kept)...]
    convert_element_type x1 -> x0, local copies, waits for them, and re-layouts: 0.53 us -> none  [on_device(): attended = ((intra + inter) * scale).astype(jnp.bfloat16)]
    dot_general x2 -> x1, matrix products: 4.33 us -> 3.81 us  [on_device(): jnp.einsum('hts,she->hte', scores, v_blk, preferred_element_type=jnp.floa...]
where the time goes in v15:
time: 39.8 us; the launch traced here: 39.1 us
  blocking collectives  14.2 us (36%)
  starting transfers between devices  7.33 us (18%)
  waiting for transfers between devices  5.99 us (15%)
  matrix products  4.29 us (11%)
  Pallas kernels  3.53 us (9%)
  other arithmetic  2.19 us (6%)
  local copies, waits for them, and re-layouts  1.57 us (4%)
    all_to_all x1, blocking collectives, on_device(): lax.all_to_all(chip_sum.astype(jnp.float16), 'chip', split_axis=0, concat...  14.2 us
    all_to_all x1, starting transfers between devices, on_device(): lax.all_to_all((earlier * down).astype(jnp.float16), 'chip', split_axis=0...  4.45 us
    dot_general x1, matrix products, on_device(): jnp.einsum('hts,she->hte', scores, v_blk, preferred_element_type=jnp.floa...  3.81 us
    pallas_call x1, Pallas kernels, combine(): pl.pallas_call(functools.partial(combine_kernel, scale), in_specs=[whole]...  3.53 us
    all_to_all x1, waiting for transfers between devices, on_device(): lax.all_to_all((earlier * down).astype(jnp.float16), 'chip', split_axis=0...  3.34 us
    ppermute x2, starting transfers between devices, swap_cores(): return lax.ppermute(x, 'core', [(0, 1), (1, 0)])  2.88 us
    ppermute x2, waiting for transfers between devices, swap_cores(): return lax.ppermute(x, 'core', [(0, 1), (1, 0)])  2.64 us
    reshape x1, local copies, waits for them, and re-layouts, on_device(): k_blk = keys.reshape(tok, HEADS, DK)  1.56 us
  transfers between devices with their start and end apart: 3, of which 3 were waited for; matrix products, arithmetic and copies ran while one was open for 10% of the time, Pallas kernels for 0%

profile of v15, /device:TPU:1, one launch (start us, length us, event | category | flops | bytes accessed | tf_op | source)
XLA Modules:
  0.0 39.1 jit_solution(2457466846761378346)
XLA Ops:
  0.0 0.0 copy-start
  0.0 1.6 %copy.9 = bf16[256,2048]{0,1:T(8,128)(2,1)S(1)} copy(bf16[256,2048]{1,0:T(8,128)(2,1)} %param.4) | data formatting | bytes 2097152 | tf_op jit(solution)/shard_map/reshape | solution.py:54
  1.6 0.0 copy-done
  1.6 0.5 %convolution_convert_fusion = f16[16,128,128]{2,1,0:T(8,128)(2,1)S(1)} fusion(bf16[256,16,128]{0,2,1:T(8,128)(2,1)S(1)} %bitcast.37, bf16[256,2048]{1,0:T(8,128)(2,1)S(1)} %copy-done), kind=kOutput, calls=%fused_computation.2 | convolution fusion | flops 134479872 | bytes 2621440 | tf_op jit(solution)/shard_map/the,thd->hed/dot_general | solution.py:56
  2.1 0.1 broadcast_select_fusion.1
  2.2 0.1 collective-permute-start
  2.4 1.5 %collective-permute-done = f16[1024,128]{1,0:T(8,128)(2,1)S(1)} collective-permute-done((f16[1024,128]{1,0:T(8,128)(2,1)S(1)}, f16[1024,128]{1,0:T(8,128)(2,1)S(1)}, u32[]{:S(2)}, u32[]{:S(2)}) %collective-permute-start) | collective-permute-done | bytes 262176 | tf_op jit(solution)/shard_map/ppermute | solution.py:45
  3.8 0.1 fusion.13
  3.9 14.2 %all_to_all.14 = f16[8,128,128]{2,1,0:T(8,128)(2,1)S(1)} all-to-all(f16[8,128,128]{2,1,0:T(8,128)(2,1)S(1)} %bitcast.39), channel_id=1, replica_groups=mesh['groups'=2,'chip'=8,'core'=2] {'chip'}, dimensions={0} | all-to-all | bytes 524288 | tf_op jit(solution)/shard_map/all_to_all | solution.py:64
  18.1 0.8 %fusion.2 = f16[8,128,128]{2,1,0:T(8,128)(2,1)} fusion(f16[8,128,128]{2,1,0:T(8,128)(2,1)S(1)} %all_to_all.14), kind=kOutput, calls=%fused_computation.5 | output fusion | flops 1441792 | bytes 524288 | tf_op jit(solution)/shard_map/jit(cumsum)/reduce_window_sum | solution.py:66
  18.9 4.5 %all-to-all-start.1 = ((f16[8,128,128]{2,1,0:T(8,128)(2,1)}), f16[8,128,128]{2,1,0:T(8,128)(2,1)S(1)}, u32[]{:S(2)}, u32[]{:S(2)}) async-start(f16[8,128,128]{2,1,0:T(8,128)(2,1)} %fusion.2), calls=%async_computation.1 | async-start | bytes 524288 | tf_op jit(solution)/shard_map/all_to_all | solution.py:70
  23.4 3.8 %fusion.intra_ref = f32[16,256,128]{2,1,0:T(8,128)} fusion(bf16[256,16,128]{0,2,1:T(8,128)(2,1)S(1)} %bitcast.38, pred[256,256]{1,0:T(8,128)(4,1)S(1)} %iota_compare_fusion, bf16[256,2048]{1,0:T(8,128)(2,1)} %q_ref.1, bf16[256,2048]{1,0:T(8,128)(2,1)S(1)} %copy-done), kind=kOutput, calls=%fused_computation.1 | convolution fusion | flops 538968064 | bytes 5308416 | tf_op jit(solution)/shard_map/hts,she->hte/dot_general | solution.py:79
  27.2 3.3 %all-to-all-done.1 = f16[8,128,128]{2,1,0:T(8,128)(2,1)S(1)} async-done(((f16[8,128,128]{2,1,0:T(8,128)(2,1)}), f16[8,128,128]{2,1,0:T(8,128)(2,1)S(1)}, u32[]{:S(2)}, u32[]{:S(2)}) %all-to-all-start.1) | async-done | bytes 262176 | tf_op jit(solution)/shard_map/all_to_all | solution.py:70
  30.6 0.1 fusion.15
  30.7 2.8 %collective-permute-start.1 = (bf16[1024,128]{1,0:T(8,128)(2,1)S(1)}, bf16[1024,128]{1,0:T(8,128)(2,1)S(1)}, u32[]{:S(2)}, u32[]{:S(2)}) collective-permute-start(bf16[1024,128]{1,0:T(8,128)(2,1)S(1)} %fusion.15), channel_id=1, source_target_pairs={{0,1},{1,0},{2,3},{3,2},{4,5},{5,4},{6,7},{7,6},{8,9},{9,8},{10,11... | collective-permute-start | bytes 786440 | tf_op jit(solution)/shard_map/ppermute | solution.py:45
  33.5 1.2 %collective-permute-done.1 = bf16[1024,128]{1,0:T(8,128)(2,1)S(1)} collective-permute-done((bf16[1024,128]{1,0:T(8,128)(2,1)S(1)}, bf16[1024,128]{1,0:T(8,128)(2,1)S(1)}, u32[]{:S(2)}, u32[]{:S(2)}) %collective-permute-start.1) | collective-permute-done | bytes 262176 | tf_op jit(solution)/shard_map/ppermute | solution.py:45
  34.6 0.1 broadcast_select_fusion.3
  34.8 0.8 %pad_maximum_fusion.p_ref = bf16[2048,128]{1,0:T(8,128)(2,1)} fusion(bf16[1024,128]{1,0:T(8,128)(2,1)S(1)} %get-tuple-element.10, bf16[1024,128]{1,0:T(8,128)(2,1)S(1)} %get-tuple-element.9), kind=kLoop, calls=%fused_computation.20 | loop fusion | flops 1048576 | bytes 1048576 | tf_op jit(solution)/shard_map/concatenate | solution.py:82
  35.6 3.5 %shard_map.37 = bf16[256,2048]{1,0:T(8,128)(2,1)} custom-call(bf16[256,2048]{1,0:T(8,128)(2,1)} %q_ref.1, bf16[2048,128]{1,0:T(8,128)(2,1)} %pad_maximum_fusion.p_ref, f32[16,256,128]{2,1,0:T(8,128)} %fusion.intra_ref), custom_call_target="tpu_custom_call" | custom-call | flops 134217728 | bytes 4718592 | tf_op jit(solution)/shard_map/pallas_call | solution.py:32
  (2 shorter events, 0.1 us)
Async XLA Ops:
  0.0 1.6 %copy-start = (bf16[256,2048]{1,0:T(8,128)(2,1)S(1)}, bf16[256,2048]{1,0:T(8,128)(2,1)}, u32[]{:S(2)}) copy-start(bf16[256,2048]{1,0:T(8,128)(2,1)} %param.5) | copy-start | bytes 3145732
  2.2 1.6 %collective-permute-start = (f16[1024,128]{1,0:T(8,128)(2,1)S(1)}, f16[1024,128]{1,0:T(8,128)(2,1)S(1)}, u32[]{:S(2)}, u32[]{:S(2)}) collective-permute-start(f16[1024,128]{1,0:T(8,128)(2,1)S(1)} %bitcast.40), channel_id=1, source_target_pairs={{0,1},{1,0},{2,3},{3,2},{4,5},{5,4},{6,7},{7,6},{8,9},{9,8},{10,11... | collective-permute-start | bytes 786440 | tf_op jit(solution)/shard_map/ppermute | solution.py:45
  18.9 11.6 %all-to-all-start.1 = ((f16[8,128,128]{2,1,0:T(8,128)(2,1)}), f16[8,128,128]{2,1,0:T(8,128)(2,1)S(1)}, u32[]{:S(2)}, u32[]{:S(2)}) async-start(f16[8,128,128]{2,1,0:T(8,128)(2,1)} %fusion.2), calls=%async_computation.1 | async-start | bytes 524288 | tf_op jit(solution)/shard_map/all_to_all | solution.py:70
  30.7 3.9 %collective-permute-start.1 = (bf16[1024,128]{1,0:T(8,128)(2,1)S(1)}, bf16[1024,128]{1,0:T(8,128)(2,1)S(1)}, u32[]{:S(2)}, u32[]{:S(2)}) collective-permute-start(bf16[1024,128]{1,0:T(8,128)(2,1)S(1)} %fusion.15), channel_id=1, source_target_pairs={{0,1},{1,0},{2,3},{3,2},{4,5},{5,4},{6,7},{7,6},{8,9},{9,8},{10,11... | collective-permute-start | bytes 786440 | tf_op jit(solution)/shard_map/ppermute | solution.py:45

commit v16 on v14

--- a/solution.py
+++ b/solution.py
@@ -34,6 +34,7 @@
     own = jnp.where(first, low, high).astype(jnp.float32)
     chip_sum = own + partner
     received = lax.all_to_all(chip_sum.astype(jnp.float16), "chip", split_axis=0, concat_axis=0, tiled=True)
+    received, keys_late, values_late = lax.optimization_barrier((received, keys, values))
     received = received.reshape(chips, half // chips, DK).astype(jnp.float32)
     earlier = jnp.cumsum(received, axis=0) - received
     bound = (chips - 1) * 2 * tok * LIMIT * LIMIT
@@ -46,10 +47,11 @@
     rows = lax.broadcasted_iota(jnp.int32, (tok, tok), 0)
     cols = lax.broadcasted_iota(jnp.int32, (tok, tok), 1)
     causal = cols <= rows
-    scores = jnp.einsum("thd,shd->hts", q_blk, k_blk, preferred_element_type=jnp.float32)
+    scores = jnp.einsum("thd,shd->hts", q_blk, keys_late.reshape(tok, HEADS, DK), preferred_element_type=jnp.float32)
     scores = jnp.where(causal[None], scores, jnp.float32(0.0)).astype(jnp.bfloat16)
-    intra = jnp.einsum("hts,she->the", scores, v_blk, preferred_element_type=jnp.float32)
-    sent, intra = lax.optimization_barrier((sent, intra))
+    intra = jnp.einsum("hts,she->het", scores, values_late.reshape(tok, HEADS, DK), preferred_element_type=jnp.float32)
+    sent, intra = lax.optimization_barrier((sent, intra.reshape(HEADS * DK, tok)))
+    intra = jnp.transpose(intra.reshape(HEADS, DK, tok), (2, 0, 1))
     got = swap_cores(sent)
     carried = jnp.concatenate([jnp.where(first, kept, got), jnp.where(first, got, kept)], axis=0).reshape(HEADS, DK, DK)
     inter = jnp.einsum("thd,hed->the", q_blk, carried, preferred_element_type=jnp.float32)

time: 38 us -> 37.3 us (0.982)
  waiting for transfers between devices: 5.95 us -> 4.25 us
  local copies, waits for them, and re-layouts: 3.59 us -> 4.37 us
    all_to_all x1, waiting for transfers between devices: 3.31 us -> 1.6 us  [on_device(): lax.all_to_all((earlier * down).astype(jnp.float16), 'chip', split_axis=0...]
    reshape x1 -> x2, local copies, waits for them, and re-layouts: 1.62 us -> 2.93 us  [the longest x1 1.62 us: on_device(): v_blk = values.reshape(tok, HEADS, DK)]
    convert_element_type x1 -> x0, local copies, waits for them, and re-layouts: 0.53 us -> none  [on_device(): attended = ((intra + inter) * scale).astype(jnp.bfloat16)]
    dot_general x1, matrix products: 3.83 us -> 4.23 us  [on_device(): jnp.einsum('hts,she->het', scores, values_late.reshape(tok, HEADS, DK), p...]
  transfers between devices with their start and end apart: 3 -> 3, of which waited for: 3 -> 3; matrix products, arithmetic and copies ran while one was open for 10% -> 15% of each run, Pallas kernels for 0% -> 0%
where the time goes in v16:
time: 37.3 us; the launch traced here: 36.7 us
  blocking collectives  14.2 us (38%)
  starting transfers between devices  7.33 us (20%)
  matrix products  5.11 us (14%)
  local copies, waits for them, and re-layouts  4.37 us (12%)
  waiting for transfers between devices  4.25 us (11%)
  other arithmetic  1.4 us (4%)
    all_to_all x1, blocking collectives, on_device(): lax.all_to_all(chip_sum.astype(jnp.float16), 'chip', split_axis=0, concat...  14.2 us
    all_to_all x1, starting transfers between devices, on_device(): lax.all_to_all((earlier * down).astype(jnp.float16), 'chip', split_axis=0...  4.45 us
    dot_general x1, matrix products, on_device(): jnp.einsum('hts,she->het', scores, values_late.reshape(tok, HEADS, DK), p...  4.23 us
    ppermute x2, starting transfers between devices, swap_cores(): return lax.ppermute(x, 'core', [(0, 1), (1, 0)])  2.88 us
    ppermute x2, waiting for transfers between devices, swap_cores(): return lax.ppermute(x, 'core', [(0, 1), (1, 0)])  2.64 us
    reshape x1, local copies, waits for them, and re-layouts, on_device(): v_blk = values.reshape(tok, HEADS, DK)  1.62 us
    all_to_all x1, waiting for transfers between devices, on_device(): lax.all_to_all((earlier * down).astype(jnp.float16), 'chip', split_axis=0...  1.6 us
    reshape x1, local copies, waits for them, and re-layouts, on_device(): return attended.reshape(tok, HEADS * DK)  1.42 us
  transfers between devices with their start and end apart: 3, of which 3 were waited for; matrix products, arithmetic and copies ran while one was open for 15% of the time, Pallas kernels for 0%

profile of v16, /device:TPU:1, one launch (start us, length us, event | category | flops | bytes accessed | tf_op | source)
XLA Modules:
  0.0 36.7 jit_solution(6233953431014036206)
XLA Ops:
  0.0 0.0 copy-start
  0.0 0.0 copy-start.3
  0.0 1.6 %copy.11 = bf16[256,2048]{0,1:T(8,128)(2,1)S(1)} copy(bf16[256,2048]{1,0:T(8,128)(2,1)} %param.5) | data formatting | bytes 2097152 | tf_op jit(solution)/shard_map/reshape | solution.py:27
  1.6 0.0 copy-done.3
  1.7 0.4 %convolution_convert_fusion = f16[16,128,128]{2,1,0:T(8,128)(2,1)S(1)} fusion(bf16[256,16,128]{0,2,1:T(8,128)(2,1)S(1)} %bitcast.63, bf16[256,2048]{1,0:T(8,128)(2,1)S(1)} %copy-done.3), kind=kOutput, calls=%fused_computation.4 | convolution fusion | flops 134479872 | bytes 2621440 | tf_op jit(solution)/shard_map/the,thd->hed/dot_general | solution.py:28
  2.1 0.0 copy-start.1
  2.1 0.2 broadcast_select_fusion.3
  2.3 0.1 collective-permute-start
  2.4 1.5 %collective-permute-done = f16[1024,128]{1,0:T(8,128)(2,1)S(1)} collective-permute-done((f16[1024,128]{1,0:T(8,128)(2,1)S(1)}, f16[1024,128]{1,0:T(8,128)(2,1)S(1)}, u32[]{:S(2)}, u32[]{:S(2)}) %collective-permute-start) | collective-permute-done | bytes 262176 | tf_op jit(solution)/shard_map/ppermute | solution.py:17
  3.9 0.1 fusion.18
  4.0 14.2 %all_to_all.17 = f16[8,128,128]{2,1,0:T(8,128)(2,1)S(1)} all-to-all(f16[8,128,128]{2,1,0:T(8,128)(2,1)S(1)} %bitcast.66), channel_id=1, replica_groups=mesh['groups'=2,'chip'=8,'core'=2] {'chip'}, dimensions={0} | all-to-all | bytes 524288 | tf_op jit(solution)/shard_map/all_to_all | solution.py:36
  18.1 0.8 %fusion.3 = f16[8,128,128]{2,1,0:T(8,128)(2,1)} fusion(f16[8,128,128]{2,1,0:T(8,128)(2,1)S(1)} %all_to_all.17), kind=kOutput, calls=%fused_computation.7 | output fusion | flops 1441792 | bytes 524288 | tf_op jit(solution)/shard_map/jit(cumsum)/reduce_window_sum | solution.py:39
  18.9 4.5 %all-to-all-start.1 = ((f16[8,128,128]{2,1,0:T(8,128)(2,1)}), f16[8,128,128]{2,1,0:T(8,128)(2,1)S(1)}, u32[]{:S(2)}, u32[]{:S(2)}) async-start(f16[8,128,128]{2,1,0:T(8,128)(2,1)} %fusion.3), calls=%async_computation.1 | async-start | bytes 524288 | tf_op jit(solution)/shard_map/all_to_all | solution.py:43
  23.4 0.0 copy-done.1
  23.4 1.3 %copy.12 = bf16[256,2048]{0,1:T(8,128)(2,1)} copy(bf16[256,2048]{1,0:T(8,128)(2,1)S(1)} %copy-done.1) | data formatting | bytes 2097152 | tf_op jit(solution)/shard_map/reshape | solution.py:52
  24.7 0.0 copy-done
  24.7 4.2 %fusion.1 = f32[16,128,256]{2,1,0:T(8,128)} fusion(bf16[256,16,128]{0,2,1:T(8,128)(2,1)} %bitcast.67, pred[256,256]{1,0:T(8,128)(4,1)S(1)} %iota_compare_fusion, bf16[256,2048]{1,0:T(8,128)(2,1)S(1)} %copy-done, bf16[256,2048]{1,0:T(8,128)(2,1)} %param.4), kind=kOutput, calls=%fused_computation.3 | convolution fusion | flops 538968064 | bytes 5308416 | tf_op jit(solution)/shard_map/hts,she->het/dot_general | solution.py:52
  29.0 1.6 %all-to-all-done.1 = f16[8,128,128]{2,1,0:T(8,128)(2,1)S(1)} async-done(((f16[8,128,128]{2,1,0:T(8,128)(2,1)}), f16[8,128,128]{2,1,0:T(8,128)(2,1)S(1)}, u32[]{:S(2)}, u32[]{:S(2)}) %all-to-all-start.1) | async-done | bytes 262176 | tf_op jit(solution)/shard_map/all_to_all | solution.py:43
  30.6 0.0 copy-start.2
  30.6 0.1 fusion.20
  30.7 2.8 %collective-permute-start.1 = (bf16[1024,128]{1,0:T(8,128)(2,1)S(1)}, bf16[1024,128]{1,0:T(8,128)(2,1)S(1)}, u32[]{:S(2)}, u32[]{:S(2)}) collective-permute-start(bf16[1024,128]{1,0:T(8,128)(2,1)S(1)} %fusion.20), channel_id=1, source_target_pairs={{0,1},{1,0},{2,3},{3,2},{4,5},{5,4},{6,7},{7,6},{8,9},{9,8},{10,11... | collective-permute-start | bytes 786440 | tf_op jit(solution)/shard_map/ppermute | solution.py:17
  33.5 1.2 %collective-permute-done.1 = bf16[1024,128]{1,0:T(8,128)(2,1)S(1)} collective-permute-done((bf16[1024,128]{1,0:T(8,128)(2,1)S(1)}, bf16[1024,128]{1,0:T(8,128)(2,1)S(1)}, u32[]{:S(2)}, u32[]{:S(2)}) %collective-permute-start.1) | collective-permute-done | bytes 262176 | tf_op jit(solution)/shard_map/ppermute | solution.py:17
  34.6 0.1 broadcast_select_fusion.1
  34.8 0.0 copy-done.2
  34.8 0.5 %multiply_convert_fusion = bf16[16,128,256]{2,1,0:T(8,128)(2,1)S(1)} fusion(f32[16,128,256]{2,1,0:T(8,128)S(1)} %copy-done.2, bf16[16,128,128]{2,1,0:T(8,128)(2,1)S(1)} %bitcast.65, bf16[256,2048]{1,0:T(8,128)(2,1)S(1)} %copy-done), kind=kOutput, calls=%fused_computation.2 | convolution fusion | flops 135790592 | bytes 4718592 | tf_op jit(solution)/shard_map/thd,hed->the/dot_general | solution.py:57
  35.3 1.4 %copy.8 = bf16[256,2048]{1,0:T(8,128)(2,1)} copy(bf16[256,2048]{0,1:T(8,128)(2,1)S(1)} %bitcast.64) | data formatting | bytes 2097152 | tf_op jit(solution)/shard_map/reshape | solution.py:60
  (3 shorter events, 0.1 us)
Async XLA Ops:
  0.0 24.7 %copy-start = (bf16[256,2048]{1,0:T(8,128)(2,1)S(1)}, bf16[256,2048]{1,0:T(8,128)(2,1)}, u32[]{:S(2)}) copy-start(bf16[256,2048]{1,0:T(8,128)(2,1)} %param.3) | copy-start | bytes 3145732
  0.0 1.6 %copy-start.3 = (bf16[256,2048]{1,0:T(8,128)(2,1)S(1)}, bf16[256,2048]{1,0:T(8,128)(2,1)}, u32[]{:S(2)}) copy-start(bf16[256,2048]{1,0:T(8,128)(2,1)} %param.4) | copy-start | bytes 3145732
  2.1 21.3 %copy-start.1 = (bf16[256,2048]{1,0:T(8,128)(2,1)S(1)}, bf16[256,2048]{1,0:T(8,128)(2,1)}, u32[]{:S(2)}) copy-start(bf16[256,2048]{1,0:T(8,128)(2,1)} %param.5) | copy-start | bytes 3145732
  2.3 1.6 %collective-permute-start = (f16[1024,128]{1,0:T(8,128)(2,1)S(1)}, f16[1024,128]{1,0:T(8,128)(2,1)S(1)}, u32[]{:S(2)}, u32[]{:S(2)}) collective-permute-start(f16[1024,128]{1,0:T(8,128)(2,1)S(1)} %bitcast.68), channel_id=1, source_target_pairs={{0,1},{1,0},{2,3},{3,2},{4,5},{5,4},{6,7},{7,6},{8,9},{9,8},{10,11... | collective-permute-start | bytes 786440 | tf_op jit(solution)/shard_map/ppermute | solution.py:17
  18.9 11.6 %all-to-all-start.1 = ((f16[8,128,128]{2,1,0:T(8,128)(2,1)}), f16[8,128,128]{2,1,0:T(8,128)(2,1)S(1)}, u32[]{:S(2)}, u32[]{:S(2)}) async-start(f16[8,128,128]{2,1,0:T(8,128)(2,1)} %fusion.3), calls=%async_computation.1 | async-start | bytes 524288 | tf_op jit(solution)/shard_map/all_to_all | solution.py:43
  30.6 4.3 %copy-start.2 = (f32[16,128,256]{2,1,0:T(8,128)S(1)}, f32[16,128,256]{2,1,0:T(8,128)}, u32[]{:S(2)}) copy-start(f32[16,128,256]{2,1,0:T(8,128)} %fusion.1) | copy-start | bytes 6291460
  30.7 3.9 %collective-permute-start.1 = (bf16[1024,128]{1,0:T(8,128)(2,1)S(1)}, bf16[1024,128]{1,0:T(8,128)(2,1)S(1)}, u32[]{:S(2)}, u32[]{:S(2)}) collective-permute-start(bf16[1024,128]{1,0:T(8,128)(2,1)S(1)} %fusion.20), channel_id=1, source_target_pairs={{0,1},{1,0},{2,3},{3,2},{4,5},{5,4},{6,7},{7,6},{8,9},{9,8},{10,11... | collective-permute-start | bytes 786440 | tf_op jit(solution)/shard_map/ppermute | solution.py:17

commit v17 on v16

--- a/solution.py
+++ b/solution.py
@@ -25,7 +25,7 @@
     q_blk = queries.reshape(tok, HEADS, DK)
     k_blk = keys.reshape(tok, HEADS, DK)
     v_blk = values.reshape(tok, HEADS, DK)
-    local_state = jnp.einsum("the,thd->hed", v_blk, k_blk, preferred_element_type=jnp.float32)
+    local_state = jnp.einsum("thd,the->hde", k_blk, v_blk, preferred_element_type=jnp.float32)
     flat = local_state.reshape(HEADS * DK, DK).astype(jnp.float16)
     half = HEADS * DK // 2
     first = core == 0
@@ -54,7 +54,7 @@
     intra = jnp.transpose(intra.reshape(HEADS, DK, tok), (2, 0, 1))
     got = swap_cores(sent)
     carried = jnp.concatenate([jnp.where(first, kept, got), jnp.where(first, got, kept)], axis=0).reshape(HEADS, DK, DK)
-    inter = jnp.einsum("thd,hed->the", q_blk, carried, preferred_element_type=jnp.float32)
+    inter = jnp.einsum("thd,hde->the", q_blk, carried, preferred_element_type=jnp.float32)
     scale = 1.0 / jnp.sqrt(jnp.float32(DK * tok * sources))
     attended = ((intra + inter) * scale).astype(jnp.bfloat16)
     return attended.reshape(tok, HEADS * DK)

time: 37.3 us -> 37.4 us (level)
  no operation moved by 1% of the time
where the time goes in v17:
time: 37.4 us; the launch traced here: 36.8 us
  blocking collectives  14.2 us (38%)
  starting transfers between devices  7.33 us (20%)
  matrix products  5.18 us (14%)
  local copies, waits for them, and re-layouts  4.37 us (12%)
  waiting for transfers between devices  4.25 us (11%)
  other arithmetic  1.4 us (4%)
    all_to_all x1, blocking collectives, on_device(): lax.all_to_all(chip_sum.astype(jnp.float16), 'chip', split_axis=0, concat...  14.2 us
    all_to_all x1, starting transfers between devices, on_device(): lax.all_to_all((earlier * down).astype(jnp.float16), 'chip', split_axis=0...  4.45 us
    dot_general x1, matrix products, on_device(): jnp.einsum('hts,she->het', scores, values_late.reshape(tok, HEADS, DK), p...  4.23 us
    ppermute x2, starting transfers between devices, swap_cores(): return lax.ppermute(x, 'core', [(0, 1), (1, 0)])  2.88 us
    ppermute x2, waiting for transfers between devices, swap_cores(): return lax.ppermute(x, 'core', [(0, 1), (1, 0)])  2.64 us
    reshape x1, local copies, waits for them, and re-layouts, on_device(): k_blk = keys.reshape(tok, HEADS, DK)  1.62 us
    all_to_all x1, waiting for transfers between devices, on_device(): lax.all_to_all((earlier * down).astype(jnp.float16), 'chip', split_axis=0...  1.61 us
    reshape x1, local copies, waits for them, and re-layouts, on_device(): return attended.reshape(tok, HEADS * DK)  1.42 us
  transfers between devices with their start and end apart: 3, of which 3 were waited for; matrix products, arithmetic and copies ran while one was open for 15% of the time, Pallas kernels for 0%

profile of v17, /device:TPU:1, one launch (start us, length us, event | category | flops | bytes accessed | tf_op | source)
XLA Modules:
  0.0 36.8 jit_solution(7214194004916029395)
XLA Ops:
  0.0 0.0 copy-start
  0.0 0.0 copy-start.1
  0.0 1.6 %copy.18 = bf16[256,2048]{0,1:T(8,128)(2,1)S(1)} copy(bf16[256,2048]{1,0:T(8,128)(2,1)} %param.4) | data formatting | bytes 2097152 | tf_op jit(solution)/shard_map/reshape | solution.py:26
  1.6 0.0 copy-done.1
  1.7 0.4 %convolution_convert_fusion = f16[16,128,128]{2,1,0:T(8,128)(2,1)S(1)} fusion(bf16[256,16,128]{0,2,1:T(8,128)(2,1)S(1)} %bitcast.63, bf16[256,2048]{1,0:T(8,128)(2,1)S(1)} %copy-done.1), kind=kOutput, calls=%fused_computation.4 | convolution fusion | flops 134479872 | bytes 2621440 | tf_op jit(solution)/shard_map/thd,the->hde/dot_general | solution.py:28
  2.1 0.2 broadcast_select_fusion.3
  2.2 0.1 collective-permute-start
  2.4 1.5 %collective-permute-done = f16[1024,128]{1,0:T(8,128)(2,1)S(1)} collective-permute-done((f16[1024,128]{1,0:T(8,128)(2,1)S(1)}, f16[1024,128]{1,0:T(8,128)(2,1)S(1)}, u32[]{:S(2)}, u32[]{:S(2)}) %collective-permute-start) | collective-permute-done | bytes 262176 | tf_op jit(solution)/shard_map/ppermute | solution.py:17
  3.8 0.1 fusion.18
  4.0 14.2 %all_to_all.17 = f16[8,128,128]{2,1,0:T(8,128)(2,1)S(1)} all-to-all(f16[8,128,128]{2,1,0:T(8,128)(2,1)S(1)} %bitcast.66), channel_id=1, replica_groups=mesh['groups'=2,'chip'=8,'core'=2] {'chip'}, dimensions={0} | all-to-all | bytes 524288 | tf_op jit(solution)/shard_map/all_to_all | solution.py:36
  18.1 0.8 %fusion.3 = f16[8,128,128]{2,1,0:T(8,128)(2,1)} fusion(f16[8,128,128]{2,1,0:T(8,128)(2,1)S(1)} %all_to_all.17), kind=kOutput, calls=%fused_computation.7 | output fusion | flops 1441792 | bytes 524288 | tf_op jit(solution)/shard_map/jit(cumsum)/reduce_window_sum | solution.py:39
  18.9 4.5 %all-to-all-start.1 = ((f16[8,128,128]{2,1,0:T(8,128)(2,1)}), f16[8,128,128]{2,1,0:T(8,128)(2,1)S(1)}, u32[]{:S(2)}, u32[]{:S(2)}) async-start(f16[8,128,128]{2,1,0:T(8,128)(2,1)} %fusion.3), calls=%async_computation.1 | async-start | bytes 524288 | tf_op jit(solution)/shard_map/all_to_all | solution.py:43
  23.4 1.3 %copy.19 = bf16[256,2048]{0,1:T(8,128)(2,1)} copy(bf16[256,2048]{1,0:T(8,128)(2,1)S(1)} %copy-done.1) | data formatting | bytes 2097152 | tf_op jit(solution)/shard_map/reshape | solution.py:52
  24.7 0.0 copy-done
  24.7 4.2 %fusion.1 = f32[16,128,256]{2,1,0:T(8,128)} fusion(bf16[256,16,128]{0,2,1:T(8,128)(2,1)} %bitcast.67, pred[256,256]{1,0:T(8,128)(4,1)S(1)} %iota_compare_fusion, bf16[256,2048]{1,0:T(8,128)(2,1)S(1)} %copy-done, bf16[256,2048]{1,0:T(8,128)(2,1)} %param.4), kind=kOutput, calls=%fused_computation.3 | convolution fusion | flops 538968064 | bytes 5308416 | tf_op jit(solution)/shard_map/hts,she->het/dot_general | solution.py:52
  28.9 1.6 %all-to-all-done.1 = f16[8,128,128]{2,1,0:T(8,128)(2,1)S(1)} async-done(((f16[8,128,128]{2,1,0:T(8,128)(2,1)}), f16[8,128,128]{2,1,0:T(8,128)(2,1)S(1)}, u32[]{:S(2)}, u32[]{:S(2)}) %all-to-all-start.1) | async-done | bytes 262176 | tf_op jit(solution)/shard_map/all_to_all | solution.py:43
  30.5 0.0 copy-start.2
  30.6 0.1 fusion.20
  30.7 2.8 %collective-permute-start.1 = (bf16[1024,128]{1,0:T(8,128)(2,1)S(1)}, bf16[1024,128]{1,0:T(8,128)(2,1)S(1)}, u32[]{:S(2)}, u32[]{:S(2)}) collective-permute-start(bf16[1024,128]{1,0:T(8,128)(2,1)S(1)} %fusion.20), channel_id=1, source_target_pairs={{0,1},{1,0},{2,3},{3,2},{4,5},{5,4},{6,7},{7,6},{8,9},{9,8},{10,11... | collective-permute-start | bytes 786440 | tf_op jit(solution)/shard_map/ppermute | solution.py:17
  33.5 1.2 %collective-permute-done.1 = bf16[1024,128]{1,0:T(8,128)(2,1)S(1)} collective-permute-done((bf16[1024,128]{1,0:T(8,128)(2,1)S(1)}, bf16[1024,128]{1,0:T(8,128)(2,1)S(1)}, u32[]{:S(2)}, u32[]{:S(2)}) %collective-permute-start.1) | collective-permute-done | bytes 262176 | tf_op jit(solution)/shard_map/ppermute | solution.py:17
  34.6 0.1 broadcast_select_fusion.1
  34.8 0.0 copy-done.2
  34.8 0.5 %multiply_convert_fusion = bf16[16,128,256]{2,1,0:T(8,128)(2,1)S(1)} fusion(f32[16,128,256]{2,1,0:T(8,128)S(1)} %copy-done.2, bf16[16,128,128]{2,1,0:T(8,128)(2,1)S(1)} %bitcast.65, bf16[256,2048]{1,0:T(8,128)(2,1)S(1)} %copy-done), kind=kOutput, calls=%fused_computation.2 | convolution fusion | flops 135790592 | bytes 4718592 | tf_op jit(solution)/shard_map/thd,hde->the/dot_general | solution.py:57
  35.4 1.4 %copy.14 = bf16[256,2048]{1,0:T(8,128)(2,1)} copy(bf16[256,2048]{0,1:T(8,128)(2,1)S(1)} %bitcast.64) | data formatting | bytes 2097152 | tf_op jit(solution)/shard_map/reshape | solution.py:60
  (3 shorter events, 0.1 us)
Async XLA Ops:
  0.0 24.7 %copy-start = (bf16[256,2048]{1,0:T(8,128)(2,1)S(1)}, bf16[256,2048]{1,0:T(8,128)(2,1)}, u32[]{:S(2)}) copy-start(bf16[256,2048]{1,0:T(8,128)(2,1)} %param.3) | copy-start | bytes 3145732
  0.0 1.6 %copy-start.1 = (bf16[256,2048]{1,0:T(8,128)(2,1)S(1)}, bf16[256,2048]{1,0:T(8,128)(2,1)}, u32[]{:S(2)}) copy-start(bf16[256,2048]{1,0:T(8,128)(2,1)} %param.5) | copy-start | bytes 3145732
  2.2 1.6 %collective-permute-start = (f16[1024,128]{1,0:T(8,128)(2,1)S(1)}, f16[1024,128]{1,0:T(8,128)(2,1)S(1)}, u32[]{:S(2)}, u32[]{:S(2)}) collective-permute-start(f16[1024,128]{1,0:T(8,128)(2,1)S(1)} %bitcast.68), channel_id=1, source_target_pairs={{0,1},{1,0},{2,3},{3,2},{4,5},{5,4},{6,7},{7,6},{8,9},{9,8},{10,11... | collective-permute-start | bytes 786440 | tf_op jit(solution)/shard_map/ppermute | solution.py:17
  18.9 11.6 %all-to-all-start.1 = ((f16[8,128,128]{2,1,0:T(8,128)(2,1)}), f16[8,128,128]{2,1,0:T(8,128)(2,1)S(1)}, u32[]{:S(2)}, u32[]{:S(2)}) async-start(f16[8,128,128]{2,1,0:T(8,128)(2,1)} %fusion.3), calls=%async_computation.1 | async-start | bytes 524288 | tf_op jit(solution)/shard_map/all_to_all | solution.py:43
  30.5 4.3 %copy-start.2 = (f32[16,128,256]{2,1,0:T(8,128)S(1)}, f32[16,128,256]{2,1,0:T(8,128)}, u32[]{:S(2)}) copy-start(f32[16,128,256]{2,1,0:T(8,128)} %fusion.1) | copy-start | bytes 6291460
  30.7 3.9 %collective-permute-start.1 = (bf16[1024,128]{1,0:T(8,128)(2,1)S(1)}, bf16[1024,128]{1,0:T(8,128)(2,1)S(1)}, u32[]{:S(2)}, u32[]{:S(2)}) collective-permute-start(bf16[1024,128]{1,0:T(8,128)(2,1)S(1)} %fusion.20), channel_id=1, source_target_pairs={{0,1},{1,0},{2,3},{3,2},{4,5},{5,4},{6,7},{7,6},{8,9},{9,8},{10,11... | collective-permute-start | bytes 786440 | tf_op jit(solution)/shard_map/ppermute | solution.py:17
